TPU v7x, 32 devices: a whole 2x2x4 slice. The times are simulated.
32 devices in a mesh: section: 2 (over core), dp: 16 (over z, y, x).
Axes of the slice: x: 2, y: 2, z: 4, core: 2. Of those that a mesh axis runs over, the one named last changes fastest.
Arguments:
- acts: bfloat16 [2, 16, 1, 64, 2, 2, 128], P('section', 'dp'), may hold values from -6 to 6
- preacts: bfloat16 [2, 16, 1, 64, 2, 2, 128], P('section', 'dp'), may hold values from -6 to 6
- top_grad: bfloat16 [16, 1, 64, 2, 2, 128], P('dp'), may hold values from -6 to 6
- weights: bfloat16 [2, 64, 1728], P('section'), may hold values from -0.21875 to 0.21875
- a_factor: bfloat16 [2, 1728, 1728], P('section', 'dp'), as said below
- g_factor: bfloat16 [2, 64, 64], P('section'), as said below
Outputs:
- act_grads: bfloat16 [2, 16, 1, 64, 2, 2, 128], P('section', 'dp')
- update: float32 [2, 1728, 64], P('section', 'dp')
- inverse: float32 [2, 1728, 1728], P('section', 'dp')
Inputs may be any that keep to these rules, and one draw needn't show every extreme that they name: `a_factor`: each matrix is symmetric and positive definite. `g_factor`: each matrix is symmetric and positive definite.
All inputs are finite; a program needn't handle non-finite values. Where the computation divides by a largest or mean magnitude, that divisor is 1e-20 or more.
Results may differ from a plain program's by a relative error of at most 0.006.
Values may be sent and summed in bfloat16 or wider, within the bound.
No kernel may reach another device: no remote copies, remote signals or barrier semaphores. Data moves between devices by JAX's collectives and lax.ppermute only.
A program may use at most 64 MiB of HBM per device.

v0:
```python
import jax
import jax.numpy as jnp
from jax import lax
from jax.sharding import PartitionSpec as P

KW = 3
MICRO = 1


def shifted(value, axis, steps):
    count = lax.axis_size(axis)
    first, last = (max(0, -steps), min(count, count - steps))
    return lax.ppermute(value, axis, [(source, source + steps) for source in range(first, last)])


def tap_offsets(kernel_width):
    middle = kernel_width // 2
    result = []
    for along_x in range(kernel_width):
        for along_y in range(kernel_width):
            for along_z in range(kernel_width):
                result.append((along_x - middle, along_y - middle, along_z - middle))
    return result


def taps_stack(volume, kernel_width, direction):
    middle = kernel_width // 2
    padded = jnp.pad(volume, ((0, 0), (middle, middle), (middle, middle), (middle, middle)))
    size_x, size_y, size_z = (volume.shape[1], volume.shape[2], volume.shape[3])
    pieces = []
    for off_x, off_y, off_z in tap_offsets(kernel_width):
        start_x = middle + direction * off_x
        start_y = middle + direction * off_y
        start_z = middle + direction * off_z
        pieces.append(
            padded[
                :,
                start_x : start_x + size_x,
                start_y : start_y + size_y,
                start_z : start_z + size_z,
            ]
        )
    stacked = jnp.stack(pieces, 0)
    return stacked.reshape(len(pieces) * volume.shape[0], size_x * size_y * size_z)


def back_input(grad_out, w_rows):
    columns = taps_stack(grad_out, KW, -1)
    summed = lax.dot_general(
        w_rows, columns, (((0,), (0,)), ((), ())), preferred_element_type=jnp.float32
    )
    return summed.astype(jnp.bfloat16).reshape(grad_out.shape)


def back_weight(volume, grad_out):
    columns = taps_stack(volume, KW, 1)
    flattened = grad_out.reshape(grad_out.shape[0], -1)
    return lax.dot_general(
        columns, flattened, (((1,), (1,)), ((), ())), preferred_element_type=jnp.float32
    )


def local_inverse(matrix):
    values = matrix.astype(jnp.float32)
    step_size = 1.0 / jnp.max(jnp.sum(jnp.abs(values), axis=1))
    identity = jnp.eye(matrix.shape[0], dtype=jnp.float32)
    resid0 = (identity - step_size * values).astype(jnp.bfloat16)
    resid1 = jnp.dot(resid0, resid0, preferred_element_type=jnp.float32).astype(jnp.bfloat16)
    cross_term = jnp.dot(resid1, resid0, preferred_element_type=jnp.float32)
    return step_size * (
        identity + resid0.astype(jnp.float32) + resid1.astype(jnp.float32) + cross_term
    )


def eye_rows(start_row, row_total, order_full):
    column_ids = lax.broadcasted_iota(jnp.int32, (row_total, order_full), 1)
    row_ids = lax.broadcasted_iota(jnp.int32, (row_total, order_full), 0)
    return (column_ids == start_row + row_ids).astype(jnp.float32)


def shards(acts, preacts, top_grad, weights, a_factor, g_factor):
    section_index = lax.axis_index("section")
    section_count = lax.axis_size("section")
    tick_count = MICRO + section_count - 1
    inputs = acts[0, 0]
    pre_values = preacts[0, 0]
    upper_grads = top_grad[0]
    channels = weights.shape[1]
    w_rows = weights[0].reshape(channels, -1, channels).transpose(1, 0, 2).reshape(-1, channels)
    zero_field = jnp.zeros(inputs.shape[1:], jnp.bfloat16)

    def one_tick(tick_index, carried):
        outgoing, stored_grads, stored_slopes = carried
        incoming = shifted(outgoing, "section", -1)
        micro_index = tick_index - (section_count - 1 - section_index)
        is_valid = jnp.logical_and(micro_index >= 0, micro_index < MICRO)
        clipped = jnp.clip(micro_index, 0, MICRO - 1)
        from_top = lax.dynamic_index_in_dim(upper_grads, clipped, 0, keepdims=False)
        arriving = jnp.where(section_index == section_count - 1, from_top, incoming)
        pre_now = lax.dynamic_index_in_dim(pre_values, clipped, 0, keepdims=False)
        grad_out = jnp.where(pre_now > 0, arriving, zero_field)
        sending = back_input(grad_out, w_rows)
        old_grad = lax.dynamic_index_in_dim(stored_grads, clipped, 0, keepdims=False)
        old_slope = lax.dynamic_index_in_dim(stored_slopes, clipped, 0, keepdims=False)
        stored_grads = lax.dynamic_update_index_in_dim(
            stored_grads, jnp.where(is_valid, sending, old_grad), clipped, 0
        )
        stored_slopes = lax.dynamic_update_index_in_dim(
            stored_slopes, jnp.where(is_valid, grad_out, old_slope), clipped, 0
        )
        return (sending, stored_grads, stored_slopes)

    start_state = (
        zero_field,
        jnp.zeros(inputs.shape, jnp.bfloat16),
        jnp.zeros(inputs.shape, jnp.bfloat16),
    )
    last_sent, stored_grads, stored_slopes = lax.fori_loop(0, tick_count, one_tick, start_state)
    local_grad = back_weight(inputs[0], stored_slopes[0])
    summed_grad = lax.psum(local_grad, "dp")
    mean_grad = summed_grad / lax.axis_size("dp")
    a_rows = a_factor[0]
    row_total = a_rows.shape[0]
    order_full = a_rows.shape[1]
    first_row = lax.axis_index("dp") * row_total
    local_max = jnp.max(jnp.sum(jnp.abs(a_rows.astype(jnp.float32)), axis=1))
    step_size = 1.0 / lax.pmax(local_max, "dp")
    own_eye = eye_rows(first_row, row_total, order_full)
    resid0 = (own_eye - step_size * a_rows.astype(jnp.float32)).astype(jnp.bfloat16)
    left_cols = resid0
    resid1 = jnp.dot(
        left_cols,
        lax.all_gather(resid0, "dp", axis=0, tiled=True),
        preferred_element_type=jnp.float32,
    ).astype(jnp.bfloat16)
    left_cols = resid1
    cross_term = jnp.dot(
        left_cols,
        lax.all_gather(resid0, "dp", axis=0, tiled=True),
        preferred_element_type=jnp.float32,
    )
    inverse_rows = step_size * (
        own_eye + resid0.astype(jnp.float32) + resid1.astype(jnp.float32) + cross_term
    )
    g_inverse = local_inverse(g_factor[0])
    preconditioned = jnp.dot(
        mean_grad, g_inverse, precision=lax.Precision.HIGHEST, preferred_element_type=jnp.float32
    )
    update_rows = jnp.dot(
        inverse_rows,
        preconditioned,
        precision=lax.Precision.HIGHEST,
        preferred_element_type=jnp.float32,
    )
    return (stored_grads[None, None], update_rows[None], inverse_rows[None])


def solution(mesh):
    placed = (
        P("section", "dp", None, None, None, None, None),
        P("section", "dp", None, None, None, None, None),
        P("dp", None, None, None, None, None),
        P("section", None, None),
        P("section", "dp", None),
        P("section", None, None),
    )
    return jax.shard_map(
        shards,
        mesh=mesh,
        in_specs=placed,
        out_specs=(
            P("section", "dp", None, None, None, None, None),
            P("section", "dp", None),
            P("section", "dp", None),
        ),
        check_vma=False,
    )
```

profile of v0, /device:TPU:0, one launch (start us, length us, event | category | flops | bytes accessed | tf_op | source)
XLA Modules:
  0.0 278.0 jit_solution(16409648565365553291)
XLA Ops:
  7.2 1.5 reshape_squeeze.6
  8.7 0.9 copy.18
  9.7 0.2 fusion.56
  10.8 0.2 fusion.82
  11.1 0.2 fusion.86
  11.7 0.2 fusion.92
  12.0 0.2 fusion.96
  13.2 2.1 reshape.70
  15.3 0.7 broadcast.39
  16.0 0.7 broadcast.40
  16.6 24.1 %while.20 = (s32[]{:T(128)}, bf16[64,2,2,128]{3,2,1,0:T(2,128)(2,1)}, bf16[1,64,2,2,128]{4,3,2,1,0:T(2,128)(2,1)}, bf16[1,64,2,2,128]{4,3,2,1,0:T(2,128)(2,1)}, ...) while((s32[]{:T(128)}, ...), condition=%wide.region_1.2_spmd.clone, body=%wide.region_0.1_spmd.clone.sunk | while | flops 113475592 | bytes 10772739 | solution.py:118
  16.6 1.3 collective-permute-start
  17.9 2.0 collective-permute-done
  20.0 1.7 fusion.173
  22.6 0.2 fusion.183
  22.9 0.2 fusion.185
  23.5 0.2 fusion.188
  23.8 0.2 fusion.190
  25.0 0.7 reshape.79
  25.7 1.5 fusion.200
  27.2 0.6 reshape.80
  28.0 0.6 copy-done.5
  28.6 1.3 collective-permute-start
  29.9 2.0 collective-permute-done
  32.0 1.7 fusion.173
  34.7 0.2 fusion.183
  35.0 0.2 fusion.185
  35.5 0.2 fusion.188
  35.8 0.2 fusion.190
  37.0 0.7 reshape.79
  37.8 1.5 fusion.200
  39.3 0.6 reshape.80
  40.1 0.6 copy-done.5
  40.7 0.9 reshape_squeeze.7
  41.6 0.6 reduce_max.18
  42.2 2.9 %fusion.129 = f32[1728,64]{0,1:T(8,128)} fusion(bf16[1728,512]{1,0:T(8,128)(2,1)} %reshape.70, bf16[64,512]{1,0:T(8,128)(2,1)S(1)} %reshape_squeeze.7), kind=kOutput, calls=%fused_computation.203 | convolution fusion | flops 113246208 | bytes 2277376 | tf_op jit(solution)/shard_map/dot_general | solution.py:58
  45.2 44.4 %pmax.7 = f32[]{:T(128)} all-reduce(f32[]{:T(128)} %reduce_max.18), channel_id=1, replica_groups=mesh['section'=2,'dp'=16] {'dp'}, use_global_device_ids=true, to_apply=%region_4.5 | all-reduce | flops 1 | bytes 8 | tf_op jit(solution)/shard_map/pmax | solution.py:127
  90.3 1.0 fusion.128
  91.4 0.6 reduce_max.19
  93.0 64.2 %all-reduce.4.cloned.1.call-done = f32[1728,64]{0,1:T(8,128)} async-done(((f32[1728,64]{0,1:T(8,128)}), f32[1728,64]{0,1:T(8,128)}) %all-reduce.4.cloned.1.call-update) | async-done | bytes 442384 | tf_op jit(solution)/shard_map/psum | solution.py:120
  157.1 1.6 fusion.60
  158.7 94.8 %all-gather.3.cloned.1.call-done = bf16[16,108,1728]{2,1,0:T(8,128)(2,1)} async-done(((bf16[1,108,1728]{2,1,0:T(8,128)(2,1)}), bf16[16,108,1728]{2,1,0:T(8,128)(2,1)}) %all-gather.3.cloned.1.call-update) | async-done | bytes 5971984 | tf_op jit(solution)/shard_map/all_gather | solution.py:133
  253.5 8.7 %reshape.72 = bf16[1728,1728]{1,0:T(8,128)(2,1)} reshape(bf16[16,108,1728]{2,1,0:T(8,128)(2,1)} %all-gather.3.cloned.1.call-done) | data formatting | bytes 11943936
  262.3 4.0 %convolution_convert_fusion.1 = bf16[108,1728]{1,0:T(8,128)(2,1)S(1)} fusion(bf16[1728,1728]{1,0:T(8,128)(2,1)} %reshape.72, bf16[1,108,1728]{2,1,0:T(8,128)(2,1)S(1)} %copy-done.3, f32[]{:T(128)S(6)} %div.12, s32[108]{0:T(128)S(1)} %iota_add_fusion), kind=kOutput, calls=%fused_computation.115 | convolution fusion | flops 646278912 | bytes 6718900 | tf_op jit(solution)/shard_map/dot_general | solution.py:131
  266.3 0.6 copy-done
  266.8 1.1 fusion.54
  267.9 1.6 convolution_bitcast_fusion
  269.5 1.7 copy.17
  (97 shorter events, 8.6 us)
Async XLA Ops:
  7.2 2.5 copy-start.2
  7.2 2.6 copy-start.1
  7.2 149.9 %all-reduce.4.cloned.1.call-start = ((), (), s32[]{:S(2)}) async-start(), calls=%async_computation | async-start | bytes 917504 | tf_op jit(solution)/shard_map/psum | solution.py:120
  16.6 3.3 %collective-permute-start = (bf16[64,2,2,128]{3,2,1,0:T(2,128)(2,1)}, bf16[64,2,2,128]{3,2,1,0:T(2,128)(2,1)S(1)}, u32[]{:S(2)}, u32[]{:S(2)}) collective-permute-start(bf16[64,2,2,128]{3,2,1,0:T(2,128)(2,1)} %get-tuple-element.362), channel_id=1, source_target_pairs={{16,0},{17,1},{18,2},{19,3},{20,4},{21,5},{22,6},{23,7},{24,8},{25... | collective-permute-start | bytes 196616 | tf_op jit(solution)/shard_map/while/body/eval_jaxpr/ppermute | solution.py:13
  25.7 2.2 copy-start.4
  28.0 0.6 copy-start.5
  28.6 3.3 %collective-permute-start = (bf16[64,2,2,128]{3,2,1,0:T(2,128)(2,1)}, bf16[64,2,2,128]{3,2,1,0:T(2,128)(2,1)S(1)}, u32[]{:S(2)}, u32[]{:S(2)}) collective-permute-start(bf16[64,2,2,128]{3,2,1,0:T(2,128)(2,1)} %get-tuple-element.362), channel_id=1, source_target_pairs={{16,0},{17,1},{18,2},{19,3},{20,4},{21,5},{22,6},{23,7},{24,8},{25... | collective-permute-start | bytes 196616 | tf_op jit(solution)/shard_map/while/body/eval_jaxpr/ppermute | solution.py:13
  37.8 2.2 copy-start.4
  40.1 0.6 copy-start.5
  40.7 49.6 %copy-start.3 = (bf16[1,108,1728]{2,1,0:T(8,128)(2,1)S(1)}, bf16[1,108,1728]{2,1,0:T(8,128)(2,1)}, u32[]{:S(2)}) copy-start(bf16[1,108,1728]{2,1,0:T(8,128)(2,1)} %param.12) | copy-start | bytes 1119748
  42.2 49.1 %copy-start.6 = (bf16[1,64,64]{2,1,0:T(8,128)(2,1)S(1)}, bf16[1,64,64]{2,1,0:T(8,128)(2,1)}, u32[]{:S(2)}) copy-start(bf16[1,64,64]{2,1,0:T(8,128)(2,1)} %param.13) | copy-start | bytes 24580
  45.1 208.4 %all-gather.3.cloned.1.call-start = ((), (), s32[]{:S(2)}) async-start(), calls=%async_computation.1 | async-start | bytes 6823936 | tf_op jit(solution)/shard_map/all_gather | solution.py:133
  262.3 4.5 %copy-start = (bf16[1728,1728]{1,0:T(8,128)(2,1)S(1)}, bf16[1728,1728]{1,0:T(8,128)(2,1)}, u32[]{:S(2)}) copy-start(bf16[1728,1728]{1,0:T(8,128)(2,1)} %reshape.72) | copy-start | bytes 17915908
Sparse Core Ops, SparseCore 0:
  45.3 111.8 all-reduce.3
  159.9 93.6 all-gather.2
where the time goes:
time: 279 us; the launch traced here: 278 us
  waiting for transfers between devices  163 us (58%)
  blocking collectives  44.4 us (16%)
  local copies, waits for them, and re-layouts  31.8 us (11%)
  between operations  15.5 us (6%)
  matrix products  14.4 us (5%)
  other arithmetic  6.04 us (2%)
    all_gather x1, waiting for transfers between devices, shards(): lax.all_gather(resid0, 'dp', axis=0, tiled=True)  94.8 us
    psum x1, waiting for transfers between devices, shards(): summed_grad = lax.psum(local_grad, 'dp')  64.2 us
    pmax x1, blocking collectives, shards(): step_size = 1.0 / lax.pmax(local_max, 'dp')  44.4 us
    unnamed x39, local copies, waits for them, and re-layouts  15.1 us
    while x60, local copies, waits for them, and re-layouts  7.65 us
  transfers between devices with their start and end apart: 4, of which 4 were waited for; matrix products, arithmetic and copies ran while one was open for 1% of the time, Pallas kernels for 0%

commit v1 on v0

--- a/solution.py
+++ b/solution.py
@@ -78,10 +78,21 @@
     return (column_ids == start_row + row_ids).astype(jnp.float32)
 
 
+def doubling_sum(value, axis):
+    count = lax.axis_size(axis)
+    assert count & (count - 1) == 0
+    stride = 1
+    while stride < count:
+        value = value + lax.ppermute(value, axis, [(i, i ^ stride) for i in range(count)])
+        stride *= 2
+    return value
+
+
 def shards(acts, preacts, top_grad, weights, a_factor, g_factor):
     section_index = lax.axis_index("section")
     section_count = lax.axis_size("section")
     tick_count = MICRO + section_count - 1
+    gathered = lax.all_gather(a_factor[0], "dp", axis=0, tiled=True)
     inputs = acts[0, 0]
     pre_values = preacts[0, 0]
     upper_grads = top_grad[0]
@@ -117,28 +128,19 @@
     )
     last_sent, stored_grads, stored_slopes = lax.fori_loop(0, tick_count, one_tick, start_state)
     local_grad = back_weight(inputs[0], stored_slopes[0])
-    summed_grad = lax.psum(local_grad, "dp")
+    summed_grad = doubling_sum(local_grad, "dp")
     mean_grad = summed_grad / lax.axis_size("dp")
     a_rows = a_factor[0]
     row_total = a_rows.shape[0]
     order_full = a_rows.shape[1]
     first_row = lax.axis_index("dp") * row_total
-    local_max = jnp.max(jnp.sum(jnp.abs(a_rows.astype(jnp.float32)), axis=1))
-    step_size = 1.0 / lax.pmax(local_max, "dp")
+    full_values = gathered.astype(jnp.float32)
+    step_size = 1.0 / jnp.max(jnp.sum(jnp.abs(full_values), axis=1))
+    full_resid0 = (jnp.eye(order_full, dtype=jnp.float32) - step_size * full_values).astype(jnp.bfloat16)
     own_eye = eye_rows(first_row, row_total, order_full)
     resid0 = (own_eye - step_size * a_rows.astype(jnp.float32)).astype(jnp.bfloat16)
-    left_cols = resid0
-    resid1 = jnp.dot(
-        left_cols,
-        lax.all_gather(resid0, "dp", axis=0, tiled=True),
-        preferred_element_type=jnp.float32,
-    ).astype(jnp.bfloat16)
-    left_cols = resid1
-    cross_term = jnp.dot(
-        left_cols,
-        lax.all_gather(resid0, "dp", axis=0, tiled=True),
-        preferred_element_type=jnp.float32,
-    )
+    resid1 = jnp.dot(resid0, full_resid0, preferred_element_type=jnp.float32).astype(jnp.bfloat16)
+    cross_term = jnp.dot(resid1, full_resid0, preferred_element_type=jnp.float32)
     inverse_rows = step_size * (
         own_eye + resid0.astype(jnp.float32) + resid1.astype(jnp.float32) + cross_term
     )

time: 279 us -> 240 us (0.86)
  blocking collectives: 44.4 us -> 0 us
  other arithmetic: 6.04 us -> 38.3 us
  waiting for transfers between devices: 163 us -> 140 us
  local copies, waits for them, and re-layouts: 31.8 us -> 24.1 us
  starting transfers between devices: 2.64 us -> 10.1 us
  matrix products: 14.4 us -> 10.2 us
    ppermute x0 -> x4, waiting for transfers between devices: none -> 99.2 us  [doubling_sum(): lax.ppermute(value, axis, [(i, i ^ stride) for i in range(count)])]
    psum x1 -> x0, waiting for transfers between devices: 64.2 us -> none  [shards(): summed_grad = lax.psum(local_grad, 'dp')]
    all_gather x1, waiting for transfers between devices: 94.8 us -> 37.1 us  [shards(): gathered = lax.all_gather(a_factor[0], 'dp', axis=0, tiled=True)]
    pmax x1 -> x0, blocking collectives: 44.4 us -> none  [shards(): step_size = 1.0 / lax.pmax(local_max, 'dp')]
    reduce_sum x1, other arithmetic: 0.17 us -> 18.9 us  [shards(): step_size = 1.0 / jnp.max(jnp.sum(jnp.abs(full_values), axis=1))]
    mul x0 -> x1, other arithmetic: none -> 14.3 us  [shards(): step_size * full_values]
    ppermute x0 -> x4, starting transfers between devices: none -> 7.51 us  [doubling_sum(): lax.ppermute(value, axis, [(i, i ^ stride) for i in range(count)])]
    unnamed x39 -> x37, local copies, waits for them, and re-layouts: 15.1 us -> 8.38 us
  transfers between devices with their start and end apart: 4 -> 7, of which waited for: 4 -> 7; matrix products, arithmetic and copies ran while one was open for 1% -> 12% of each run, Pallas kernels for 0% -> 0%
where the time goes in v1:
time: 240 us; the launch traced here: 239 us
  waiting for transfers between devices  140 us (58%)
  other arithmetic  38.3 us (16%)
  local copies, waits for them, and re-layouts  24.1 us (10%)
  between operations  15.6 us (6%)
  matrix products  10.2 us (4%)
  starting transfers between devices  10.1 us (4%)
    ppermute x4, waiting for transfers between devices, doubling_sum(): lax.ppermute(value, axis, [(i, i ^ stride) for i in range(count)])  99.2 us
    all_gather x1, waiting for transfers between devices, shards(): gathered = lax.all_gather(a_factor[0], 'dp', axis=0, tiled=True)  37.1 us
    reduce_sum x1, other arithmetic, shards(): step_size = 1.0 / jnp.max(jnp.sum(jnp.abs(full_values), axis=1))  18.9 us
    mul x1, other arithmetic, shards(): step_size * full_values  14.3 us
    unnamed x37, local copies, waits for them, and re-layouts  8.38 us
    while x60, local copies, waits for them, and re-layouts  7.65 us
    ppermute x4, starting transfers between devices, doubling_sum(): lax.ppermute(value, axis, [(i, i ^ stride) for i in range(count)])  7.51 us
  transfers between devices with their start and end apart: 7, of which 7 were waited for; matrix products, arithmetic and copies ran while one was open for 12% of the time, Pallas kernels for 0%

profile of v1, /device:TPU:0, one launch (start us, length us, event | category | flops | bytes accessed | tf_op | source)
XLA Modules:
  0.0 238.9 jit_solution(13392514546595699222)
XLA Ops:
  7.2 2.5 %copy.17 = bf16[1,108,1728]{2,0,1:T(2,128)(2,1)} copy(bf16[1,108,1728]{2,1,0:T(8,128)(2,1)} %param.12) | data formatting | bytes 746496 | tf_op args[4]
  9.8 0.5 reshape_squeeze.6
  10.3 0.9 copy.19
  12.3 0.2 fusion.85
  12.6 0.2 fusion.89
  13.1 0.2 fusion.95
  13.4 0.2 fusion.99
  14.6 2.3 reshape.66
  16.9 0.7 broadcast.37
  17.5 0.6 broadcast.38
  18.2 24.1 %while.20 = (s32[]{:T(128)}, bf16[64,2,2,128]{3,2,1,0:T(2,128)(2,1)}, bf16[1,64,2,2,128]{4,3,2,1,0:T(2,128)(2,1)}, bf16[1,64,2,2,128]{4,3,2,1,0:T(2,128)(2,1)}, ...) while((s32[]{:T(128)}, ...), condition=%wide.region_1.2_spmd.clone, body=%wide.region_0.1_spmd.clone.sunk | while | flops 113475592 | bytes 10772739 | solution.py:129
  18.2 1.3 collective-permute-start
  19.5 2.0 collective-permute-done
  21.5 1.7 fusion.172
  25.1 0.2 fusion.187
  26.6 0.7 reshape.81
  27.3 1.5 fusion.199
  28.8 0.6 reshape.82
  29.6 0.6 copy-done.3
  30.3 1.3 collective-permute-start
  31.6 2.0 collective-permute-done
  33.6 1.7 fusion.172
  36.3 0.2 fusion.182
  37.1 0.2 fusion.187
  38.6 0.7 reshape.81
  39.4 1.5 fusion.199
  40.9 0.6 reshape.82
  41.7 0.6 copy-done.3
  42.3 0.9 reshape_squeeze.7
  43.2 2.1 fusion.130
  45.3 3.0 %collective-permute-start.1 = (f32[1728,64]{0,1:T(8,128)S(1)}, f32[1728,64]{0,1:T(8,128)S(1)}, u32[]{:S(2)}, u32[]{:S(2)}) collective-permute-start(f32[1728,64]{0,1:T(8,128)S(1)} %fusion.130), channel_id=1, source_target_pairs={{0,1},{1,0},{2,3},{3,2},{4,5},{5,4},{6,7},{7,6},{8,9},{9,8},{10,11... | collective-permute-start | bytes 1327112 | tf_op jit(solution)/shard_map/ppermute | solution.py:86
  48.3 20.3 %collective-permute-done.1 = f32[1728,64]{0,1:T(8,128)S(1)} collective-permute-done((f32[1728,64]{0,1:T(8,128)S(1)}, f32[1728,64]{0,1:T(8,128)S(1)}, u32[]{:S(2)}, u32[]{:S(2)}) %collective-permute-start.1) | collective-permute-done | bytes 442400 | tf_op jit(solution)/shard_map/ppermute | solution.py:86
  68.7 2.0 collective-permute-start.2
  70.8 9.7 %collective-permute-done.2 = f32[1728,64]{0,1:T(8,128)S(1)} collective-permute-done((f32[1728,64]{0,1:T(8,128)S(1)}, f32[1728,64]{0,1:T(8,128)S(1)}, u32[]{:S(2)}, u32[]{:S(2)}) %collective-permute-start.2) | collective-permute-done | bytes 442400 | tf_op jit(solution)/shard_map/ppermute | solution.py:86
  80.5 1.6 collective-permute-start.3
  82.2 0.6 reduce_max.19
  83.5 19.4 %collective-permute-done.3 = f32[1728,64]{0,1:T(8,128)S(1)} collective-permute-done((f32[1728,64]{0,1:T(8,128)S(1)}, f32[1728,64]{0,1:T(8,128)S(1)}, u32[]{:S(2)}, u32[]{:S(2)}) %collective-permute-start.3) | collective-permute-done | bytes 442400 | tf_op jit(solution)/shard_map/ppermute | solution.py:86
  103.0 0.9 collective-permute-start.4
  104.2 49.6 %collective-permute-done.4 = f32[1728,64]{0,1:T(8,128)S(1)} collective-permute-done((f32[1728,64]{0,1:T(8,128)S(1)}, f32[1728,64]{0,1:T(8,128)S(1)}, u32[]{:S(2)}, u32[]{:S(2)}) %collective-permute-start.4) | collective-permute-done | bytes 442400 | tf_op jit(solution)/shard_map/ppermute | solution.py:86
  153.8 0.6 fusion.61
  154.4 37.1 %all-gather.3.cloned.1.call-done = bf16[1,1728,1728]{2,0,1:T(2,128)(2,1)} async-done(((bf16[1,108,1728]{2,0,1:T(2,128)(2,1)}), bf16[1,1728,1728]{2,0,1:T(2,128)(2,1)}) %all-gather.3.cloned.1.call-update) | async-done | bytes 5971984 | tf_op jit(solution)/shard_map/all_gather | solution.py:95
  191.5 18.9 %abs_reduce_fusion = f32[1728]{0:T(1024)S(1)} fusion(bf16[1,1728,1728]{2,0,1:T(2,128)(2,1)} %all-gather.3.cloned.1.call-done), kind=kLoop, calls=%fused_computation.89 | loop fusion | flops 8956224 | bytes 5978880 | tf_op jit(solution)/shard_map/reduce_sum | solution.py:138
  210.4 0.6 reduce_max.18
  211.7 14.3 %convert_multiply_fusion = f32[1,1728,1728]{2,0,1:T(1,128)S(1)} fusion(bf16[1,1728,1728]{2,0,1:T(2,128)(2,1)} %all-gather.3.cloned.1.call-done, f32[]{:T(128)S(6)} %div.12), kind=kLoop, calls=%fused_computation.90 | loop fusion | flops 5971968 | bytes 17915908 | tf_op jit(solution)/shard_map/mul | solution.py:139
  226.0 1.3 convolution_convert_fusion.1
  227.4 1.4 fusion.55
  228.8 1.6 convolution_bitcast_fusion
  230.4 1.7 copy.18
  (102 shorter events, 9.6 us)
Async XLA Ops:
  7.2 2.7 %copy-start.4 = (bf16[1,64,1728]{2,1,0:T(8,128)(2,1)S(1)}, bf16[1,64,1728]{2,1,0:T(8,128)(2,1)}, u32[]{:S(2)}) copy-start(bf16[1,64,1728]{2,1,0:T(8,128)(2,1)} %param.11) | copy-start | bytes 663556
  7.2 4.1 %copy-start = (bf16[1,1,1,64,2,2,128]{6,5,4,3,2,1,0:T(2,128)(2,1)S(1)}, bf16[1,1,1,64,2,2,128]{6,5,4,3,2,1,0:T(2,128)(2,1)}, u32[]{:S(2)}) copy-start(bf16[1,1,1,64,2,2,128]{6,5,4,3,2,1,0:T(2,128)(2,1)} %param.8) | copy-start | bytes 196612
  7.2 184.3 %all-gather.3.cloned.1.call-start = ((), (), s32[]{:S(2)}) async-start(), calls=%async_computation | async-start | bytes 13160448 | tf_op jit(solution)/shard_map/all_gather | solution.py:95
  18.2 3.3 %collective-permute-start = (bf16[64,2,2,128]{3,2,1,0:T(2,128)(2,1)}, bf16[64,2,2,128]{3,2,1,0:T(2,128)(2,1)S(1)}, u32[]{:S(2)}, u32[]{:S(2)}) collective-permute-start(bf16[64,2,2,128]{3,2,1,0:T(2,128)(2,1)} %get-tuple-element.362), channel_id=1, source_target_pairs={{16,0},{17,1},{18,2},{19,3},{20,4},{21,5},{22,6},{23,7},{24,8},{25... | collective-permute-start | bytes 196616 | tf_op jit(solution)/shard_map/while/body/eval_jaxpr/ppermute | solution.py:13
  27.3 2.2 copy-start.2
  29.6 0.6 copy-start.3
  30.3 3.3 %collective-permute-start = (bf16[64,2,2,128]{3,2,1,0:T(2,128)(2,1)}, bf16[64,2,2,128]{3,2,1,0:T(2,128)(2,1)S(1)}, u32[]{:S(2)}, u32[]{:S(2)}) collective-permute-start(bf16[64,2,2,128]{3,2,1,0:T(2,128)(2,1)} %get-tuple-element.362), channel_id=1, source_target_pairs={{16,0},{17,1},{18,2},{19,3},{20,4},{21,5},{22,6},{23,7},{24,8},{25... | collective-permute-start | bytes 196616 | tf_op jit(solution)/shard_map/while/body/eval_jaxpr/ppermute | solution.py:13
  39.4 2.2 copy-start.2
  41.7 0.6 copy-start.3
  45.3 36.8 %copy-start.5 = (bf16[1,64,64]{2,1,0:T(8,128)(2,1)S(1)}, bf16[1,64,64]{2,1,0:T(8,128)(2,1)}, u32[]{:S(2)}) copy-start(bf16[1,64,64]{2,1,0:T(8,128)(2,1)} %param.13) | copy-start | bytes 24580
  45.3 23.4 %collective-permute-start.1 = (f32[1728,64]{0,1:T(8,128)S(1)}, f32[1728,64]{0,1:T(8,128)S(1)}, u32[]{:S(2)}, u32[]{:S(2)}) collective-permute-start(f32[1728,64]{0,1:T(8,128)S(1)} %fusion.130), channel_id=1, source_target_pairs={{0,1},{1,0},{2,3},{3,2},{4,5},{5,4},{6,7},{7,6},{8,9},{9,8},{10,11... | collective-permute-start | bytes 1327112 | tf_op jit(solution)/shard_map/ppermute | solution.py:86
  68.7 11.8 %collective-permute-start.2 = (f32[1728,64]{0,1:T(8,128)S(1)}, f32[1728,64]{0,1:T(8,128)S(1)}, u32[]{:S(2)}, u32[]{:S(2)}) collective-permute-start(f32[1728,64]{0,1:T(8,128)S(1)} %add.76), channel_id=1, source_target_pairs={{0,2},{1,3},{2,0},{3,1},{4,6},{5,7},{6,4},{7,5},{8,10},{9,11},{10,... | collective-permute-start | bytes 1327112 | tf_op jit(solution)/shard_map/ppermute | solution.py:86
  80.5 22.4 %collective-permute-start.3 = (f32[1728,64]{0,1:T(8,128)S(1)}, f32[1728,64]{0,1:T(8,128)S(1)}, u32[]{:S(2)}, u32[]{:S(2)}) collective-permute-start(f32[1728,64]{0,1:T(8,128)S(1)} %add.77), channel_id=1, source_target_pairs={{0,4},{1,5},{2,6},{3,7},{4,0},{5,1},{6,2},{7,3},{8,12},{9,13},{10,... | collective-permute-start | bytes 1327112 | tf_op jit(solution)/shard_map/ppermute | solution.py:86
  103.0 50.8 %collective-permute-start.4 = (f32[1728,64]{0,1:T(8,128)S(1)}, f32[1728,64]{0,1:T(8,128)S(1)}, u32[]{:S(2)}, u32[]{:S(2)}) collective-permute-start(f32[1728,64]{0,1:T(8,128)S(1)} %add.78), channel_id=1, source_target_pairs={{0,8},{1,9},{2,10},{3,11},{4,12},{5,13},{6,14},{7,15},{8,0},{9,1},... | collective-permute-start | bytes 1327112 | tf_op jit(solution)/shard_map/ppermute | solution.py:86
  211.7 14.3 %copy-start.1 = (bf16[1,108,1728]{2,1,0:T(8,128)(2,1)S(1)}, bf16[1,108,1728]{2,1,0:T(8,128)(2,1)}, u32[]{:S(2)}) copy-start(bf16[1,108,1728]{2,1,0:T(8,128)(2,1)} %param.12) | copy-start | bytes 1119748
Sparse Core Ops, SparseCore 0:
  11.4 180.0 all-gather.2

commit v2 on v1

--- a/solution.py
+++ b/solution.py
@@ -78,12 +78,23 @@
     return (column_ids == start_row + row_ids).astype(jnp.float32)
 
 
-def doubling_sum(value, axis):
+def halving_sum(value, axis):
     count = lax.axis_size(axis)
-    assert count & (count - 1) == 0
+    assert count & (count - 1) == 0 and value.shape[0] % count == 0
+    index = lax.axis_index(axis)
+    stride = count // 2
+    while stride >= 1:
+        half = value.shape[0] // 2
+        upper = (index // stride) % 2 == 1
+        keep = jnp.where(upper, value[half:], value[:half])
+        send = jnp.where(upper, value[:half], value[half:])
+        value = keep + lax.ppermute(send, axis, [(i, i ^ stride) for i in range(count)])
+        stride //= 2
     stride = 1
     while stride < count:
-        value = value + lax.ppermute(value, axis, [(i, i ^ stride) for i in range(count)])
+        other = lax.ppermute(value, axis, [(i, i ^ stride) for i in range(count)])
+        upper = (index // stride) % 2 == 1
+        value = jnp.where(upper, jnp.concatenate([other, value]), jnp.concatenate([value, other]))
         stride *= 2
     return value
 
@@ -92,7 +103,7 @@
     section_index = lax.axis_index("section")
     section_count = lax.axis_size("section")
     tick_count = MICRO + section_count - 1
-    gathered = lax.all_gather(a_factor[0], "dp", axis=0, tiled=True)
+    gathered = lax.all_gather(a_factor[0], "dp", axis=0)
     inputs = acts[0, 0]
     pre_values = preacts[0, 0]
     upper_grads = top_grad[0]
@@ -128,19 +139,31 @@
     )
     last_sent, stored_grads, stored_slopes = lax.fori_loop(0, tick_count, one_tick, start_state)
     local_grad = back_weight(inputs[0], stored_slopes[0])
-    summed_grad = doubling_sum(local_grad, "dp")
+    summed_grad = halving_sum(local_grad, "dp")
     mean_grad = summed_grad / lax.axis_size("dp")
     a_rows = a_factor[0]
     row_total = a_rows.shape[0]
     order_full = a_rows.shape[1]
     first_row = lax.axis_index("dp") * row_total
     full_values = gathered.astype(jnp.float32)
-    step_size = 1.0 / jnp.max(jnp.sum(jnp.abs(full_values), axis=1))
-    full_resid0 = (jnp.eye(order_full, dtype=jnp.float32) - step_size * full_values).astype(jnp.bfloat16)
+    step_size = 1.0 / jnp.max(jnp.sum(jnp.abs(full_values), axis=2))
+    shard_count = gathered.shape[0]
+    block_ids = lax.broadcasted_iota(jnp.int32, gathered.shape, 0)
+    row_ids = lax.broadcasted_iota(jnp.int32, gathered.shape, 1)
+    column_ids = lax.broadcasted_iota(jnp.int32, gathered.shape, 2)
+    full_eye = (column_ids == block_ids * row_total + row_ids).astype(jnp.float32)
+    full_resid0 = (full_eye - step_size * full_values).astype(jnp.bfloat16)
+    contract = (((1, 2), (0, 1)), ((), ()))
     own_eye = eye_rows(first_row, row_total, order_full)
     resid0 = (own_eye - step_size * a_rows.astype(jnp.float32)).astype(jnp.bfloat16)
-    resid1 = jnp.dot(resid0, full_resid0, preferred_element_type=jnp.float32).astype(jnp.bfloat16)
-    cross_term = jnp.dot(resid1, full_resid0, preferred_element_type=jnp.float32)
+    resid1 = lax.dot_general(
+        resid0.reshape(row_total, shard_count, row_total), full_resid0, contract,
+        preferred_element_type=jnp.float32,
+    ).astype(jnp.bfloat16)
+    cross_term = lax.dot_general(
+        resid1.reshape(row_total, shard_count, row_total), full_resid0, contract,
+        preferred_element_type=jnp.float32,
+    )
     inverse_rows = step_size * (
         own_eye + resid0.astype(jnp.float32) + resid1.astype(jnp.float32) + cross_term
     )

time: 240 us -> 156 us (0.65)
  waiting for transfers between devices: 140 us -> 71.5 us
  other arithmetic: 38.3 us -> 10.5 us
  matrix products: 10.2 us -> 19.6 us
  starting transfers between devices: 10.1 us -> 14.2 us
    all_gather x1, waiting for transfers between devices: 37.1 us -> 0.4 us  [shards(): gathered = lax.all_gather(a_factor[0], 'dp', axis=0)]
    ppermute x4 -> x8, waiting for transfers between devices: 99.2 us -> 66.3 us  [the longest x4 33.8 us: halving_sum(): lax.ppermute(send, axis, [(i, i ^ stride) for i in range(count)])]
    reduce_sum x1, other arithmetic: 18.9 us -> 4.21 us  [shards(): step_size = 1.0 / jnp.max(jnp.sum(jnp.abs(full_values), axis=2))]
    mul x1 -> x2, other arithmetic: 14.3 us -> 0.06 us  [the longest x1 0.06 us: shards(): step_size * a_rows.astype(jnp.float32)]
    dot_general x2, matrix products: 2.72 us -> 11.9 us  [the longest x1 6.21 us: shards(): lax.dot_general(resid0.reshape(row_total, shard_count, row_total), full_r...]
    ppermute x4 -> x8, starting transfers between devices: 7.51 us -> 11.6 us  [the longest x4 7.15 us: halving_sum(): lax.ppermute(send, axis, [(i, i ^ stride) for i in range(count)])]
    unnamed x37 -> x34, local copies, waits for them, and re-layouts: 8.38 us -> 5.82 us
  transfers between devices with their start and end apart: 7 -> 11, of which waited for: 7 -> 11; matrix products, arithmetic and copies ran while one was open for 12% -> 20% of each run, Pallas kernels for 0% -> 0%
where the time goes in v2:
time: 156 us
  waiting for transfers between devices  71.5 us (46%)
  local copies, waits for them, and re-layouts  24.2 us (16%)
  matrix products  19.6 us (13%)
  between operations  15.7 us (10%)
  starting transfers between devices  14.2 us (9%)
  other arithmetic  10.5 us (7%)
    ppermute x4, waiting for transfers between devices, halving_sum(): lax.ppermute(send, axis, [(i, i ^ stride) for i in range(count)])  33.8 us
    ppermute x4, waiting for transfers between devices, halving_sum(): other = lax.ppermute(value, axis, [(i, i ^ stride) for i in range(count)])  32.6 us
    while x60, local copies, waits for them, and re-layouts  7.66 us
    ppermute x4, starting transfers between devices, halving_sum(): lax.ppermute(send, axis, [(i, i ^ stride) for i in range(count)])  7.15 us
    dot_general x1, matrix products, shards(): lax.dot_general(resid0.reshape(row_total, shard_count, row_total), full_r...  6.21 us
    unnamed x34, local copies, waits for them, and re-layouts  5.82 us
    dot_general x1, matrix products, shards(): lax.dot_general(resid1.reshape(row_total, shard_count, row_total), full_r...  5.69 us
    ppermute x4, starting transfers between devices, halving_sum(): other = lax.ppermute(value, axis, [(i, i ^ stride) for i in range(count)])  4.41 us
  transfers between devices with their start and end apart: 11, of which 11 were waited for; matrix products, arithmetic and copies ran while one was open for 20% of the time, Pallas kernels for 0%

profile of v2, /device:TPU:0, one launch (start us, length us, event | category | flops | bytes accessed | tf_op | source)
XLA Modules:
  0.0 155.8 jit_solution(18202354857161093187)
XLA Ops:
  7.2 0.7 all-gather.2.cloned.1.call-update
  7.9 1.4 reshape_squeeze.6
  9.4 0.9 copy.31
  13.7 2.1 %reshape.91 = bf16[1728,512]{1,0:T(8,128)(2,1)} reshape(bf16[27,64,2,2,128]{4,3,2,1,0:T(2,128)(2,1)S(1)} %fusion.128) | data formatting | bytes 3538944 | tf_op jit(solution)/shard_map/reshape | solution.py:44
  15.8 0.7 broadcast.64
  16.4 0.7 broadcast.65
  17.1 24.1 %while.20 = (s32[]{:T(128)}, bf16[64,2,2,128]{3,2,1,0:T(2,128)(2,1)}, bf16[1,64,2,2,128]{4,3,2,1,0:T(2,128)(2,1)}, bf16[1,64,2,2,128]{4,3,2,1,0:T(2,128)(2,1)}, ...) while((s32[]{:T(128)}, ...), condition=%wide.region_1.2_spmd.clone, body=%wide.region_0.1_spmd.clone.sunk | while | flops 113475592 | bytes 10772739 | solution.py:140
  17.1 1.3 collective-permute-start
  18.4 2.0 %collective-permute-done = bf16[64,2,2,128]{3,2,1,0:T(2,128)(2,1)S(1)} collective-permute-done((bf16[64,2,2,128]{3,2,1,0:T(2,128)(2,1)}, bf16[64,2,2,128]{3,2,1,0:T(2,128)(2,1)S(1)}, u32[]{:S(2)}, u32[]{:S(2)}) %collective-permute-start) | collective-permute-done | bytes 65568 | tf_op jit(solution)/shard_map/while/body/eval_jaxpr/ppermute | solution.py:13
  20.4 1.7 %fusion.183 = (bf16[1,64,2,2,128]{4,3,2,1,0:T(2,128)(2,1)}, bf16[64,2,2,128]{3,2,1,0:T(2,128)(2,1)S(1)}) fusion(pred[]{:T(512)S(6)} %and.61, bf16[1,64,2,2,128]{4,3,2,1,0:T(2,128)(2,1)} %get-tuple-element.376, bf16[64,2,2,128]{3,2,1,0:T(2,128)(2,1)S(1)} %collective-permute-done, bf16[1,64,2,2,128]{4,3,2,1,0:T(2,128)(2,1)} %get-tuple-element.390, ...), kind=kLoop, calls=%fused_computation.33.clone.1 | loop fusion | flops 131072 | bytes 393218 | tf_op jit(solution)/shard_map/while/body/eval_jaxpr/jit(dynamic_update_index_in_dim)/broadcast_in_dim | solution.py:130
  25.5 0.7 reshape.100
  26.2 1.5 fusion.210
  27.7 0.7 reshape.101
  28.5 0.6 copy-done.2
  29.2 1.3 collective-permute-start
  30.5 2.0 %collective-permute-done = bf16[64,2,2,128]{3,2,1,0:T(2,128)(2,1)S(1)} collective-permute-done((bf16[64,2,2,128]{3,2,1,0:T(2,128)(2,1)}, bf16[64,2,2,128]{3,2,1,0:T(2,128)(2,1)S(1)}, u32[]{:S(2)}, u32[]{:S(2)}) %collective-permute-start) | collective-permute-done | bytes 65568 | tf_op jit(solution)/shard_map/while/body/eval_jaxpr/ppermute | solution.py:13
  32.5 1.7 %fusion.183 = (bf16[1,64,2,2,128]{4,3,2,1,0:T(2,128)(2,1)}, bf16[64,2,2,128]{3,2,1,0:T(2,128)(2,1)S(1)}) fusion(pred[]{:T(512)S(6)} %and.61, bf16[1,64,2,2,128]{4,3,2,1,0:T(2,128)(2,1)} %get-tuple-element.376, bf16[64,2,2,128]{3,2,1,0:T(2,128)(2,1)S(1)} %collective-permute-done, bf16[1,64,2,2,128]{4,3,2,1,0:T(2,128)(2,1)} %get-tuple-element.390, ...), kind=kLoop, calls=%fused_computation.33.clone.1 | loop fusion | flops 131072 | bytes 393218 | tf_op jit(solution)/shard_map/while/body/eval_jaxpr/jit(dynamic_update_index_in_dim)/broadcast_in_dim | solution.py:130
  37.6 0.7 reshape.100
  38.3 1.5 fusion.210
  39.8 0.7 reshape.101
  40.6 0.6 copy-done.2
  41.2 0.9 reshape_squeeze.7
  42.1 2.1 %fusion.142 = f32[1728,64]{0,1:T(8,128)S(1)} fusion(bf16[1728,512]{1,0:T(8,128)(2,1)} %reshape.91, bf16[64,512]{1,0:T(8,128)(2,1)S(1)} %reshape_squeeze.7), kind=kOutput, calls=%fused_computation.231 | convolution fusion | flops 113246208 | bytes 2277376 | tf_op jit(solution)/shard_map/dot_general | solution.py:58
  44.4 4.1 %collective-permute-start.1 = (f32[864,64]{0,1:T(8,128)S(1)}, f32[864,64]{0,1:T(8,128)S(1)}, u32[]{:S(2)}, u32[]{:S(2)}) collective-permute-start(f32[864,64]{0,1:T(8,128)S(1)} %slice_select_fusion), channel_id=1, source_target_pairs={{0,8},{1,9},{2,10},{3,11},{4,12},{5,13},{6,14},{7,15},{8,0},{9,1},... | collective-permute-start | bytes 663560 | tf_op jit(solution)/shard_map/ppermute | solution.py:91
  48.5 22.3 %collective-permute-done.1 = f32[864,64]{0,1:T(8,128)S(1)} collective-permute-done((f32[864,64]{0,1:T(8,128)S(1)}, f32[864,64]{0,1:T(8,128)S(1)}, u32[]{:S(2)}, u32[]{:S(2)}) %collective-permute-start.1) | collective-permute-done | bytes 221216 | tf_op jit(solution)/shard_map/ppermute | solution.py:91
  71.1 5.4 %collective-permute-done.2 = f32[432,64]{0,1:T(8,128)S(1)} collective-permute-done((f32[432,64]{0,1:T(8,128)S(1)}, f32[432,64]{0,1:T(8,128)S(1)}, u32[]{:S(2)}, u32[]{:S(2)}) %collective-permute-start.2) | collective-permute-done | bytes 110624 | tf_op jit(solution)/shard_map/ppermute | solution.py:91
  76.8 1.5 collective-permute-start.3
  78.4 0.6 reduce_max.19
  79.7 2.9 %collective-permute-done.3 = f32[216,64]{0,1:T(8,128)S(1)} collective-permute-done((f32[216,64]{0,1:T(8,128)S(1)}, f32[216,64]{0,1:T(8,128)S(1)}, u32[]{:S(2)}, u32[]{:S(2)}) %collective-permute-start.3) | collective-permute-done | bytes 55328 | tf_op jit(solution)/shard_map/ppermute | solution.py:91
  82.7 1.4 collective-permute-start.4
  84.3 3.2 %collective-permute-done.4 = f32[108,64]{0,1:T(8,128)S(1)} collective-permute-done((f32[108,64]{0,1:T(8,128)S(1)}, f32[108,64]{0,1:T(8,128)S(1)}, u32[]{:S(2)}, u32[]{:S(2)}) %collective-permute-start.4) | collective-permute-done | bytes 27680 | tf_op jit(solution)/shard_map/ppermute | solution.py:91
  87.6 1.4 collective-permute-start.5
  89.0 3.3 %collective-permute-done.5 = f32[108,64]{0,1:T(8,128)S(1)} collective-permute-done((f32[108,64]{0,1:T(8,128)S(1)}, f32[108,64]{0,1:T(8,128)S(1)}, u32[]{:S(2)}, u32[]{:S(2)}) %collective-permute-start.5) | collective-permute-done | bytes 27680 | tf_op jit(solution)/shard_map/ppermute | solution.py:95
  92.4 1.5 collective-permute-start.6
  94.0 4.3 %collective-permute-done.6 = f32[216,64]{0,1:T(8,128)S(1)} collective-permute-done((f32[216,64]{0,1:T(8,128)S(1)}, f32[216,64]{0,1:T(8,128)S(1)}, u32[]{:S(2)}, u32[]{:S(2)}) %collective-permute-start.6) | collective-permute-done | bytes 55328 | tf_op jit(solution)/shard_map/ppermute | solution.py:95
  98.7 6.8 %collective-permute-done.7 = f32[432,64]{0,1:T(8,128)S(1)} collective-permute-done((f32[432,64]{0,1:T(8,128)S(1)}, f32[432,64]{0,1:T(8,128)S(1)}, u32[]{:S(2)}, u32[]{:S(2)}) %collective-permute-start.7) | collective-permute-done | bytes 110624 | tf_op jit(solution)/shard_map/ppermute | solution.py:95
  105.6 1.2 collective-permute-start.8
  106.9 18.1 %collective-permute-done.8 = f32[864,64]{0,1:T(8,128)S(1)} collective-permute-done((f32[864,64]{0,1:T(8,128)S(1)}, f32[864,64]{0,1:T(8,128)S(1)}, u32[]{:S(2)}, u32[]{:S(2)}) %collective-permute-start.8) | collective-permute-done | bytes 221216 | tf_op jit(solution)/shard_map/ppermute | solution.py:95
  125.1 0.7 fusion.64
  125.8 0.4 all-gather.2.cloned.1.call-done
  126.2 4.2 %fusion.54 = f32[16,108]{1,0:T(8,128)S(1)} fusion(bf16[16,108,1728]{2,1,0:T(8,128)(2,1)} %all-gather.2.cloned.1.call-done), kind=kLoop, calls=%fused_computation.89 | loop fusion | flops 8956224 | bytes 5978880 | tf_op jit(solution)/shard_map/reduce_sum | solution.py:149
  130.4 0.6 reduce_max.18
  131.8 0.9 mul.57
  132.9 6.2 %fusion.59 = bf16[108,1728]{1,0:T(8,128)(2,1)S(1)} fusion(bf16[108,16,108]{2,1,0:T(8,128)(2,1)S(1)} %subtract_convert_fusion, bf16[16,108,1728]{2,1,0:T(8,128)(2,1)} %all-gather.2.cloned.1.call-done, f32[]{:T(128)S(6)} %div.39, s32[16]{0:T(128)S(1)} %iota_multiply_fusion), kind=kOutput, calls=%fused_computation.123 | convolution fusion | flops 666061056 | bytes 6718532 | tf_op jit(solution)/shard_map/dot_general | solution.py:159
  139.1 0.9 reshape.90
  140.0 5.7 %fusion.58 = f32[108,1728]{1,0:T(8,128)S(1)} fusion(bf16[108,1728]{1,0:T(8,128)(2,1)S(1)} %fusion.59, bf16[108,16,108]{2,1,0:T(8,128)(2,1)S(1)} %reshape.90, s32[108]{0:T(128)S(1)} %iota_add_fusion, f32[]{:T(128)S(6)} %div.39, bf16[16,108,1728]{2,1,0:T(8,128)(2,1)} %all-gather.2.cloned.1.call-done, s32[16]{0:T(128)S(1)} %iota_multiply_fusion, ...), kind=kOutput, calls=%fused_computation.122 | convolution fusion | flops 668113920 | bytes 7838708 | tf_op jit(solution)/shard_map/dot_general | solution.py:163
  145.7 1.6 %convolution_bitcast_fusion.2 = f32[1,108,64]{1,2,0:T(8,128)} fusion(f32[108,1728]{1,0:T(8,128)S(1)} %fusion.58, f32[1728,64]{0,1:T(8,128)S(1)} %fusion.64), kind=kOutput, calls=%fused_computation.124 | convolution fusion | flops 143327232 | bytes 1216512 | tf_op jit(solution)/shard_map/dot_general | solution.py:174
  147.3 1.7 %copy.30 = f32[1,108,1728]{2,0,1:T(1,128)} copy(f32[1,108,1728]{2,1,0:T(8,128)S(1)} %bitcast.359) | data formatting | bytes 1492992
  (120 shorter events, 12.4 us)
Async XLA Ops:
  7.2 3.1 %copy-start = (bf16[1,1,1,64,2,2,128]{6,5,4,3,2,1,0:T(2,128)(2,1)S(1)}, bf16[1,1,1,64,2,2,128]{6,5,4,3,2,1,0:T(2,128)(2,1)}, u32[]{:S(2)}) copy-start(bf16[1,1,1,64,2,2,128]{6,5,4,3,2,1,0:T(2,128)(2,1)} %param.8) | copy-start | bytes 196612
  7.2 119.0 %all-gather.2.cloned.1.call-start = ((), (), s32[]{:S(2)}) async-start(), calls=%async_computation | async-start | bytes 6823936 | tf_op jit(solution)/shard_map/all_gather | solution.py:106
  17.1 3.3 %collective-permute-start = (bf16[64,2,2,128]{3,2,1,0:T(2,128)(2,1)}, bf16[64,2,2,128]{3,2,1,0:T(2,128)(2,1)S(1)}, u32[]{:S(2)}, u32[]{:S(2)}) collective-permute-start(bf16[64,2,2,128]{3,2,1,0:T(2,128)(2,1)} %get-tuple-element.374), channel_id=1, source_target_pairs={{16,0},{17,1},{18,2},{19,3},{20,4},{21,5},{22,6},{23,7},{24,8},{25... | collective-permute-start | bytes 196616 | tf_op jit(solution)/shard_map/while/body/eval_jaxpr/ppermute | solution.py:13
  26.2 2.2 %copy-start.1 = (bf16[1,64,2,2,128]{4,3,2,1,0:T(2,128)(2,1)S(1)}, bf16[1,64,2,2,128]{4,3,2,1,0:T(2,128)(2,1)}, u32[]{:S(2)}) copy-start(bf16[1,64,2,2,128]{4,3,2,1,0:T(2,128)(2,1)} %get-tuple-element.375) | copy-start | bytes 196612 | tf_op jit(solution)/shard_map/while
  28.5 0.6 copy-start.2
  29.2 3.3 %collective-permute-start = (bf16[64,2,2,128]{3,2,1,0:T(2,128)(2,1)}, bf16[64,2,2,128]{3,2,1,0:T(2,128)(2,1)S(1)}, u32[]{:S(2)}, u32[]{:S(2)}) collective-permute-start(bf16[64,2,2,128]{3,2,1,0:T(2,128)(2,1)} %get-tuple-element.374), channel_id=1, source_target_pairs={{16,0},{17,1},{18,2},{19,3},{20,4},{21,5},{22,6},{23,7},{24,8},{25... | collective-permute-start | bytes 196616 | tf_op jit(solution)/shard_map/while/body/eval_jaxpr/ppermute | solution.py:13
  38.3 2.2 %copy-start.1 = (bf16[1,64,2,2,128]{4,3,2,1,0:T(2,128)(2,1)S(1)}, bf16[1,64,2,2,128]{4,3,2,1,0:T(2,128)(2,1)}, u32[]{:S(2)}) copy-start(bf16[1,64,2,2,128]{4,3,2,1,0:T(2,128)(2,1)} %get-tuple-element.375) | copy-start | bytes 196612 | tf_op jit(solution)/shard_map/while
  40.6 0.6 copy-start.2
  44.2 34.1 %copy-start.4 = (bf16[1,64,64]{2,1,0:T(8,128)(2,1)S(1)}, bf16[1,64,64]{2,1,0:T(8,128)(2,1)}, u32[]{:S(2)}) copy-start(bf16[1,64,64]{2,1,0:T(8,128)(2,1)} %param.13) | copy-start | bytes 24580
  44.4 26.4 %collective-permute-start.1 = (f32[864,64]{0,1:T(8,128)S(1)}, f32[864,64]{0,1:T(8,128)S(1)}, u32[]{:S(2)}, u32[]{:S(2)}) collective-permute-start(f32[864,64]{0,1:T(8,128)S(1)} %slice_select_fusion), channel_id=1, source_target_pairs={{0,8},{1,9},{2,10},{3,11},{4,12},{5,13},{6,14},{7,15},{8,0},{9,1},... | collective-permute-start | bytes 663560 | tf_op jit(solution)/shard_map/ppermute | solution.py:91
  71.0 5.6 %collective-permute-start.2 = (f32[432,64]{0,1:T(8,128)S(1)}, f32[432,64]{0,1:T(8,128)S(1)}, u32[]{:S(2)}, u32[]{:S(2)}) collective-permute-start(f32[432,64]{0,1:T(8,128)S(1)} %slice_select_fusion.1), channel_id=1, source_target_pairs={{0,4},{1,5},{2,6},{3,7},{4,0},{5,1},{6,2},{7,3},{8,12},{9,13},{10,... | collective-permute-start | bytes 331784 | tf_op jit(solution)/shard_map/ppermute | solution.py:91
  76.8 5.8 %collective-permute-start.3 = (f32[216,64]{0,1:T(8,128)S(1)}, f32[216,64]{0,1:T(8,128)S(1)}, u32[]{:S(2)}, u32[]{:S(2)}) collective-permute-start(f32[216,64]{0,1:T(8,128)S(1)} %slice_select_fusion.2), channel_id=1, source_target_pairs={{0,2},{1,3},{2,0},{3,1},{4,6},{5,7},{6,4},{7,5},{8,10},{9,11},{10,... | collective-permute-start | bytes 165896 | tf_op jit(solution)/shard_map/ppermute | solution.py:91
  82.7 4.8 %collective-permute-start.4 = (f32[108,64]{0,1:T(8,128)S(1)}, f32[108,64]{0,1:T(8,128)S(1)}, u32[]{:S(2)}, u32[]{:S(2)}) collective-permute-start(f32[108,64]{0,1:T(8,128)S(1)} %slice_select_fusion.3), channel_id=1, source_target_pairs={{0,1},{1,0},{2,3},{3,2},{4,5},{5,4},{6,7},{7,6},{8,9},{9,8},{10,11... | collective-permute-start | bytes 82952 | tf_op jit(solution)/shard_map/ppermute | solution.py:91
  87.6 4.7 %collective-permute-start.5 = (f32[108,64]{0,1:T(8,128)S(1)}, f32[108,64]{0,1:T(8,128)S(1)}, u32[]{:S(2)}, u32[]{:S(2)}) collective-permute-start(f32[108,64]{0,1:T(8,128)S(1)} %select_add_fusion.3), channel_id=1, source_target_pairs={{0,1},{1,0},{2,3},{3,2},{4,5},{5,4},{6,7},{7,6},{8,9},{9,8},{10,11... | collective-permute-start | bytes 82952 | tf_op jit(solution)/shard_map/ppermute | solution.py:95
  92.4 5.9 %collective-permute-start.6 = (f32[216,64]{0,1:T(8,128)S(1)}, f32[216,64]{0,1:T(8,128)S(1)}, u32[]{:S(2)}, u32[]{:S(2)}) collective-permute-start(f32[216,64]{0,1:T(8,128)S(1)} %maximum_select_fusion.3), channel_id=1, source_target_pairs={{0,2},{1,3},{2,0},{3,1},{4,6},{5,7},{6,4},{7,5},{8,10},{9,11},{10,... | collective-permute-start | bytes 165896 | tf_op jit(solution)/shard_map/ppermute | solution.py:95
  98.4 7.0 %collective-permute-start.7 = (f32[432,64]{0,1:T(8,128)S(1)}, f32[432,64]{0,1:T(8,128)S(1)}, u32[]{:S(2)}, u32[]{:S(2)}) collective-permute-start(f32[432,64]{0,1:T(8,128)S(1)} %maximum_select_fusion.2), channel_id=1, source_target_pairs={{0,4},{1,5},{2,6},{3,7},{4,0},{5,1},{6,2},{7,3},{8,12},{9,13},{10,... | collective-permute-start | bytes 331784 | tf_op jit(solution)/shard_map/ppermute | solution.py:95
  105.6 19.5 %collective-permute-start.8 = (f32[864,64]{0,1:T(8,128)S(1)}, f32[864,64]{0,1:T(8,128)S(1)}, u32[]{:S(2)}, u32[]{:S(2)}) collective-permute-start(f32[864,64]{0,1:T(8,128)S(1)} %maximum_select_fusion.1), channel_id=1, source_target_pairs={{0,8},{1,9},{2,10},{3,11},{4,12},{5,13},{6,14},{7,15},{8,0},{9,1},... | collective-permute-start | bytes 663560 | tf_op jit(solution)/shard_map/ppermute | solution.py:95
  125.8 5.9 %copy-start.3 = (bf16[1,108,1728]{2,1,0:T(8,128)(2,1)S(1)}, bf16[1,108,1728]{2,1,0:T(8,128)(2,1)}, u32[]{:S(2)}) copy-start(bf16[1,108,1728]{2,1,0:T(8,128)(2,1)} %param.12) | copy-start | bytes 1119748
Sparse Core Ops, SparseCore 0:
  10.7 115.4 all-gather.1

commit v3 on v1

--- a/solution.py
+++ b/solution.py
@@ -78,21 +78,105 @@
     return (column_ids == start_row + row_ids).astype(jnp.float32)
 
 
-def doubling_sum(value, axis):
+def halving_sum(value, axis):
     count = lax.axis_size(axis)
-    assert count & (count - 1) == 0
+    assert count & (count - 1) == 0 and value.shape[0] % count == 0
+    index = lax.axis_index(axis)
     stride = 1
     while stride < count:
-        value = value + lax.ppermute(value, axis, [(i, i ^ stride) for i in range(count)])
+        half = value.shape[0] // 2
+        upper = (index // stride) % 2 == 1
+        keep = jnp.where(upper, value[half:], value[:half])
+        send = jnp.where(upper, value[:half], value[half:])
+        value = keep + lax.ppermute(send, axis, [(i, i ^ stride) for i in range(count)])
         stride *= 2
+    stride = count // 2
+    while stride >= 1:
+        other = lax.ppermute(value, axis, [(i, i ^ stride) for i in range(count)])
+        upper = (index // stride) % 2 == 1
+        value = jnp.where(upper, jnp.concatenate([other, value]), jnp.concatenate([value, other]))
+        stride //= 2
     return value
+
+
+def compressed_products(gathered, a_rows, own_eye, shard_count, row_total):
+    kept = shard_count // 2 + 1
+    order_full = a_rows.shape[1]
+    mirrored = shard_count - kept
+    magnitudes = jnp.abs(gathered.astype(jnp.float32))
+    direct_sums = jnp.sum(jnp.sum(magnitudes, axis=3), axis=1)
+    column_sums = jnp.sum(magnitudes, axis=2)
+    for offset in range(1, mirrored + 1):
+        direct_sums = direct_sums + jnp.roll(column_sums[:, offset], offset, axis=0)
+    step_size = 1.0 / jnp.max(direct_sums)
+    block_eye = jnp.logical_and(
+        lax.broadcasted_iota(jnp.int32, gathered.shape, 1) == 0,
+        lax.broadcasted_iota(jnp.int32, gathered.shape, 2)
+        == lax.broadcasted_iota(jnp.int32, gathered.shape, 3),
+    ).astype(jnp.float32)
+    resid_blocks = (block_eye - step_size * gathered.astype(jnp.float32)).astype(jnp.bfloat16)
+    direct_right = jnp.stack(
+        [jnp.roll(resid_blocks[:, offset], offset, axis=0) for offset in range(kept)], 0
+    )
+    mirror_right = resid_blocks[:, 1 : mirrored + 1].transpose(1, 0, 2, 3)
+
+    def times_resid0(left_rows):
+        left = left_rows.reshape(row_total, shard_count, row_total).transpose(1, 0, 2)
+        direct_left = jnp.stack([jnp.roll(left, offset, axis=0) for offset in range(kept)], 0)
+        mirror_left = jnp.stack(
+            [jnp.roll(left, -offset, axis=0) for offset in range(1, mirrored + 1)], 0
+        )
+        product = jnp.einsum(
+            "kjab,kjbc->jac", direct_left, direct_right, preferred_element_type=jnp.float32
+        ) + jnp.einsum(
+            "mjab,mjcb->jac", mirror_left, mirror_right, preferred_element_type=jnp.float32
+        )
+        return product.transpose(1, 0, 2).reshape(row_total, order_full)
+
+    resid0 = (own_eye - step_size * a_rows.astype(jnp.float32)).astype(jnp.bfloat16)
+    resid1 = times_resid0(resid0).astype(jnp.bfloat16)
+    cross_term = times_resid0(resid1)
+    return step_size, resid0, resid1, cross_term
+
+
+def dense_products(gathered, a_rows, own_eye):
+    row_total = a_rows.shape[0]
+    shard_count = gathered.shape[0]
+    full_values = gathered.astype(jnp.float32)
+    step_size = 1.0 / jnp.max(jnp.sum(jnp.abs(full_values), axis=2))
+    block_ids = lax.broadcasted_iota(jnp.int32, gathered.shape, 0)
+    row_ids = lax.broadcasted_iota(jnp.int32, gathered.shape, 1)
+    column_ids = lax.broadcasted_iota(jnp.int32, gathered.shape, 2)
+    full_eye = (column_ids == block_ids * row_total + row_ids).astype(jnp.float32)
+    full_resid0 = (full_eye - step_size * full_values).astype(jnp.bfloat16)
+    contract = (((1, 2), (0, 1)), ((), ()))
+    resid0 = (own_eye - step_size * a_rows.astype(jnp.float32)).astype(jnp.bfloat16)
+    resid1 = lax.dot_general(
+        resid0.reshape(row_total, shard_count, row_total), full_resid0, contract,
+        preferred_element_type=jnp.float32,
+    ).astype(jnp.bfloat16)
+    cross_term = lax.dot_general(
+        resid1.reshape(row_total, shard_count, row_total), full_resid0, contract,
+        preferred_element_type=jnp.float32,
+    )
+    return step_size, resid0, resid1, cross_term
 
 
 def shards(acts, preacts, top_grad, weights, a_factor, g_factor):
     section_index = lax.axis_index("section")
     section_count = lax.axis_size("section")
     tick_count = MICRO + section_count - 1
-    gathered = lax.all_gather(a_factor[0], "dp", axis=0, tiled=True)
+    shard_count = lax.axis_size("dp")
+    row_total = a_factor.shape[1]
+    compressed = shard_count % 2 == 0 and row_total >= 64
+    if compressed:
+        kept = shard_count // 2 + 1
+        own_blocks = a_factor[0].reshape(row_total, shard_count, row_total).transpose(1, 0, 2)
+        twice = jnp.concatenate([own_blocks, own_blocks], axis=0)
+        upper_blocks = lax.dynamic_slice_in_dim(twice, lax.axis_index("dp"), kept, 0)
+        gathered = lax.all_gather(upper_blocks, "dp", axis=0)
+    else:
+        gathered = lax.all_gather(a_factor[0], "dp", axis=0)
     inputs = acts[0, 0]
     pre_values = preacts[0, 0]
     upper_grads = top_grad[0]
@@ -128,19 +212,18 @@
     )
     last_sent, stored_grads, stored_slopes = lax.fori_loop(0, tick_count, one_tick, start_state)
     local_grad = back_weight(inputs[0], stored_slopes[0])
-    summed_grad = doubling_sum(local_grad, "dp")
+    summed_grad = halving_sum(local_grad, "dp")
     mean_grad = summed_grad / lax.axis_size("dp")
     a_rows = a_factor[0]
-    row_total = a_rows.shape[0]
     order_full = a_rows.shape[1]
     first_row = lax.axis_index("dp") * row_total
-    full_values = gathered.astype(jnp.float32)
-    step_size = 1.0 / jnp.max(jnp.sum(jnp.abs(full_values), axis=1))
-    full_resid0 = (jnp.eye(order_full, dtype=jnp.float32) - step_size * full_values).astype(jnp.bfloat16)
     own_eye = eye_rows(first_row, row_total, order_full)
-    resid0 = (own_eye - step_size * a_rows.astype(jnp.float32)).astype(jnp.bfloat16)
-    resid1 = jnp.dot(resid0, full_resid0, preferred_element_type=jnp.float32).astype(jnp.bfloat16)
-    cross_term = jnp.dot(resid1, full_resid0, preferred_element_type=jnp.float32)
+    if compressed:
+        step_size, resid0, resid1, cross_term = compressed_products(
+            gathered, a_rows, own_eye, shard_count, row_total
+        )
+    else:
+        step_size, resid0, resid1, cross_term = dense_products(gathered, a_rows, own_eye)
     inverse_rows = step_size * (
         own_eye + resid0.astype(jnp.float32) + resid1.astype(jnp.float32) + cross_term
     )

time: 240 us -> 143 us (0.60)
  waiting for transfers between devices: 140 us -> 45.8 us
  other arithmetic: 38.3 us -> 18.6 us
  local copies, waits for them, and re-layouts: 24.1 us -> 34.9 us
  matrix products: 10.2 us -> 13.1 us
  starting transfers between devices: 10.1 us -> 13 us
    ppermute x4 -> x8, waiting for transfers between devices: 99.2 us -> 41.7 us  [the longest x4 22.7 us: halving_sum(): lax.ppermute(send, axis, [(i, i ^ stride) for i in range(count)])]
    all_gather x1, waiting for transfers between devices: 37.1 us -> 0.02 us  [shards(): gathered = lax.all_gather(upper_blocks, 'dp', axis=0)]
    reduce_sum x1 -> x2, other arithmetic: 18.9 us -> 4.04 us  [the longest x1 4.01 us: compressed_products(): column_sums = jnp.sum(magnitudes, axis=2)]
    mul x1 -> x2, other arithmetic: 14.3 us -> 2.22 us  [the longest x1 1.68 us: shards(): step_size * (own_eye + resid0.astype(jnp.float32) + resid1.astype(jnp.flo...]
    unnamed x1 -> x35, other arithmetic: 0.01 us -> 4.16 us
    ppermute x4 -> x8, starting transfers between devices: 7.51 us -> 10.4 us  [the longest x4 7.54 us: halving_sum(): lax.ppermute(send, axis, [(i, i ^ stride) for i in range(count)])]
    dot_general x2 -> x4, matrix products: 2.72 us -> 5.2 us  [the longest x2 2.65 us: times_resid0(): jnp.einsum('kjab,kjbc->jac', direct_left, direct_right, preferred_element...]
    unnamed x37 -> x54, local copies, waits for them, and re-layouts: 8.38 us -> 10.8 us
  transfers between devices with their start and end apart: 7 -> 11, of which waited for: 7 -> 10; matrix products, arithmetic and copies ran while one was open for 12% -> 23% of each run, Pallas kernels for 0% -> 0%
where the time goes in v3:
time: 143 us; the launch traced here: 142 us
  waiting for transfers between devices  45.8 us (32%)
  local copies, waits for them, and re-layouts  34.9 us (24%)
  other arithmetic  18.6 us (13%)
  between operations  16.4 us (11%)
  matrix products  13.1 us (9%)
  starting transfers between devices  13 us (9%)
    ppermute x4, waiting for transfers between devices, halving_sum(): lax.ppermute(send, axis, [(i, i ^ stride) for i in range(count)])  22.7 us
    ppermute x4, waiting for transfers between devices, halving_sum(): other = lax.ppermute(value, axis, [(i, i ^ stride) for i in range(count)])  19 us
    unnamed x54, local copies, waits for them, and re-layouts  10.8 us
    while x60, local copies, waits for them, and re-layouts  7.65 us
    ppermute x4, starting transfers between devices, halving_sum(): lax.ppermute(send, axis, [(i, i ^ stride) for i in range(count)])  7.54 us
    unnamed x35, other arithmetic  4.16 us
    ppermute x2, waiting for transfers between devices, shifted(): lax.ppermute(value, axis, [(source, source + steps) for source in range(f...  4.09 us
    reduce_sum x1, other arithmetic, compressed_products(): column_sums = jnp.sum(magnitudes, axis=2)  4.01 us
  transfers between devices with their start and end apart: 11, of which 10 were waited for; matrix products, arithmetic and copies ran while one was open for 23% of the time, Pallas kernels for 0%

profile of v3, /device:TPU:0, one launch (start us, length us, event | category | flops | bytes accessed | tf_op | source)
XLA Modules:
  0.0 142.1 jit_solution(16063615422541310807)
XLA Ops:
  7.2 1.9 %reshape_squeeze.10 = bf16[108,16,108]{2,1,0:T(8,128)(2,1)S(1)} reshape(bf16[1,108,1728]{2,1,0:T(8,128)(2,1)} %param.12) | data formatting | bytes 746496 | tf_op jit(solution)/shard_map/reshape;squeeze | solution.py:174
  9.6 0.8 copy.129
  10.4 0.9 constant_dynamic-update-slice_fusion.26
  11.3 0.8 constant_dynamic-update-slice_fusion.25
  12.1 0.9 constant_dynamic-update-slice_fusion.24
  13.0 0.9 constant_dynamic-update-slice_fusion.23
  16.8 2.1 %reshape.169 = bf16[1728,512]{1,0:T(8,128)(2,1)} reshape(bf16[27,64,2,2,128]{4,3,2,1,0:T(2,128)(2,1)S(1)} %constant_dynamic-update-slice_fusion) | data formatting | bytes 3538944 | tf_op jit(solution)/shard_map/reshape | solution.py:44
  19.4 0.9 copy.170
  21.7 24.1 %while.20 = (s32[]{:T(128)}, bf16[64,2,2,128]{3,2,1,0:T(2,128)(2,1)}, bf16[1,64,2,2,128]{4,3,2,1,0:T(2,128)(2,1)}, bf16[1,64,2,2,128]{4,3,2,1,0:T(2,128)(2,1)}, ...) while((s32[]{:T(128)}, ...), condition=%wide.region_1.2_spmd.clone, body=%wide.region_0.1_spmd.clone.sunk | while | flops 113475592 | bytes 10772731 | solution.py:213
  21.7 1.3 collective-permute-start
  23.0 2.0 %collective-permute-done = bf16[64,2,2,128]{3,2,1,0:T(2,128)(2,1)S(1)} collective-permute-done((bf16[64,2,2,128]{3,2,1,0:T(2,128)(2,1)}, bf16[64,2,2,128]{3,2,1,0:T(2,128)(2,1)S(1)}, u32[]{:S(2)}, u32[]{:S(2)}) %collective-permute-start) | collective-permute-done | bytes 65568 | tf_op jit(solution)/shard_map/while/body/eval_jaxpr/ppermute | solution.py:13
  25.0 1.7 %fusion.262 = (bf16[1,64,2,2,128]{4,3,2,1,0:T(2,128)(2,1)}, bf16[64,2,2,128]{3,2,1,0:T(2,128)(2,1)S(1)}) fusion(pred[]{:T(512)S(6)} %and.68, bf16[1,64,2,2,128]{4,3,2,1,0:T(2,128)(2,1)} %get-tuple-element.429, bf16[64,2,2,128]{3,2,1,0:T(2,128)(2,1)S(1)} %collective-permute-done, bf16[1,64,2,2,128]{4,3,2,1,0:T(2,128)(2,1)} %get-tuple-element.443, ...), kind=kLoop, calls=%fused_computation.33.clone.1 | loop fusion | flops 131072 | bytes 393218 | tf_op jit(solution)/shard_map/while/body/eval_jaxpr/jit(dynamic_update_index_in_dim)/broadcast_in_dim | solution.py:203
  30.1 0.7 reshape.190
  30.8 1.5 %fusion.289 = bf16[64,512]{1,0:T(8,128)(2,1)S(1)} fusion(bf16[1728,512]{1,0:T(8,128)(2,1)S(1)} %reshape.190, bf16[1728,64]{1,0:T(8,128)(2,1)} %get-tuple-element.444), kind=kOutput, calls=%fused_computation.27.clone.1 | convolution fusion | flops 113278976 | bytes 2056192 | tf_op jit(solution)/shard_map/while/body/eval_jaxpr/dot_general | solution.py:49
  33.7 1.3 collective-permute-start
  35.0 2.0 %collective-permute-done = bf16[64,2,2,128]{3,2,1,0:T(2,128)(2,1)S(1)} collective-permute-done((bf16[64,2,2,128]{3,2,1,0:T(2,128)(2,1)}, bf16[64,2,2,128]{3,2,1,0:T(2,128)(2,1)S(1)}, u32[]{:S(2)}, u32[]{:S(2)}) %collective-permute-start) | collective-permute-done | bytes 65568 | tf_op jit(solution)/shard_map/while/body/eval_jaxpr/ppermute | solution.py:13
  37.1 1.7 %fusion.262 = (bf16[1,64,2,2,128]{4,3,2,1,0:T(2,128)(2,1)}, bf16[64,2,2,128]{3,2,1,0:T(2,128)(2,1)S(1)}) fusion(pred[]{:T(512)S(6)} %and.68, bf16[1,64,2,2,128]{4,3,2,1,0:T(2,128)(2,1)} %get-tuple-element.429, bf16[64,2,2,128]{3,2,1,0:T(2,128)(2,1)S(1)} %collective-permute-done, bf16[1,64,2,2,128]{4,3,2,1,0:T(2,128)(2,1)} %get-tuple-element.443, ...), kind=kLoop, calls=%fused_computation.33.clone.1 | loop fusion | flops 131072 | bytes 393218 | tf_op jit(solution)/shard_map/while/body/eval_jaxpr/jit(dynamic_update_index_in_dim)/broadcast_in_dim | solution.py:203
  42.1 0.7 reshape.190
  42.9 1.5 %fusion.289 = bf16[64,512]{1,0:T(8,128)(2,1)S(1)} fusion(bf16[1728,512]{1,0:T(8,128)(2,1)S(1)} %reshape.190, bf16[1728,64]{1,0:T(8,128)(2,1)} %get-tuple-element.444), kind=kOutput, calls=%fused_computation.27.clone.1 | convolution fusion | flops 113278976 | bytes 2056192 | tf_op jit(solution)/shard_map/while/body/eval_jaxpr/dot_general | solution.py:49
  45.8 0.9 reshape_squeeze.11
  46.7 2.1 %fusion.217 = f32[1728,64]{0,1:T(8,128)S(1)} fusion(bf16[1728,512]{1,0:T(8,128)(2,1)} %reshape.169, bf16[64,512]{1,0:T(8,128)(2,1)S(1)} %reshape_squeeze.11), kind=kOutput, calls=%fused_computation.403 | convolution fusion | flops 113246208 | bytes 2277376 | tf_op jit(solution)/shard_map/dot_general | solution.py:58
  48.9 3.0 %collective-permute-start.1 = (f32[864,64]{0,1:T(8,128)S(1)}, f32[864,64]{0,1:T(8,128)S(1)}, u32[]{:S(2)}, u32[]{:S(2)}) collective-permute-start(f32[864,64]{0,1:T(8,128)S(1)} %slice_select_fusion), channel_id=1, source_target_pairs={{0,1},{1,0},{2,3},{3,2},{4,5},{5,4},{6,7},{7,6},{8,9},{9,8},{10,11... | collective-permute-start | bytes 663560 | tf_op jit(solution)/shard_map/ppermute | solution.py:91
  52.0 6.0 %collective-permute-done.1 = f32[864,64]{0,1:T(8,128)S(1)} collective-permute-done((f32[864,64]{0,1:T(8,128)S(1)}, f32[864,64]{0,1:T(8,128)S(1)}, u32[]{:S(2)}, u32[]{:S(2)}) %collective-permute-start.1) | collective-permute-done | bytes 221216 | tf_op jit(solution)/shard_map/ppermute | solution.py:91
  58.2 1.8 %collective-permute-start.2 = (f32[432,64]{0,1:T(8,128)S(1)}, f32[432,64]{0,1:T(8,128)S(1)}, u32[]{:S(2)}, u32[]{:S(2)}) collective-permute-start(f32[432,64]{0,1:T(8,128)S(1)} %slice_select_fusion.1), channel_id=1, source_target_pairs={{0,2},{1,3},{2,0},{3,1},{4,6},{5,7},{6,4},{7,5},{8,10},{9,11},{10,... | collective-permute-start | bytes 331784 | tf_op jit(solution)/shard_map/ppermute | solution.py:91
  60.0 5.2 %collective-permute-done.2 = f32[432,64]{0,1:T(8,128)S(1)} collective-permute-done((f32[432,64]{0,1:T(8,128)S(1)}, f32[432,64]{0,1:T(8,128)S(1)}, u32[]{:S(2)}, u32[]{:S(2)}) %collective-permute-start.2) | collective-permute-done | bytes 110624 | tf_op jit(solution)/shard_map/ppermute | solution.py:91
  65.3 1.5 %collective-permute-start.3 = (f32[216,64]{0,1:T(8,128)S(1)}, f32[216,64]{0,1:T(8,128)S(1)}, u32[]{:S(2)}, u32[]{:S(2)}) collective-permute-start(f32[216,64]{0,1:T(8,128)S(1)} %slice_select_fusion.2), channel_id=1, source_target_pairs={{0,4},{1,5},{2,6},{3,7},{4,0},{5,1},{6,2},{7,3},{8,12},{9,13},{10,... | collective-permute-start | bytes 165896 | tf_op jit(solution)/shard_map/ppermute | solution.py:91
  68.3 5.2 %collective-permute-done.3 = f32[216,64]{0,1:T(8,128)S(1)} collective-permute-done((f32[216,64]{0,1:T(8,128)S(1)}, f32[216,64]{0,1:T(8,128)S(1)}, u32[]{:S(2)}, u32[]{:S(2)}) %collective-permute-start.3) | collective-permute-done | bytes 55328 | tf_op jit(solution)/shard_map/ppermute | solution.py:91
  73.7 1.2 collective-permute-start.4
  75.0 6.4 %collective-permute-done.4 = f32[108,64]{0,1:T(8,128)S(1)} collective-permute-done((f32[108,64]{0,1:T(8,128)S(1)}, f32[108,64]{0,1:T(8,128)S(1)}, u32[]{:S(2)}, u32[]{:S(2)}) %collective-permute-start.4) | collective-permute-done | bytes 27680 | tf_op jit(solution)/shard_map/ppermute | solution.py:91
  81.4 6.6 %collective-permute-done.5 = f32[108,64]{0,1:T(8,128)S(1)} collective-permute-done((f32[108,64]{0,1:T(8,128)S(1)}, f32[108,64]{0,1:T(8,128)S(1)}, u32[]{:S(2)}, u32[]{:S(2)}) %collective-permute-start.5) | collective-permute-done | bytes 27680 | tf_op jit(solution)/shard_map/ppermute | solution.py:95
  88.2 4.2 %collective-permute-done.6 = f32[216,64]{0,1:T(8,128)S(1)} collective-permute-done((f32[216,64]{0,1:T(8,128)S(1)}, f32[216,64]{0,1:T(8,128)S(1)}, u32[]{:S(2)}, u32[]{:S(2)}) %collective-permute-start.6) | collective-permute-done | bytes 55328 | tf_op jit(solution)/shard_map/ppermute | solution.py:95
  92.6 1.3 collective-permute-start.7
  93.9 3.7 %collective-permute-done.7 = f32[432,64]{0,1:T(8,128)S(1)} collective-permute-done((f32[432,64]{0,1:T(8,128)S(1)}, f32[432,64]{0,1:T(8,128)S(1)}, u32[]{:S(2)}, u32[]{:S(2)}) %collective-permute-start.7) | collective-permute-done | bytes 110624 | tf_op jit(solution)/shard_map/ppermute | solution.py:95
  97.7 1.5 %collective-permute-start.8 = (f32[864,64]{0,1:T(8,128)S(1)}, f32[864,64]{0,1:T(8,128)S(1)}, u32[]{:S(2)}, u32[]{:S(2)}) collective-permute-start(f32[864,64]{0,1:T(8,128)S(1)} %maximum_select_fusion.1), channel_id=1, source_target_pairs={{0,1},{1,0},{2,3},{3,2},{4,5},{5,4},{6,7},{7,6},{8,9},{9,8},{10,11... | collective-permute-start | bytes 663560 | tf_op jit(solution)/shard_map/ppermute | solution.py:95
  99.4 4.5 %collective-permute-done.8 = f32[864,64]{0,1:T(8,128)S(1)} collective-permute-done((f32[864,64]{0,1:T(8,128)S(1)}, f32[864,64]{0,1:T(8,128)S(1)}, u32[]{:S(2)}, u32[]{:S(2)}) %collective-permute-start.8) | collective-permute-done | bytes 221216 | tf_op jit(solution)/shard_map/ppermute | solution.py:95
  103.8 0.7 fusion.126
  104.6 4.0 %fusion.55 = (f32[144,108]{1,0:T(8,128)S(1)}, f32[144,108]{1,0:T(8,128)S(1)}) fusion(bf16[144,108,108]{2,1,0:T(8,128)(2,1)} %all-gather.3.cloned.1.call-done), kind=kLoop, calls=%fused_computation.90 | loop fusion | flops 6687360 | bytes 3483648 | tf_op jit(solution)/shard_map/reduce_sum | solution.py:108
  111.3 1.9 %copy-done.1 = bf16[144,108,108]{2,1,0:T(8,128)(2,1)S(1)} copy-done((bf16[144,108,108]{2,1,0:T(8,128)(2,1)S(1)}, bf16[144,108,108]{2,1,0:T(8,128)(2,1)}, u32[]{:S(2)}) %copy-start.1) | copy-done | bytes 3359256
  113.7 0.8 fusion.56
  117.3 1.3 convolution_bitcast_fusion
  119.3 1.4 bitcast_dynamic-update-slice_fusion.2
  122.5 1.1 fusion.63
  124.6 1.4 fusion.70
  126.2 1.3 reshape.170
  128.3 1.3 reshape.172
  130.0 1.7 %fusion.84 = f32[1,108,1728]{2,1,0:T(8,128)S(1)} fusion(f32[1,108,1728]{2,1,0:T(8,128)} %reshape.170, f32[1,108,1728]{2,1,0:T(8,128)} %reshape.172, bf16[1,108,1728]{2,1,0:T(8,128)(2,1)S(1)} %copy-done.4, s32[108]{0:T(128)S(1)} %iota_add_fusion, f32[]{:T(128)S(6)} %div.39), kind=kLoop, calls=%fused_computation.153 | loop fusion | flops 2052864 | bytes 2613172 | tf_op jit(solution)/shard_map/mul | solution.py:227
  131.7 1.7 %copy.168 = f32[1,108,1728]{2,0,1:T(1,128)} copy(f32[1,108,1728]{2,1,0:T(8,128)S(1)} %fusion.84) | data formatting | bytes 1492992
  133.4 1.9 %convolution_bitcast_fusion.1 = f32[1,108,64]{1,2,0:T(8,128)} fusion(f32[1728,64]{0,1:T(8,128)S(1)} %fusion.126, f32[108,1728]{1,0:T(8,128)S(1)} %reshape.168, f32[108,1728]{1,0:T(8,128)S(1)} %reshape.171, bf16[1,108,1728]{2,1,0:T(8,128)(2,1)S(1)} %copy-done.4, f32[]{:T(128)S(6)} %div.39, s32[108]{0:T(128)S(1)} %iota_add_fusion), kind=kOutput, calls=%fused_computation.134 | convolution fusion | flops 145380096 | bytes 2336692 | tf_op jit(solution)/shard_map/dot_general | solution.py:234
  (252 shorter events, 26.4 us)
Async XLA Ops:
  7.2 6.7 %copy-start = (bf16[1,1,1,64,2,2,128]{6,5,4,3,2,1,0:T(2,128)(2,1)S(1)}, bf16[1,1,1,64,2,2,128]{6,5,4,3,2,1,0:T(2,128)(2,1)}, u32[]{:S(2)}) copy-start(bf16[1,1,1,64,2,2,128]{6,5,4,3,2,1,0:T(2,128)(2,1)} %param.8) | copy-start | bytes 196612
  7.2 97.4 %all-gather.3.cloned.1.call-start = ((), (), s32[]{:S(2)}) async-start(), calls=%async_computation | async-start | bytes 4386816 | tf_op jit(solution)/shard_map/all_gather | solution.py:177
  9.2 9.8 %copy-start.2 = (bf16[108,16,108]{2,1,0:T(8,128)(2,1)}, bf16[108,16,108]{2,1,0:T(8,128)(2,1)S(1)}, u32[]{:S(2)}) copy-start(bf16[108,16,108]{2,1,0:T(8,128)(2,1)S(1)} %reshape_squeeze.10) | copy-start | bytes 1119748
  14.0 5.0 %copy-start.7 = (bf16[1,64,1728]{2,1,0:T(8,128)(2,1)S(1)}, bf16[1,64,1728]{2,1,0:T(8,128)(2,1)}, u32[]{:S(2)}) copy-start(bf16[1,64,1728]{2,1,0:T(8,128)(2,1)} %param.11) | copy-start | bytes 663556
  21.7 3.3 %collective-permute-start = (bf16[64,2,2,128]{3,2,1,0:T(2,128)(2,1)}, bf16[64,2,2,128]{3,2,1,0:T(2,128)(2,1)S(1)}, u32[]{:S(2)}, u32[]{:S(2)}) collective-permute-start(bf16[64,2,2,128]{3,2,1,0:T(2,128)(2,1)} %get-tuple-element.427), channel_id=1, source_target_pairs={{16,0},{17,1},{18,2},{19,3},{20,4},{21,5},{22,6},{23,7},{24,8},{25... | collective-permute-start | bytes 196616 | tf_op jit(solution)/shard_map/while/body/eval_jaxpr/ppermute | solution.py:13
  30.8 2.2 %copy-start.5 = (bf16[1,64,2,2,128]{4,3,2,1,0:T(2,128)(2,1)S(1)}, bf16[1,64,2,2,128]{4,3,2,1,0:T(2,128)(2,1)}, u32[]{:S(2)}) copy-start(bf16[1,64,2,2,128]{4,3,2,1,0:T(2,128)(2,1)} %get-tuple-element.428) | copy-start | bytes 196612 | tf_op jit(solution)/shard_map/while
  33.1 0.6 copy-start.6
  33.7 3.3 %collective-permute-start = (bf16[64,2,2,128]{3,2,1,0:T(2,128)(2,1)}, bf16[64,2,2,128]{3,2,1,0:T(2,128)(2,1)S(1)}, u32[]{:S(2)}, u32[]{:S(2)}) collective-permute-start(bf16[64,2,2,128]{3,2,1,0:T(2,128)(2,1)} %get-tuple-element.427), channel_id=1, source_target_pairs={{16,0},{17,1},{18,2},{19,3},{20,4},{21,5},{22,6},{23,7},{24,8},{25... | collective-permute-start | bytes 196616 | tf_op jit(solution)/shard_map/while/body/eval_jaxpr/ppermute | solution.py:13
  42.8 2.2 %copy-start.5 = (bf16[1,64,2,2,128]{4,3,2,1,0:T(2,128)(2,1)S(1)}, bf16[1,64,2,2,128]{4,3,2,1,0:T(2,128)(2,1)}, u32[]{:S(2)}) copy-start(bf16[1,64,2,2,128]{4,3,2,1,0:T(2,128)(2,1)} %get-tuple-element.428) | copy-start | bytes 196612 | tf_op jit(solution)/shard_map/while
  45.1 0.6 copy-start.6
  45.8 21.1 %copy-start.8 = (bf16[1,64,64]{2,1,0:T(8,128)(2,1)S(1)}, bf16[1,64,64]{2,1,0:T(8,128)(2,1)}, u32[]{:S(2)}) copy-start(bf16[1,64,64]{2,1,0:T(8,128)(2,1)} %param.13) | copy-start | bytes 24580
  48.9 9.0 %collective-permute-start.1 = (f32[864,64]{0,1:T(8,128)S(1)}, f32[864,64]{0,1:T(8,128)S(1)}, u32[]{:S(2)}, u32[]{:S(2)}) collective-permute-start(f32[864,64]{0,1:T(8,128)S(1)} %slice_select_fusion), channel_id=1, source_target_pairs={{0,1},{1,0},{2,3},{3,2},{4,5},{5,4},{6,7},{7,6},{8,9},{9,8},{10,11... | collective-permute-start | bytes 663560 | tf_op jit(solution)/shard_map/ppermute | solution.py:91
  58.2 7.0 %collective-permute-start.2 = (f32[432,64]{0,1:T(8,128)S(1)}, f32[432,64]{0,1:T(8,128)S(1)}, u32[]{:S(2)}, u32[]{:S(2)}) collective-permute-start(f32[432,64]{0,1:T(8,128)S(1)} %slice_select_fusion.1), channel_id=1, source_target_pairs={{0,2},{1,3},{2,0},{3,1},{4,6},{5,7},{6,4},{7,5},{8,10},{9,11},{10,... | collective-permute-start | bytes 331784 | tf_op jit(solution)/shard_map/ppermute | solution.py:91
  65.3 8.2 %collective-permute-start.3 = (f32[216,64]{0,1:T(8,128)S(1)}, f32[216,64]{0,1:T(8,128)S(1)}, u32[]{:S(2)}, u32[]{:S(2)}) collective-permute-start(f32[216,64]{0,1:T(8,128)S(1)} %slice_select_fusion.2), channel_id=1, source_target_pairs={{0,4},{1,5},{2,6},{3,7},{4,0},{5,1},{6,2},{7,3},{8,12},{9,13},{10,... | collective-permute-start | bytes 165896 | tf_op jit(solution)/shard_map/ppermute | solution.py:91
  73.7 7.7 %collective-permute-start.4 = (f32[108,64]{0,1:T(8,128)S(1)}, f32[108,64]{0,1:T(8,128)S(1)}, u32[]{:S(2)}, u32[]{:S(2)}) collective-permute-start(f32[108,64]{0,1:T(8,128)S(1)} %slice_select_fusion.3), channel_id=1, source_target_pairs={{0,8},{1,9},{2,10},{3,11},{4,12},{5,13},{6,14},{7,15},{8,0},{9,1},... | collective-permute-start | bytes 82952 | tf_op jit(solution)/shard_map/ppermute | solution.py:91
  81.4 6.6 %collective-permute-start.5 = (f32[108,64]{0,1:T(8,128)S(1)}, f32[108,64]{0,1:T(8,128)S(1)}, u32[]{:S(2)}, u32[]{:S(2)}) collective-permute-start(f32[108,64]{0,1:T(8,128)S(1)} %select_add_fusion.3), channel_id=1, source_target_pairs={{0,8},{1,9},{2,10},{3,11},{4,12},{5,13},{6,14},{7,15},{8,0},{9,1},... | collective-permute-start | bytes 82952 | tf_op jit(solution)/shard_map/ppermute | solution.py:95
  88.1 4.3 %collective-permute-start.6 = (f32[216,64]{0,1:T(8,128)S(1)}, f32[216,64]{0,1:T(8,128)S(1)}, u32[]{:S(2)}, u32[]{:S(2)}) collective-permute-start(f32[216,64]{0,1:T(8,128)S(1)} %maximum_select_fusion.3), channel_id=1, source_target_pairs={{0,4},{1,5},{2,6},{3,7},{4,0},{5,1},{6,2},{7,3},{8,12},{9,13},{10,... | collective-permute-start | bytes 165896 | tf_op jit(solution)/shard_map/ppermute | solution.py:95
  92.6 5.0 %collective-permute-start.7 = (f32[432,64]{0,1:T(8,128)S(1)}, f32[432,64]{0,1:T(8,128)S(1)}, u32[]{:S(2)}, u32[]{:S(2)}) collective-permute-start(f32[432,64]{0,1:T(8,128)S(1)} %maximum_select_fusion.2), channel_id=1, source_target_pairs={{0,2},{1,3},{2,0},{3,1},{4,6},{5,7},{6,4},{7,5},{8,10},{9,11},{10,... | collective-permute-start | bytes 331784 | tf_op jit(solution)/shard_map/ppermute | solution.py:95
  97.7 12.6 %copy-start.3 = (bf16[108,16,108]{2,1,0:T(8,128)(2,1)S(1)}, bf16[108,16,108]{2,1,0:T(8,128)(2,1)}, u32[]{:S(2)}) copy-start(bf16[108,16,108]{2,1,0:T(8,128)(2,1)} %copy-done.2) | copy-start | bytes 1119748
  97.7 6.1 %collective-permute-start.8 = (f32[864,64]{0,1:T(8,128)S(1)}, f32[864,64]{0,1:T(8,128)S(1)}, u32[]{:S(2)}, u32[]{:S(2)}) collective-permute-start(f32[864,64]{0,1:T(8,128)S(1)} %maximum_select_fusion.1), channel_id=1, source_target_pairs={{0,1},{1,0},{2,3},{3,2},{4,5},{5,4},{6,7},{7,6},{8,9},{9,8},{10,11... | collective-permute-start | bytes 663560 | tf_op jit(solution)/shard_map/ppermute | solution.py:95
  111.0 2.2 %copy-start.1 = (bf16[144,108,108]{2,1,0:T(8,128)(2,1)S(1)}, bf16[144,108,108]{2,1,0:T(8,128)(2,1)}, u32[]{:S(2)}) copy-start(bf16[144,108,108]{2,1,0:T(8,128)(2,1)} %all-gather.3.cloned.1.call-done) | copy-start | bytes 10077700
  127.5 2.5 %copy-start.4 = (bf16[1,108,1728]{2,1,0:T(8,128)(2,1)S(1)}, bf16[1,108,1728]{2,1,0:T(8,128)(2,1)}, u32[]{:S(2)}) copy-start(bf16[1,108,1728]{2,1,0:T(8,128)(2,1)} %param.12) | copy-start | bytes 1119748
Sparse Core Ops, SparseCore 0:
  10.8 79.6 all-gather.2

commit v4 on v3

--- a/solution.py
+++ b/solution.py
@@ -162,6 +162,25 @@
     return step_size, resid0, resid1, cross_term
 
 
+def conv_back_input(grad_out, weights_now):
+    channels = weights_now.shape[0]
+    kernel = weights_now.reshape(channels, KW, KW, KW, channels)[:, ::-1, ::-1, ::-1, :]
+    summed = lax.conv_general_dilated(
+        grad_out[None], kernel.transpose(4, 0, 1, 2, 3), (1, 1, 1), ((KW // 2, KW // 2),) * 3,
+        dimension_numbers=("NCDHW", "OIDHW", "NCDHW"), preferred_element_type=jnp.float32,
+    )
+    return summed[0].astype(jnp.bfloat16)
+
+
+def conv_back_weight(volume, grad_out):
+    channels = volume.shape[0]
+    summed = lax.conv_general_dilated(
+        volume[:, None], grad_out[:, None], (1, 1, 1), ((KW // 2, KW // 2),) * 3,
+        dimension_numbers=("NCDHW", "OIDHW", "NCDHW"), preferred_element_type=jnp.float32,
+    )
+    return summed.transpose(2, 3, 4, 0, 1).reshape(KW ** 3 * channels, grad_out.shape[0])
+
+
 def shards(acts, preacts, top_grad, weights, a_factor, g_factor):
     section_index = lax.axis_index("section")
     section_count = lax.axis_size("section")
@@ -180,38 +199,29 @@
     inputs = acts[0, 0]
     pre_values = preacts[0, 0]
     upper_grads = top_grad[0]
-    channels = weights.shape[1]
-    w_rows = weights[0].reshape(channels, -1, channels).transpose(1, 0, 2).reshape(-1, channels)
+    micro_count = inputs.shape[0]
     zero_field = jnp.zeros(inputs.shape[1:], jnp.bfloat16)
-
-    def one_tick(tick_index, carried):
-        outgoing, stored_grads, stored_slopes = carried
-        incoming = shifted(outgoing, "section", -1)
+    outgoing = zero_field
+    stored_grads = [zero_field] * micro_count
+    stored_slopes = [zero_field] * micro_count
+    for tick_index in range(micro_count + section_count - 1):
+        incoming = shifted(outgoing, "section", -1) if tick_index > 0 else zero_field
         micro_index = tick_index - (section_count - 1 - section_index)
-        is_valid = jnp.logical_and(micro_index >= 0, micro_index < MICRO)
-        clipped = jnp.clip(micro_index, 0, MICRO - 1)
+        is_valid = jnp.logical_and(micro_index >= 0, micro_index < micro_count)
+        clipped = jnp.clip(micro_index, 0, micro_count - 1)
         from_top = lax.dynamic_index_in_dim(upper_grads, clipped, 0, keepdims=False)
         arriving = jnp.where(section_index == section_count - 1, from_top, incoming)
         pre_now = lax.dynamic_index_in_dim(pre_values, clipped, 0, keepdims=False)
         grad_out = jnp.where(pre_now > 0, arriving, zero_field)
-        sending = back_input(grad_out, w_rows)
-        old_grad = lax.dynamic_index_in_dim(stored_grads, clipped, 0, keepdims=False)
-        old_slope = lax.dynamic_index_in_dim(stored_slopes, clipped, 0, keepdims=False)
-        stored_grads = lax.dynamic_update_index_in_dim(
-            stored_grads, jnp.where(is_valid, sending, old_grad), clipped, 0
-        )
-        stored_slopes = lax.dynamic_update_index_in_dim(
-            stored_slopes, jnp.where(is_valid, grad_out, old_slope), clipped, 0
-        )
-        return (sending, stored_grads, stored_slopes)
-
-    start_state = (
-        zero_field,
-        jnp.zeros(inputs.shape, jnp.bfloat16),
-        jnp.zeros(inputs.shape, jnp.bfloat16),
-    )
-    last_sent, stored_grads, stored_slopes = lax.fori_loop(0, tick_count, one_tick, start_state)
-    local_grad = back_weight(inputs[0], stored_slopes[0])
+        outgoing = conv_back_input(grad_out, weights[0])
+        for micro in range(micro_count):
+            keep = jnp.logical_and(is_valid, clipped == micro)
+            stored_grads[micro] = jnp.where(keep, outgoing, stored_grads[micro])
+            stored_slopes[micro] = jnp.where(keep, grad_out, stored_slopes[micro])
+    local_grad = conv_back_weight(inputs[0], stored_slopes[0])
+    for micro in range(1, micro_count):
+        local_grad = local_grad + conv_back_weight(inputs[micro], stored_slopes[micro])
+    stored_grads = jnp.stack(stored_grads, 0)
     summed_grad = halving_sum(local_grad, "dp")
     mean_grad = summed_grad / lax.axis_size("dp")
     a_rows = a_factor[0]

time: 143 us -> 136 us (0.951)
  local copies, waits for them, and re-layouts: 34.9 us -> 16.3 us
  waiting for transfers between devices: 45.8 us -> 61.4 us
  other arithmetic: 18.6 us -> 14.8 us
    ppermute x4, waiting for transfers between devices: 19 us -> 31 us  [halving_sum(): other = lax.ppermute(value, axis, [(i, i ^ stride) for i in range(count)])]
    while x60 -> x0, local copies, waits for them, and re-layouts: 7.65 us -> none
    ppermute x4, waiting for transfers between devices: 22.7 us -> 28.8 us  [halving_sum(): lax.ppermute(send, axis, [(i, i ^ stride) for i in range(count)])]
    dot_general x3 -> x0, matrix products: 5.11 us -> none  [the longest x2 2.99 us: back_input(): lax.dot_general(w_rows, columns, (((0,), (0,)), ((), ())), preferred_elem...]
    reshape x7 -> x0, local copies, waits for them, and re-layouts: 4.88 us -> none  [the longest x3 3.53 us: taps_stack(): stacked.reshape(len(pieces) * volume.shape[0], size_x * size_y * size_z)]
    unnamed x54 -> x28, local copies, waits for them, and re-layouts: 10.8 us -> 6.25 us
    transpose x0 -> x1, matrix products: none -> 3.67 us  [conv_back_weight(): summed.transpose(2, 3, 4, 0, 1)]
    broadcast_in_dim x2 -> x1, other arithmetic: 3.37 us -> 0.31 us  [conv_back_weight(): grad_out[:, None]]
  transfers between devices with their start and end apart: 11 -> 10, of which waited for: 10 -> 9; matrix products, arithmetic and copies ran while one was open for 23% -> 9% of each run, Pallas kernels for 0% -> 0%
where the time goes in v4:
time: 136 us
  waiting for transfers between devices  61.4 us (45%)
  between operations  16.5 us (12%)
  local copies, waits for them, and re-layouts  16.3 us (12%)
  other arithmetic  14.8 us (11%)
  starting transfers between devices  13.5 us (10%)
  matrix products  13.4 us (10%)
    ppermute x4, waiting for transfers between devices, halving_sum(): other = lax.ppermute(value, axis, [(i, i ^ stride) for i in range(count)])  31 us
    ppermute x4, waiting for transfers between devices, halving_sum(): lax.ppermute(send, axis, [(i, i ^ stride) for i in range(count)])  28.8 us
    ppermute x4, starting transfers between devices, halving_sum(): lax.ppermute(send, axis, [(i, i ^ stride) for i in range(count)])  8.23 us
    unnamed x28, local copies, waits for them, and re-layouts  6.25 us
    unnamed x34, other arithmetic  4.16 us
    reduce_sum x1, other arithmetic, compressed_products(): column_sums = jnp.sum(magnitudes, axis=2)  4.01 us
    ppermute x4, starting transfers between devices, halving_sum(): other = lax.ppermute(value, axis, [(i, i ^ stride) for i in range(count)])  3.74 us
    transpose x1, matrix products, conv_back_weight(): summed.transpose(2, 3, 4, 0, 1)  3.67 us
  transfers between devices with their start and end apart: 10, of which 9 were waited for; matrix products, arithmetic and copies ran while one was open for 9% of the time, Pallas kernels for 0%

profile of v4, /device:TPU:0, one launch (start us, length us, event | category | flops | bytes accessed | tf_op | source)
XLA Modules:
  0.0 135.8 jit_solution(17064481068163545085)
XLA Ops:
  7.2 2.0 %reshape_squeeze.8 = bf16[108,16,108]{2,1,0:T(8,128)(2,1)S(1)} reshape(bf16[1,108,1728]{2,1,0:T(8,128)(2,1)} %param.10) | data formatting | bytes 746496 | tf_op jit(solution)/shard_map/reshape;squeeze | solution.py:193
  9.2 0.4 fusion.82
  9.6 0.8 copy.115
  10.4 1.0 copy.104
  11.4 1.0 copy.105
  12.8 0.3 reshape_squeeze.7
  13.2 0.7 fusion.21
  14.1 1.5 %collective-permute-start = (bf16[64,2,2,128]{0,2,3,1:T(2,128)(2,1)S(1)}, bf16[64,2,2,128]{0,2,3,1:T(2,128)(2,1)S(1)}, u32[]{:S(2)}, u32[]{:S(2)}) collective-permute-start(bf16[64,2,2,128]{0,2,3,1:T(2,128)(2,1)S(1)} %slice_bitcast_fusion.25), channel_id=1, source_target_pairs={{16,0},{17,1},{18,2},{19,3},{20,4},{21,5},{22,6},{23,7},{24,8},{25... | collective-permute-start | bytes 196616 | tf_op jit(solution)/shard_map/ppermute | solution.py:13
  15.9 1.5 %collective-permute-done = bf16[64,2,2,128]{0,2,3,1:T(2,128)(2,1)S(1)} collective-permute-done((bf16[64,2,2,128]{0,2,3,1:T(2,128)(2,1)S(1)}, bf16[64,2,2,128]{0,2,3,1:T(2,128)(2,1)S(1)}, u32[]{:S(2)}, u32[]{:S(2)}) %collective-permute-start) | collective-permute-done | bytes 65568 | tf_op jit(solution)/shard_map/ppermute | solution.py:13
  17.4 0.3 fusion.108
  17.7 3.7 %fusion.93 = f32[3,3,3,64,64]{4,3,2,1,0:T(8,128)S(1)} fusion(bf16[64,1,2,2,128]{0,1,4,3,2:T(2,128)(2,1)S(1)} %copy.152, bf16[64,1,2,2,128]{0,3,4,2,1:T(2,128)(2,1)S(1)} %get-tuple-element.73), kind=kOutput, calls=%fused_computation.161 | convolution fusion | flops 50069504 | bytes 573440 | tf_op jit(solution)/shard_map/transpose | solution.py:181
  21.4 3.0 %collective-permute-start.1 = (f32[864,64]{1,0:T(8,128)S(1)}, f32[864,64]{1,0:T(8,128)S(1)}, u32[]{:S(2)}, u32[]{:S(2)}) collective-permute-start(f32[864,64]{1,0:T(8,128)S(1)} %slice_select_fusion), channel_id=1, source_target_pairs={{0,1},{1,0},{2,3},{3,2},{4,5},{5,4},{6,7},{7,6},{8,9},{9,8},{10,11... | collective-permute-start | bytes 663560 | tf_op jit(solution)/shard_map/ppermute | solution.py:91
  24.6 0.6 reduce_max.19
  25.9 10.8 %collective-permute-done.1 = f32[864,64]{1,0:T(8,128)S(1)} collective-permute-done((f32[864,64]{1,0:T(8,128)S(1)}, f32[864,64]{1,0:T(8,128)S(1)}, u32[]{:S(2)}, u32[]{:S(2)}) %collective-permute-start.1) | collective-permute-done | bytes 221216 | tf_op jit(solution)/shard_map/ppermute | solution.py:91
  36.7 1.6 %collective-permute-start.2 = (f32[432,64]{1,0:T(8,128)S(1)}, f32[432,64]{1,0:T(8,128)S(1)}, u32[]{:S(2)}, u32[]{:S(2)}) collective-permute-start(f32[432,64]{1,0:T(8,128)S(1)} %slice_select_fusion.1), channel_id=1, source_target_pairs={{0,2},{1,3},{2,0},{3,1},{4,6},{5,7},{6,4},{7,5},{8,10},{9,11},{10,... | collective-permute-start | bytes 331784 | tf_op jit(solution)/shard_map/ppermute | solution.py:91
  38.5 7.6 %collective-permute-done.2 = f32[432,64]{1,0:T(8,128)S(1)} collective-permute-done((f32[432,64]{1,0:T(8,128)S(1)}, f32[432,64]{1,0:T(8,128)S(1)}, u32[]{:S(2)}, u32[]{:S(2)}) %collective-permute-start.2) | collective-permute-done | bytes 110624 | tf_op jit(solution)/shard_map/ppermute | solution.py:91
  46.2 1.1 collective-permute-start.3
  47.5 5.7 %collective-permute-done.3 = f32[216,64]{1,0:T(8,128)S(1)} collective-permute-done((f32[216,64]{1,0:T(8,128)S(1)}, f32[216,64]{1,0:T(8,128)S(1)}, u32[]{:S(2)}, u32[]{:S(2)}) %collective-permute-start.3) | collective-permute-done | bytes 55328 | tf_op jit(solution)/shard_map/ppermute | solution.py:91
  53.2 2.4 %collective-permute-start.4 = (f32[108,64]{1,0:T(8,128)S(1)}, f32[108,64]{1,0:T(8,128)S(1)}, u32[]{:S(2)}, u32[]{:S(2)}) collective-permute-start(f32[108,64]{1,0:T(8,128)S(1)} %slice_select_fusion.3), channel_id=1, source_target_pairs={{0,8},{1,9},{2,10},{3,11},{4,12},{5,13},{6,14},{7,15},{8,0},{9,1},... | collective-permute-start | bytes 82952 | tf_op jit(solution)/shard_map/ppermute | solution.py:91
  55.6 4.7 %collective-permute-done.4 = f32[108,64]{1,0:T(8,128)S(1)} collective-permute-done((f32[108,64]{1,0:T(8,128)S(1)}, f32[108,64]{1,0:T(8,128)S(1)}, u32[]{:S(2)}, u32[]{:S(2)}) %collective-permute-start.4) | collective-permute-done | bytes 27680 | tf_op jit(solution)/shard_map/ppermute | solution.py:91
  60.4 0.5 collective-permute-start.5
  60.9 4.6 %collective-permute-done.5 = f32[108,64]{1,0:T(8,128)S(1)} collective-permute-done((f32[108,64]{1,0:T(8,128)S(1)}, f32[108,64]{1,0:T(8,128)S(1)}, u32[]{:S(2)}, u32[]{:S(2)}) %collective-permute-start.5) | collective-permute-done | bytes 27680 | tf_op jit(solution)/shard_map/ppermute | solution.py:95
  65.8 11.5 %collective-permute-done.6 = f32[216,64]{1,0:T(8,128)S(1)} collective-permute-done((f32[216,64]{1,0:T(8,128)S(1)}, f32[216,64]{1,0:T(8,128)S(1)}, u32[]{:S(2)}, u32[]{:S(2)}) %collective-permute-start.6) | collective-permute-done | bytes 55328 | tf_op jit(solution)/shard_map/ppermute | solution.py:95
  77.4 1.6 %collective-permute-start.7 = (f32[432,64]{1,0:T(8,128)S(1)}, f32[432,64]{1,0:T(8,128)S(1)}, u32[]{:S(2)}, u32[]{:S(2)}) collective-permute-start(f32[432,64]{1,0:T(8,128)S(1)} %maximum_select_fusion.2), channel_id=1, source_target_pairs={{0,2},{1,3},{2,0},{3,1},{4,6},{5,7},{6,4},{7,5},{8,10},{9,11},{10,... | collective-permute-start | bytes 331784 | tf_op jit(solution)/shard_map/ppermute | solution.py:95
  79.0 0.7 fusion.23
  79.9 6.1 %collective-permute-done.7 = f32[432,64]{1,0:T(8,128)S(1)} collective-permute-done((f32[432,64]{1,0:T(8,128)S(1)}, f32[432,64]{1,0:T(8,128)S(1)}, u32[]{:S(2)}, u32[]{:S(2)}) %collective-permute-start.7) | collective-permute-done | bytes 110624 | tf_op jit(solution)/shard_map/ppermute | solution.py:95
  86.0 1.5 %collective-permute-start.8 = (f32[864,64]{1,0:T(8,128)S(1)}, f32[864,64]{1,0:T(8,128)S(1)}, u32[]{:S(2)}, u32[]{:S(2)}) collective-permute-start(f32[864,64]{1,0:T(8,128)S(1)} %maximum_select_fusion.1), channel_id=1, source_target_pairs={{0,1},{1,0},{2,3},{3,2},{4,5},{5,4},{6,7},{7,6},{8,9},{9,8},{10,11... | collective-permute-start | bytes 663560 | tf_op jit(solution)/shard_map/ppermute | solution.py:95
  87.7 0.7 copy.156
  88.4 8.7 %collective-permute-done.8 = f32[864,64]{1,0:T(8,128)S(1)} collective-permute-done((f32[864,64]{1,0:T(8,128)S(1)}, f32[864,64]{1,0:T(8,128)S(1)}, u32[]{:S(2)}, u32[]{:S(2)}) %collective-permute-start.8) | collective-permute-done | bytes 221216 | tf_op jit(solution)/shard_map/ppermute | solution.py:95
  97.1 1.2 fusion.26
  98.4 4.0 %fusion.1 = (f32[144,108]{1,0:T(8,128)S(1)}, f32[144,108]{1,0:T(8,128)S(1)}) fusion(bf16[144,108,108]{2,1,0:T(8,128)(2,1)} %all-gather.3.cloned.1.call-done), kind=kLoop, calls=%fused_computation.3 | loop fusion | flops 6687360 | bytes 3483648 | tf_op jit(solution)/shard_map/reduce_sum | solution.py:108
  102.8 0.6 fusion.130
  105.1 1.7 %copy-done = bf16[144,108,108]{2,1,0:T(8,128)(2,1)S(1)} copy-done((bf16[144,108,108]{2,1,0:T(8,128)(2,1)S(1)}, bf16[144,108,108]{2,1,0:T(8,128)(2,1)}, u32[]{:S(2)}) %copy-start) | copy-done | bytes 3359256
  106.8 0.5 convert_multiply_fusion
  107.4 0.8 fusion.2
  111.2 1.3 convolution_bitcast_fusion
  113.2 1.2 bitcast_dynamic-update-slice_fusion.1
  116.1 1.2 fusion.9
  118.2 1.4 %fusion.16 = f32[108,16,108]{2,0,1:T(8,128)S(1)} fusion(f32[16,108,108]{2,1,0:T(8,128)S(1)} %fusion.9, bf16[9,16,108,108]{3,2,1,0:T(8,128)(2,1)S(1)} %fusion.74, bf16[9,16,108,108]{3,2,0,1:T(8,128)(2,1)S(1)} %get-tuple-element.78), kind=kOutput, calls=%fused_computation.18 | convolution fusion | flops 362983680 | bytes 8211456 | tf_op jit(solution)/shard_map/kjab,kjbc->jac/dot_general | solution.py:129
  119.6 0.3 copy.151
  119.9 1.3 reshape.203
  121.2 0.4 reshape.201
  121.7 0.3 copy.149
  121.9 1.3 reshape.219
  123.3 0.4 reshape.218
  123.7 1.7 %fusion.41 = f32[1,108,1728]{2,1,0:T(8,128)S(1)} fusion(f32[1,108,1728]{2,1,0:T(8,128)} %reshape.203, f32[1,108,1728]{2,1,0:T(8,128)} %reshape.219, bf16[1,108,1728]{2,1,0:T(8,128)(2,1)S(1)} %copy-done.1, s32[108]{0:T(128)S(1)} %iota_add_fusion, f32[]{:T(128)S(6)} %div.39), kind=kLoop, calls=%fused_computation.53 | loop fusion | flops 2052864 | bytes 2613172 | tf_op jit(solution)/shard_map/mul | solution.py:237
  125.4 1.7 %copy.157 = f32[1,108,1728]{2,0,1:T(1,128)} copy(f32[1,108,1728]{2,1,0:T(8,128)S(1)} %fusion.41) | data formatting | bytes 1492992
  127.1 1.9 %convolution_bitcast_fusion.1 = f32[1,108,64]{1,2,0:T(8,128)} fusion(f32[1728,64]{0,1:T(8,128)S(1)} %fusion.26, f32[108,1728]{1,0:T(8,128)S(1)} %reshape.201, f32[108,1728]{1,0:T(8,128)S(1)} %reshape.218, bf16[1,108,1728]{2,1,0:T(8,128)(2,1)S(1)} %copy-done.1, f32[]{:T(128)S(6)} %div.39, s32[108]{0:T(128)S(1)} %iota_add_fusion), kind=kOutput, calls=%fused_computation.26 | convolution fusion | flops 145380096 | bytes 2336692 | tf_op jit(solution)/shard_map/dot_general | solution.py:244
  (158 shorter events, 9.1 us)
Async XLA Ops:
  7.2 6.0 %copy-start.5 = (pred[8,17]{0,1:T(8,128)(4,1)S(1)}, pred[8,17]{0,1:T(8,128)(4,1)}, u32[]{:S(2)}) copy-start(pred[8,17]{0,1:T(8,128)(4,1)} %constant.134) | copy-start | bytes 412
  7.2 5.7 %copy-start.2 = (bf16[1,64,1728]{2,1,0:T(8,128)(2,1)S(1)}, bf16[1,64,1728]{2,1,0:T(8,128)(2,1)}, u32[]{:S(2)}) copy-start(bf16[1,64,1728]{2,1,0:T(8,128)(2,1)} %param.9) | copy-start | bytes 663556
  7.2 8.5 %copy-start.3 = (bf16[1,1,1,64,2,2,128]{6,5,4,3,2,1,0:T(2,128)(2,1)S(1)}, bf16[1,1,1,64,2,2,128]{6,5,4,3,2,1,0:T(2,128)(2,1)}, u32[]{:S(2)}) copy-start(bf16[1,1,1,64,2,2,128]{6,5,4,3,2,1,0:T(2,128)(2,1)} %param.6) | copy-start | bytes 196612
  7.2 91.2 %all-gather.3.cloned.1.call-start = ((), (), s32[]{:S(2)}) async-start(), calls=%async_computation | async-start | bytes 4386816 | tf_op jit(solution)/shard_map/all_gather | solution.py:196
  14.1 3.2 %collective-permute-start = (bf16[64,2,2,128]{0,2,3,1:T(2,128)(2,1)S(1)}, bf16[64,2,2,128]{0,2,3,1:T(2,128)(2,1)S(1)}, u32[]{:S(2)}, u32[]{:S(2)}) collective-permute-start(bf16[64,2,2,128]{0,2,3,1:T(2,128)(2,1)S(1)} %slice_bitcast_fusion.25), channel_id=1, source_target_pairs={{16,0},{17,1},{18,2},{19,3},{20,4},{21,5},{22,6},{23,7},{24,8},{25... | collective-permute-start | bytes 196616 | tf_op jit(solution)/shard_map/ppermute | solution.py:13
  17.7 6.8 %copy-start.4 = (bf16[1,64,64]{2,1,0:T(8,128)(2,1)S(1)}, bf16[1,64,64]{2,1,0:T(8,128)(2,1)}, u32[]{:S(2)}) copy-start(bf16[1,64,64]{2,1,0:T(8,128)(2,1)} %param.11) | copy-start | bytes 24580
  21.4 15.2 %collective-permute-start.1 = (f32[864,64]{1,0:T(8,128)S(1)}, f32[864,64]{1,0:T(8,128)S(1)}, u32[]{:S(2)}, u32[]{:S(2)}) collective-permute-start(f32[864,64]{1,0:T(8,128)S(1)} %slice_select_fusion), channel_id=1, source_target_pairs={{0,1},{1,0},{2,3},{3,2},{4,5},{5,4},{6,7},{7,6},{8,9},{9,8},{10,11... | collective-permute-start | bytes 663560 | tf_op jit(solution)/shard_map/ppermute | solution.py:91
  36.7 9.4 %collective-permute-start.2 = (f32[432,64]{1,0:T(8,128)S(1)}, f32[432,64]{1,0:T(8,128)S(1)}, u32[]{:S(2)}, u32[]{:S(2)}) collective-permute-start(f32[432,64]{1,0:T(8,128)S(1)} %slice_select_fusion.1), channel_id=1, source_target_pairs={{0,2},{1,3},{2,0},{3,1},{4,6},{5,7},{6,4},{7,5},{8,10},{9,11},{10,... | collective-permute-start | bytes 331784 | tf_op jit(solution)/shard_map/ppermute | solution.py:91
  46.2 7.0 %collective-permute-start.3 = (f32[216,64]{1,0:T(8,128)S(1)}, f32[216,64]{1,0:T(8,128)S(1)}, u32[]{:S(2)}, u32[]{:S(2)}) collective-permute-start(f32[216,64]{1,0:T(8,128)S(1)} %slice_select_fusion.2), channel_id=1, source_target_pairs={{0,4},{1,5},{2,6},{3,7},{4,0},{5,1},{6,2},{7,3},{8,12},{9,13},{10,... | collective-permute-start | bytes 165896 | tf_op jit(solution)/shard_map/ppermute | solution.py:91
  53.2 7.2 %collective-permute-start.4 = (f32[108,64]{1,0:T(8,128)S(1)}, f32[108,64]{1,0:T(8,128)S(1)}, u32[]{:S(2)}, u32[]{:S(2)}) collective-permute-start(f32[108,64]{1,0:T(8,128)S(1)} %slice_select_fusion.3), channel_id=1, source_target_pairs={{0,8},{1,9},{2,10},{3,11},{4,12},{5,13},{6,14},{7,15},{8,0},{9,1},... | collective-permute-start | bytes 82952 | tf_op jit(solution)/shard_map/ppermute | solution.py:91
  60.4 5.1 %collective-permute-start.5 = (f32[108,64]{1,0:T(8,128)S(1)}, f32[108,64]{1,0:T(8,128)S(1)}, u32[]{:S(2)}, u32[]{:S(2)}) collective-permute-start(f32[108,64]{1,0:T(8,128)S(1)} %select_add_fusion.3), channel_id=1, source_target_pairs={{0,8},{1,9},{2,10},{3,11},{4,12},{5,13},{6,14},{7,15},{8,0},{9,1},... | collective-permute-start | bytes 82952 | tf_op jit(solution)/shard_map/ppermute | solution.py:95
  65.6 11.8 %collective-permute-start.6 = (f32[216,64]{1,0:T(8,128)S(1)}, f32[216,64]{1,0:T(8,128)S(1)}, u32[]{:S(2)}, u32[]{:S(2)}) collective-permute-start(f32[216,64]{1,0:T(8,128)S(1)} %maximum_select_fusion.3), channel_id=1, source_target_pairs={{0,4},{1,5},{2,6},{3,7},{4,0},{5,1},{6,2},{7,3},{8,12},{9,13},{10,... | collective-permute-start | bytes 165896 | tf_op jit(solution)/shard_map/ppermute | solution.py:95
  77.4 8.6 %collective-permute-start.7 = (f32[432,64]{1,0:T(8,128)S(1)}, f32[432,64]{1,0:T(8,128)S(1)}, u32[]{:S(2)}, u32[]{:S(2)}) collective-permute-start(f32[432,64]{1,0:T(8,128)S(1)} %maximum_select_fusion.2), channel_id=1, source_target_pairs={{0,2},{1,3},{2,0},{3,1},{4,6},{5,7},{6,4},{7,5},{8,10},{9,11},{10,... | collective-permute-start | bytes 331784 | tf_op jit(solution)/shard_map/ppermute | solution.py:95
  86.0 11.1 %collective-permute-start.8 = (f32[864,64]{1,0:T(8,128)S(1)}, f32[864,64]{1,0:T(8,128)S(1)}, u32[]{:S(2)}, u32[]{:S(2)}) collective-permute-start(f32[864,64]{1,0:T(8,128)S(1)} %maximum_select_fusion.1), channel_id=1, source_target_pairs={{0,1},{1,0},{2,3},{3,2},{4,5},{5,4},{6,7},{7,6},{8,9},{9,8},{10,11... | collective-permute-start | bytes 663560 | tf_op jit(solution)/shard_map/ppermute | solution.py:95
  104.7 2.2 %copy-start = (bf16[144,108,108]{2,1,0:T(8,128)(2,1)S(1)}, bf16[144,108,108]{2,1,0:T(8,128)(2,1)}, u32[]{:S(2)}) copy-start(bf16[144,108,108]{2,1,0:T(8,128)(2,1)} %all-gather.3.cloned.1.call-done) | copy-start | bytes 10077700
  119.9 3.8 %copy-start.1 = (bf16[1,108,1728]{2,1,0:T(8,128)(2,1)S(1)}, bf16[1,108,1728]{2,1,0:T(8,128)(2,1)}, u32[]{:S(2)}) copy-start(bf16[1,108,1728]{2,1,0:T(8,128)(2,1)} %param.10) | copy-start | bytes 1119748
Sparse Core Ops, SparseCore 0:
  11.4 85.9 all-gather.2

commit v5 on v4

--- a/solution.py
+++ b/solution.py
@@ -1,4 +1,5 @@
 import jax
+import numpy as np
 import jax.numpy as jnp
 from jax import lax
 from jax.sharding import PartitionSpec as P
@@ -99,44 +100,49 @@
     return value
 
 
-def compressed_products(gathered, a_rows, own_eye, shard_count, row_total):
+def compressed_products(gathered, a_rows, own_eye, shard_count, row_total, step_size):
     kept = shard_count // 2 + 1
     order_full = a_rows.shape[1]
     mirrored = shard_count - kept
-    magnitudes = jnp.abs(gathered.astype(jnp.float32))
-    direct_sums = jnp.sum(jnp.sum(magnitudes, axis=3), axis=1)
-    column_sums = jnp.sum(magnitudes, axis=2)
-    for offset in range(1, mirrored + 1):
-        direct_sums = direct_sums + jnp.roll(column_sums[:, offset], offset, axis=0)
-    step_size = 1.0 / jnp.max(direct_sums)
     block_eye = jnp.logical_and(
         lax.broadcasted_iota(jnp.int32, gathered.shape, 1) == 0,
         lax.broadcasted_iota(jnp.int32, gathered.shape, 2)
         == lax.broadcasted_iota(jnp.int32, gathered.shape, 3),
     ).astype(jnp.float32)
     resid_blocks = (block_eye - step_size * gathered.astype(jnp.float32)).astype(jnp.bfloat16)
-    direct_right = jnp.stack(
-        [jnp.roll(resid_blocks[:, offset], offset, axis=0) for offset in range(kept)], 0
-    )
+    columns = np.arange(shard_count)[None, :]
+    direct_index = (columns - np.arange(kept)[:, None]) % shard_count
+    mirror_index = (columns + np.arange(1, mirrored + 1)[:, None]) % shard_count
+    direct_right = resid_blocks[direct_index, np.arange(kept)[:, None]]
     mirror_right = resid_blocks[:, 1 : mirrored + 1].transpose(1, 0, 2, 3)
 
-    def times_resid0(left_rows):
-        left = left_rows.reshape(row_total, shard_count, row_total).transpose(1, 0, 2)
-        direct_left = jnp.stack([jnp.roll(left, offset, axis=0) for offset in range(kept)], 0)
-        mirror_left = jnp.stack(
-            [jnp.roll(left, -offset, axis=0) for offset in range(1, mirrored + 1)], 0
-        )
-        product = jnp.einsum(
-            "kjab,kjbc->jac", direct_left, direct_right, preferred_element_type=jnp.float32
+    def times_resid0(left):
+        return jnp.einsum(
+            "kjab,kjbc->jac", left[direct_index], direct_right, preferred_element_type=jnp.float32
         ) + jnp.einsum(
-            "mjab,mjcb->jac", mirror_left, mirror_right, preferred_element_type=jnp.float32
-        )
-        return product.transpose(1, 0, 2).reshape(row_total, order_full)
+            "mjab,mjcb->jac", left[mirror_index], mirror_right, preferred_element_type=jnp.float32
+        )
+
+    def as_blocks(rows):
+        return rows.reshape(row_total, shard_count, row_total).transpose(1, 0, 2)
 
     resid0 = (own_eye - step_size * a_rows.astype(jnp.float32)).astype(jnp.bfloat16)
-    resid1 = times_resid0(resid0).astype(jnp.bfloat16)
+    resid1 = times_resid0(as_blocks(resid0)).astype(jnp.bfloat16)
     cross_term = times_resid0(resid1)
-    return step_size, resid0, resid1, cross_term
+    total = (
+        as_blocks(own_eye) + as_blocks(resid0).astype(jnp.float32) + resid1.astype(jnp.float32)
+        + cross_term
+    )
+    return (step_size * total).transpose(1, 0, 2).reshape(row_total, order_full)
+
+
+def largest(value, axis):
+    count = lax.axis_size(axis)
+    stride = 1
+    while stride < count:
+        value = jnp.maximum(value, lax.ppermute(value, axis, [(i, i ^ stride) for i in range(count)]))
+        stride *= 2
+    return value
 
 
 def dense_products(gathered, a_rows, own_eye):
@@ -194,6 +200,8 @@
         twice = jnp.concatenate([own_blocks, own_blocks], axis=0)
         upper_blocks = lax.dynamic_slice_in_dim(twice, lax.axis_index("dp"), kept, 0)
         gathered = lax.all_gather(upper_blocks, "dp", axis=0)
+        local_largest = jnp.max(jnp.sum(jnp.abs(a_factor[0].astype(jnp.float32)), axis=1))
+        step_size = 1.0 / largest(local_largest, "dp")
     else:
         gathered = lax.all_gather(a_factor[0], "dp", axis=0)
     inputs = acts[0, 0]
@@ -229,14 +237,14 @@
     first_row = lax.axis_index("dp") * row_total
     own_eye = eye_rows(first_row, row_total, order_full)
     if compressed:
-        step_size, resid0, resid1, cross_term = compressed_products(
-            gathered, a_rows, own_eye, shard_count, row_total
+        inverse_rows = compressed_products(
+            gathered, a_rows, own_eye, shard_count, row_total, step_size
         )
     else:
         step_size, resid0, resid1, cross_term = dense_products(gathered, a_rows, own_eye)
-    inverse_rows = step_size * (
-        own_eye + resid0.astype(jnp.float32) + resid1.astype(jnp.float32) + cross_term
-    )
+        inverse_rows = step_size * (
+            own_eye + resid0.astype(jnp.float32) + resid1.astype(jnp.float32) + cross_term
+        )
     g_inverse = local_inverse(g_factor[0])
     preconditioned = jnp.dot(
         mean_grad, g_inverse, precision=lax.Precision.HIGHEST, preferred_element_type=jnp.float32

time: 136 us -> 151 us (1.11)
  local copies, waits for them, and re-layouts: 16.3 us -> 30.2 us
  waiting for transfers between devices: 61.4 us -> 49.8 us
  starting transfers between devices: 13.5 us -> 23.7 us
  matrix products: 13.4 us -> 20 us
  other arithmetic: 14.8 us -> 8.49 us
  between operations: 16.5 us -> 18.6 us
    gather x0 -> x5, local copies, waits for them, and re-layouts: none -> 18.6 us  [the longest x2 6.71 us: times_resid0(): left[direct_index]]
    ppermute x4, waiting for transfers between devices: 31 us -> 13.3 us  [halving_sum(): other = lax.ppermute(value, axis, [(i, i ^ stride) for i in range(count)])]
    ppermute x0 -> x4, starting transfers between devices: none -> 13.7 us  [largest(): lax.ppermute(value, axis, [(i, i ^ stride) for i in range(count)])]
    dot_general x4, matrix products: 4.98 us -> 11.8 us  [the longest x2 9.52 us: times_resid0(): jnp.einsum('kjab,kjbc->jac', left[direct_index], direct_right, preferred_...]
    ppermute x4, waiting for transfers between devices: 28.8 us -> 34.2 us  [halving_sum(): lax.ppermute(send, axis, [(i, i ^ stride) for i in range(count)])]
    unnamed x34 -> x0, other arithmetic: 4.16 us -> none
    ppermute x4, starting transfers between devices: 8.23 us -> 4.35 us  [halving_sum(): lax.ppermute(send, axis, [(i, i ^ stride) for i in range(count)])]
    reduce_sum x2 -> x1, other arithmetic: 4.04 us -> 0.17 us  [shards(): jnp.sum(jnp.abs(a_factor[0].astype(jnp.float32)), axis=1)]
  transfers between devices with their start and end apart: 10 -> 14, of which waited for: 9 -> 10; matrix products, arithmetic and copies ran while one was open for 9% -> 13% of each run, Pallas kernels for 0% -> 0%
where the time goes in v5:
time: 151 us
  waiting for transfers between devices  49.8 us (33%)
  local copies, waits for them, and re-layouts  30.2 us (20%)
  starting transfers between devices  23.7 us (16%)
  matrix products  20 us (13%)
  between operations  18.6 us (12%)
  other arithmetic  8.49 us (6%)
    ppermute x4, waiting for transfers between devices, halving_sum(): lax.ppermute(send, axis, [(i, i ^ stride) for i in range(count)])  34.2 us
    ppermute x4, starting transfers between devices, largest(): lax.ppermute(value, axis, [(i, i ^ stride) for i in range(count)])  13.7 us
    ppermute x4, waiting for transfers between devices, halving_sum(): other = lax.ppermute(value, axis, [(i, i ^ stride) for i in range(count)])  13.3 us
    dot_general x2, matrix products, times_resid0(): jnp.einsum('kjab,kjbc->jac', left[direct_index], direct_right, preferred_...  9.52 us
    gather x2, local copies, waits for them, and re-layouts, times_resid0(): left[direct_index]  6.71 us
    gather x1, local copies, waits for them, and re-layouts, compressed_products(): direct_right = resid_blocks[direct_index, np.arange(kept)[:, None]]  6.55 us
    gather x2, local copies, waits for them, and re-layouts, times_resid0(): left[mirror_index]  5.31 us
    unnamed x27, local copies, waits for them, and re-layouts  4.41 us
  transfers between devices with their start and end apart: 14, of which 10 were waited for; matrix products, arithmetic and copies ran while one was open for 13% of the time, Pallas kernels for 0%

profile of v5, /device:TPU:0, one launch (start us, length us, event | category | flops | bytes accessed | tf_op | source)
XLA Modules:
  0.0 150.9 jit_solution(2558874992587100521)
XLA Ops:
  7.3 2.0 %squeeze.17 = bf16[108,16,108]{2,1,0:T(8,128)(2,1)S(1)} reshape(bf16[1,108,1728]{2,1,0:T(8,128)(2,1)} %param.19) | data formatting | bytes 746496 | tf_op jit(solution)/shard_map/squeeze | solution.py:203
  9.3 0.4 fusion.26
  9.7 0.8 copy.84
  10.5 1.0 copy.72
  11.5 1.0 copy.73
  13.3 0.7 fusion.12
  14.2 1.5 collective-permute-start
  15.9 0.6 reduce_max.18
  16.5 3.0 %collective-permute-start.1 = (f32[]{:T(128)}, f32[]{:T(128)}, u32[]{:S(2)}, u32[]{:S(2)}) collective-permute-start(f32[]{:T(128)} %reduce_max.18), channel_id=1, source_target_pairs={{0,1},{1,0},{2,3},{3,2},{4,5},{5,4},{6,7},{7,6},{8,9},{9,8},{10,11... | collective-permute-start | bytes 20 | tf_op jit(solution)/shard_map/ppermute | solution.py:143
  19.8 0.6 reduce_max.19
  21.5 3.7 %fusion.33 = f32[3,3,3,64,64]{4,3,2,1,0:T(8,128)S(1)} fusion(bf16[64,1,2,2,128]{0,1,4,3,2:T(2,128)(2,1)S(1)} %copy.87, bf16[64,1,2,2,128]{0,3,4,2,1:T(2,128)(2,1)S(1)} %get-tuple-element.12), kind=kOutput, calls=%fused_computation.61 | convolution fusion | flops 50069504 | bytes 573440 | tf_op jit(solution)/shard_map/transpose | solution.py:187
  25.6 12.8 %collective-permute-done.5 = f32[864,64]{1,0:T(8,128)S(1)} collective-permute-done((f32[864,64]{1,0:T(8,128)S(1)}, f32[864,64]{1,0:T(8,128)S(1)}, u32[]{:S(2)}, u32[]{:S(2)}) %collective-permute-start.5) | collective-permute-done | bytes 221216 | tf_op jit(solution)/shard_map/ppermute | solution.py:92
  38.5 1.6 %collective-permute-start.6 = (f32[432,64]{1,0:T(8,128)S(1)}, f32[432,64]{1,0:T(8,128)S(1)}, u32[]{:S(2)}, u32[]{:S(2)}) collective-permute-start(f32[432,64]{1,0:T(8,128)S(1)} %slice_select_fusion.1), channel_id=1, source_target_pairs={{0,2},{1,3},{2,0},{3,1},{4,6},{5,7},{6,4},{7,5},{8,10},{9,11},{10,... | collective-permute-start | bytes 331784 | tf_op jit(solution)/shard_map/ppermute | solution.py:92
  40.0 9.5 %collective-permute-done.6 = f32[432,64]{1,0:T(8,128)S(1)} collective-permute-done((f32[432,64]{1,0:T(8,128)S(1)}, f32[432,64]{1,0:T(8,128)S(1)}, u32[]{:S(2)}, u32[]{:S(2)}) %collective-permute-start.6) | collective-permute-done | bytes 110624 | tf_op jit(solution)/shard_map/ppermute | solution.py:92
  49.6 1.6 %collective-permute-start.7 = (f32[216,64]{1,0:T(8,128)S(1)}, f32[216,64]{1,0:T(8,128)S(1)}, u32[]{:S(2)}, u32[]{:S(2)}) collective-permute-start(f32[216,64]{1,0:T(8,128)S(1)} %slice_select_fusion.2), channel_id=1, source_target_pairs={{0,4},{1,5},{2,6},{3,7},{4,0},{5,1},{6,2},{7,3},{8,12},{9,13},{10,... | collective-permute-start | bytes 165896 | tf_op jit(solution)/shard_map/ppermute | solution.py:92
  51.3 7.2 %collective-permute-done.7 = f32[216,64]{1,0:T(8,128)S(1)} collective-permute-done((f32[216,64]{1,0:T(8,128)S(1)}, f32[216,64]{1,0:T(8,128)S(1)}, u32[]{:S(2)}, u32[]{:S(2)}) %collective-permute-start.7) | collective-permute-done | bytes 55328 | tf_op jit(solution)/shard_map/ppermute | solution.py:92
  58.5 1.1 collective-permute-start.8
  59.6 4.8 %collective-permute-done.8 = f32[108,64]{1,0:T(8,128)S(1)} collective-permute-done((f32[108,64]{1,0:T(8,128)S(1)}, f32[108,64]{1,0:T(8,128)S(1)}, u32[]{:S(2)}, u32[]{:S(2)}) %collective-permute-start.8) | collective-permute-done | bytes 27680 | tf_op jit(solution)/shard_map/ppermute | solution.py:92
  64.4 0.5 collective-permute-start.9
  66.2 3.5 %collective-permute-start.2 = (f32[]{:T(128)}, f32[]{:T(128)}, u32[]{:S(2)}, u32[]{:S(2)}) collective-permute-start(f32[]{:T(128)} %max.21), channel_id=1, source_target_pairs={{0,2},{1,3},{2,0},{3,1},{4,6},{5,7},{6,4},{7,5},{8,10},{9,11},{10,... | collective-permute-start | bytes 20 | tf_op jit(solution)/shard_map/ppermute | solution.py:143
  70.7 3.6 %collective-permute-start.3 = (f32[]{:T(128)}, f32[]{:T(128)}, u32[]{:S(2)}, u32[]{:S(2)}) collective-permute-start(f32[]{:T(128)} %max.22), channel_id=1, source_target_pairs={{0,4},{1,5},{2,6},{3,7},{4,0},{5,1},{6,2},{7,3},{8,12},{9,13},{10,... | collective-permute-start | bytes 20 | tf_op jit(solution)/shard_map/ppermute | solution.py:143
  75.3 3.6 %collective-permute-start.4 = (f32[]{:T(128)}, f32[]{:T(128)}, u32[]{:S(2)}, u32[]{:S(2)}) collective-permute-start(f32[]{:T(128)} %max.23), channel_id=1, source_target_pairs={{0,8},{1,9},{2,10},{3,11},{4,12},{5,13},{6,14},{7,15},{8,0},{9,1},... | collective-permute-start | bytes 20 | tf_op jit(solution)/shard_map/ppermute | solution.py:143
  78.9 1.7 %collective-permute-done.4 = f32[]{:T(128)} collective-permute-done((f32[]{:T(128)}, f32[]{:T(128)}, u32[]{:S(2)}, u32[]{:S(2)}) %collective-permute-start.4) | collective-permute-done | bytes 36 | tf_op jit(solution)/shard_map/ppermute | solution.py:143
  81.3 1.4 collective-permute-start.10
  83.0 3.4 %gather_fusion = bf16[144,108,108]{2,1,0:T(8,128)(2,1)} fusion(bf16[16,108,108]{2,1,0:T(8,128)(2,1)S(1)} %fusion.58, s32[1024]{0:T(1024)S(1)} %pad_clamp_fusion.1), kind=kCustom, calls=%fused_computation | custom fusion | bytes 6719040 | tf_op jit(solution)/shard_map/gather | solution.py:121
  86.3 2.7 %gather_fusion.2 = bf16[112,108,108]{2,1,0:T(8,128)(2,1)} fusion(bf16[16,108,108]{2,1,0:T(8,128)(2,1)S(1)} %fusion.58, s32[1024]{0:T(1024)S(1)} %pad_clamp_fusion), kind=kCustom, calls=%fused_computation.2 | custom fusion | bytes 5225920 | tf_op jit(solution)/shard_map/gather | solution.py:123
  89.2 2.5 %collective-permute-done.10 = f32[216,64]{1,0:T(8,128)S(1)} collective-permute-done((f32[216,64]{1,0:T(8,128)S(1)}, f32[216,64]{1,0:T(8,128)S(1)}, u32[]{:S(2)}, u32[]{:S(2)}) %collective-permute-start.10) | collective-permute-done | bytes 55328 | tf_op jit(solution)/shard_map/ppermute | solution.py:96
  91.7 1.6 %collective-permute-start.11 = (f32[432,64]{1,0:T(8,128)S(1)}, f32[432,64]{1,0:T(8,128)S(1)}, u32[]{:S(2)}, u32[]{:S(2)}) collective-permute-start(f32[432,64]{1,0:T(8,128)S(1)} %maximum_select_fusion.2), channel_id=1, source_target_pairs={{0,2},{1,3},{2,0},{3,1},{4,6},{5,7},{6,4},{7,5},{8,10},{9,11},{10,... | collective-permute-start | bytes 331784 | tf_op jit(solution)/shard_map/ppermute | solution.py:96
  93.3 0.7 fusion.14
  94.1 3.6 %collective-permute-done.11 = f32[432,64]{1,0:T(8,128)S(1)} collective-permute-done((f32[432,64]{1,0:T(8,128)S(1)}, f32[432,64]{1,0:T(8,128)S(1)}, u32[]{:S(2)}, u32[]{:S(2)}) %collective-permute-start.11) | collective-permute-done | bytes 110624 | tf_op jit(solution)/shard_map/ppermute | solution.py:96
  97.8 0.7 collective-permute-start.12
  98.6 0.7 copy.90
  99.3 7.1 %collective-permute-done.12 = f32[864,64]{1,0:T(8,128)S(1)} collective-permute-done((f32[864,64]{1,0:T(8,128)S(1)}, f32[864,64]{1,0:T(8,128)S(1)}, u32[]{:S(2)}, u32[]{:S(2)}) %collective-permute-start.12) | collective-permute-done | bytes 221216 | tf_op jit(solution)/shard_map/ppermute | solution.py:96
  106.4 1.2 fusion.19
  107.7 2.7 %convert_multiply_fusion = f32[144,108,108]{2,1,0:T(8,128)S(1)} fusion(bf16[144,108,108]{2,1,0:T(8,128)(2,1)} %all-gather.3.cloned.1.call-done, f32[]{:T(128)S(6)} %div.39), kind=kLoop, calls=%fused_computation.7 | loop fusion | flops 3359232 | bytes 10077700 | tf_op jit(solution)/shard_map/mul | solution.py:112
  110.4 2.8 %fusion = bf16[16,9,108,108]{3,2,0,1:T(8,128)(2,1)} fusion(f32[16,9,108,108]{3,2,1,0:T(8,128)S(1)} %bitcast.137, pred[9]{0:T(512)(128)(4,1)S(1)} %iota_compare_fusion.4), kind=kLoop, calls=%fused_computation.6 | loop fusion | flops 8398080 | bytes 10077705 | tf_op jit(solution)/shard_map/convert_element_type | solution.py:112
  113.2 6.5 %gather_fusion.1 = bf16[144,108,108]{2,1,0:T(8,128)(2,1)} fusion(bf16[16,9,108,108]{3,2,0,1:T(8,128)(2,1)} %fusion, s32[144]{0:T(256)S(1)} %copy-done.3), kind=kCustom, calls=%fused_computation.1 | custom fusion | bytes 6719616 | tf_op jit(solution)/shard_map/gather | solution.py:116
  119.7 4.8 %convolution_bitcast_fusion.1 = f32[16,108,108]{2,1,0:T(8,128)S(1)} fusion(bf16[9,16,108,108]{3,2,1,0:T(8,128)(2,1)} %bitcast.138, bf16[9,16,108,108]{3,2,1,0:T(8,128)(2,1)} %bitcast.135), kind=kOutput, calls=%fused_computation.16 | convolution fusion | flops 362797056 | bytes 7464960 | tf_op jit(solution)/shard_map/kjab,kjbc->jac/dot_general | solution.py:120
  124.5 0.8 copy-done.2
  125.3 1.1 fusion.11
  126.4 3.4 %gather_fusion.3 = bf16[144,108,108]{2,1,0:T(8,128)(2,1)} fusion(bf16[16,108,108]{2,1,0:T(8,128)(2,1)S(1)} %fusion.11, s32[1024]{0:T(1024)S(1)} %pad_clamp_fusion.1), kind=kCustom, calls=%fused_computation.3 | custom fusion | bytes 6719040 | tf_op jit(solution)/shard_map/gather | solution.py:121
  129.8 2.7 %gather_fusion.4 = bf16[112,108,108]{2,1,0:T(8,128)(2,1)} fusion(bf16[16,108,108]{2,1,0:T(8,128)(2,1)S(1)} %fusion.11, s32[1024]{0:T(1024)S(1)} %pad_clamp_fusion), kind=kCustom, calls=%fused_computation.4 | custom fusion | bytes 5225920 | tf_op jit(solution)/shard_map/gather | solution.py:123
  132.4 4.8 %convolution_bitcast_fusion = f32[16,108,108]{2,1,0:T(8,128)S(1)} fusion(bf16[9,16,108,108]{3,2,1,0:T(8,128)(2,1)} %bitcast.139, bf16[9,16,108,108]{3,2,1,0:T(8,128)(2,1)} %bitcast.136), kind=kOutput, calls=%fused_computation.15 | convolution fusion | flops 362797056 | bytes 7464960 | tf_op jit(solution)/shard_map/kjab,kjbc->jac/dot_general | solution.py:120
  137.2 0.8 copy-done.4
  138.0 1.2 fusion.9
  139.5 0.4 reshape.131
  139.9 2.5 %broadcast_in_dim_reshape.4 = f32[1,108,1728]{2,0,1:T(1,128)} reshape(f32[108,16,108]{2,1,0:T(8,128)S(1)} %copy.86) | data formatting | bytes 1492992 | tf_op jit(solution)/shard_map/broadcast_in_dim;reshape | solution.py:258
  142.4 1.6 %convolution_bitcast_fusion.2 = f32[1,108,64]{1,2,0:T(8,128)} fusion(f32[108,1728]{1,0:T(8,128)S(1)} %reshape.131, f32[1728,64]{0,1:T(8,128)S(1)} %fusion.19), kind=kOutput, calls=%fused_computation.30 | convolution fusion | flops 143327232 | bytes 1216512 | tf_op jit(solution)/shard_map/dot_general | solution.py:252
  (67 shorter events, 3.9 us)
Async XLA Ops:
  7.2 6.1 %copy-start.11 = (pred[8,17]{0,1:T(8,128)(4,1)S(1)}, pred[8,17]{0,1:T(8,128)(4,1)}, u32[]{:S(2)}) copy-start(pred[8,17]{0,1:T(8,128)(4,1)} %constant.156) | copy-start | bytes 412
  7.2 8.5 %copy-start.5 = (bf16[1,108,1728]{2,1,0:T(8,128)(2,1)S(1)}, bf16[1,108,1728]{2,1,0:T(8,128)(2,1)}, u32[]{:S(2)}) copy-start(bf16[1,108,1728]{2,1,0:T(8,128)(2,1)} %param.19) | copy-start | bytes 1119748
  7.2 5.7 %copy-start.6 = (bf16[1,64,1728]{2,1,0:T(8,128)(2,1)S(1)}, bf16[1,64,1728]{2,1,0:T(8,128)(2,1)}, u32[]{:S(2)}) copy-start(bf16[1,64,1728]{2,1,0:T(8,128)(2,1)} %param.18) | copy-start | bytes 663556
  7.2 12.2 %copy-start.7 = (bf16[1,1,1,64,2,2,128]{6,5,4,3,2,1,0:T(2,128)(2,1)S(1)}, bf16[1,1,1,64,2,2,128]{6,5,4,3,2,1,0:T(2,128)(2,1)}, u32[]{:S(2)}) copy-start(bf16[1,1,1,64,2,2,128]{6,5,4,3,2,1,0:T(2,128)(2,1)} %param.15) | copy-start | bytes 196612
  7.2 12.4 %copy-start.8 = (bf16[1,64,64]{2,1,0:T(8,128)(2,1)S(1)}, bf16[1,64,64]{2,1,0:T(8,128)(2,1)}, u32[]{:S(2)}) copy-start(bf16[1,64,64]{2,1,0:T(8,128)(2,1)} %param.20) | copy-start | bytes 24580
  7.2 100.4 %all-gather.3.cloned.1.call-start = ((), (), s32[]{:S(2)}) async-start(), calls=%async_computation | async-start | bytes 4386816 | tf_op jit(solution)/shard_map/all_gather | solution.py:202
  14.2 7.0 %collective-permute-start = (bf16[64,2,2,128]{0,2,3,1:T(2,128)(2,1)S(1)}, bf16[64,2,2,128]{0,2,3,1:T(2,128)(2,1)S(1)}, u32[]{:S(2)}, u32[]{:S(2)}) collective-permute-start(bf16[64,2,2,128]{0,2,3,1:T(2,128)(2,1)S(1)} %slice_bitcast_fusion.20), channel_id=1, source_target_pairs={{16,0},{17,1},{18,2},{19,3},{20,4},{21,5},{22,6},{23,7},{24,8},{25... | collective-permute-start | bytes 196616 | tf_op jit(solution)/shard_map/ppermute | solution.py:14
  16.5 48.4 %collective-permute-start.1 = (f32[]{:T(128)}, f32[]{:T(128)}, u32[]{:S(2)}, u32[]{:S(2)}) collective-permute-start(f32[]{:T(128)} %reduce_max.18), channel_id=1, source_target_pairs={{0,1},{1,0},{2,3},{3,2},{4,5},{5,4},{6,7},{7,6},{8,9},{9,8},{10,11... | collective-permute-start | bytes 20 | tf_op jit(solution)/shard_map/ppermute | solution.py:143
  21.5 18.5 %copy-start.9 = (s32[144]{0:T(256)S(1)}, s32[144]{0:T(256)}, u32[]{:S(2)}) copy-start(s32[144]{0:T(256)} %constant.175) | copy-start | bytes 1732
  25.3 26.0 %copy-start.10 = (s32[112]{0:T(128)S(1)}, s32[112]{0:T(128)}, u32[]{:S(2)}) copy-start(s32[112]{0:T(128)} %constant.184) | copy-start | bytes 1348
  25.4 13.0 %collective-permute-start.5 = (f32[864,64]{1,0:T(8,128)S(1)}, f32[864,64]{1,0:T(8,128)S(1)}, u32[]{:S(2)}, u32[]{:S(2)}) collective-permute-start(f32[864,64]{1,0:T(8,128)S(1)} %slice_select_fusion), channel_id=1, source_target_pairs={{0,1},{1,0},{2,3},{3,2},{4,5},{5,4},{6,7},{7,6},{8,9},{9,8},{10,11... | collective-permute-start | bytes 663560 | tf_op jit(solution)/shard_map/ppermute | solution.py:92
  38.5 11.1 %collective-permute-start.6 = (f32[432,64]{1,0:T(8,128)S(1)}, f32[432,64]{1,0:T(8,128)S(1)}, u32[]{:S(2)}, u32[]{:S(2)}) collective-permute-start(f32[432,64]{1,0:T(8,128)S(1)} %slice_select_fusion.1), channel_id=1, source_target_pairs={{0,2},{1,3},{2,0},{3,1},{4,6},{5,7},{6,4},{7,5},{8,10},{9,11},{10,... | collective-permute-start | bytes 331784 | tf_op jit(solution)/shard_map/ppermute | solution.py:92
  49.6 8.9 %collective-permute-start.7 = (f32[216,64]{1,0:T(8,128)S(1)}, f32[216,64]{1,0:T(8,128)S(1)}, u32[]{:S(2)}, u32[]{:S(2)}) collective-permute-start(f32[216,64]{1,0:T(8,128)S(1)} %slice_select_fusion.2), channel_id=1, source_target_pairs={{0,4},{1,5},{2,6},{3,7},{4,0},{5,1},{6,2},{7,3},{8,12},{9,13},{10,... | collective-permute-start | bytes 165896 | tf_op jit(solution)/shard_map/ppermute | solution.py:92
  58.5 5.8 %collective-permute-start.8 = (f32[108,64]{1,0:T(8,128)S(1)}, f32[108,64]{1,0:T(8,128)S(1)}, u32[]{:S(2)}, u32[]{:S(2)}) collective-permute-start(f32[108,64]{1,0:T(8,128)S(1)} %slice_select_fusion.3), channel_id=1, source_target_pairs={{0,8},{1,9},{2,10},{3,11},{4,12},{5,13},{6,14},{7,15},{8,0},{9,1},... | collective-permute-start | bytes 82952 | tf_op jit(solution)/shard_map/ppermute | solution.py:92
  64.4 16.9 %collective-permute-start.9 = (f32[108,64]{1,0:T(8,128)S(1)}, f32[108,64]{1,0:T(8,128)S(1)}, u32[]{:S(2)}, u32[]{:S(2)}) collective-permute-start(f32[108,64]{1,0:T(8,128)S(1)} %select_add_fusion.3), channel_id=1, source_target_pairs={{0,8},{1,9},{2,10},{3,11},{4,12},{5,13},{6,14},{7,15},{8,0},{9,1},... | collective-permute-start | bytes 82952 | tf_op jit(solution)/shard_map/ppermute | solution.py:96
  66.2 3.9 %collective-permute-start.2 = (f32[]{:T(128)}, f32[]{:T(128)}, u32[]{:S(2)}, u32[]{:S(2)}) collective-permute-start(f32[]{:T(128)} %max.21), channel_id=1, source_target_pairs={{0,2},{1,3},{2,0},{3,1},{4,6},{5,7},{6,4},{7,5},{8,10},{9,11},{10,... | collective-permute-start | bytes 20 | tf_op jit(solution)/shard_map/ppermute | solution.py:143
  70.7 3.9 %collective-permute-start.3 = (f32[]{:T(128)}, f32[]{:T(128)}, u32[]{:S(2)}, u32[]{:S(2)}) collective-permute-start(f32[]{:T(128)} %max.22), channel_id=1, source_target_pairs={{0,4},{1,5},{2,6},{3,7},{4,0},{5,1},{6,2},{7,3},{8,12},{9,13},{10,... | collective-permute-start | bytes 20 | tf_op jit(solution)/shard_map/ppermute | solution.py:143
  75.3 5.3 %collective-permute-start.4 = (f32[]{:T(128)}, f32[]{:T(128)}, u32[]{:S(2)}, u32[]{:S(2)}) collective-permute-start(f32[]{:T(128)} %max.23), channel_id=1, source_target_pairs={{0,8},{1,9},{2,10},{3,11},{4,12},{5,13},{6,14},{7,15},{8,0},{9,1},... | collective-permute-start | bytes 20 | tf_op jit(solution)/shard_map/ppermute | solution.py:143
  81.3 10.4 %collective-permute-start.10 = (f32[216,64]{1,0:T(8,128)S(1)}, f32[216,64]{1,0:T(8,128)S(1)}, u32[]{:S(2)}, u32[]{:S(2)}) collective-permute-start(f32[216,64]{1,0:T(8,128)S(1)} %maximum_select_fusion.3), channel_id=1, source_target_pairs={{0,4},{1,5},{2,6},{3,7},{4,0},{5,1},{6,2},{7,3},{8,12},{9,13},{10,... | collective-permute-start | bytes 165896 | tf_op jit(solution)/shard_map/ppermute | solution.py:96
  91.7 6.0 %collective-permute-start.11 = (f32[432,64]{1,0:T(8,128)S(1)}, f32[432,64]{1,0:T(8,128)S(1)}, u32[]{:S(2)}, u32[]{:S(2)}) collective-permute-start(f32[432,64]{1,0:T(8,128)S(1)} %maximum_select_fusion.2), channel_id=1, source_target_pairs={{0,2},{1,3},{2,0},{3,1},{4,6},{5,7},{6,4},{7,5},{8,10},{9,11},{10,... | collective-permute-start | bytes 331784 | tf_op jit(solution)/shard_map/ppermute | solution.py:96
  97.8 8.7 %collective-permute-start.12 = (f32[864,64]{1,0:T(8,128)S(1)}, f32[864,64]{1,0:T(8,128)S(1)}, u32[]{:S(2)}, u32[]{:S(2)}) collective-permute-start(f32[864,64]{1,0:T(8,128)S(1)} %maximum_select_fusion.1), channel_id=1, source_target_pairs={{0,1},{1,0},{2,3},{3,2},{4,5},{5,4},{6,7},{7,6},{8,9},{9,8},{10,11... | collective-permute-start | bytes 663560 | tf_op jit(solution)/shard_map/ppermute | solution.py:96
  110.4 2.8 %copy-start.3 = (s32[144]{0:T(256)S(1)}, s32[144]{0:T(256)}, u32[]{:S(2)}) copy-start(s32[144]{0:T(256)} %constant.183) | copy-start | bytes 1732
  119.7 4.8 %copy-start = (bf16[16,9,108,108]{3,2,0,1:T(8,128)(2,1)S(1)}, bf16[16,9,108,108]{3,2,0,1:T(8,128)(2,1)}, u32[]{:S(2)}) copy-start(bf16[16,9,108,108]{3,2,0,1:T(8,128)(2,1)} %fusion) | copy-start | bytes 10077700
  119.7 5.6 %copy-start.2 = (bf16[112,108,108]{2,1,0:T(8,128)(2,1)S(1)}, bf16[112,108,108]{2,1,0:T(8,128)(2,1)}, u32[]{:S(2)}) copy-start(bf16[112,108,108]{2,1,0:T(8,128)(2,1)} %gather_fusion.2) | copy-start | bytes 7838212
  132.4 4.8 %copy-start.1 = (bf16[16,9,108,108]{3,2,0,1:T(8,128)(2,1)S(1)}, bf16[16,9,108,108]{3,2,0,1:T(8,128)(2,1)}, u32[]{:S(2)}) copy-start(bf16[16,9,108,108]{3,2,0,1:T(8,128)(2,1)} %fusion) | copy-start | bytes 10077700
  132.4 5.6 %copy-start.4 = (bf16[112,108,108]{2,1,0:T(8,128)(2,1)S(1)}, bf16[112,108,108]{2,1,0:T(8,128)(2,1)}, u32[]{:S(2)}) copy-start(bf16[112,108,108]{2,1,0:T(8,128)(2,1)} %gather_fusion.4) | copy-start | bytes 7838212
Sparse Core Ops, SparseCore 0:
  11.4 81.7 all-gather.2

commit v6 on v4

--- a/solution.py
+++ b/solution.py
@@ -115,16 +115,20 @@
         == lax.broadcasted_iota(jnp.int32, gathered.shape, 3),
     ).astype(jnp.float32)
     resid_blocks = (block_eye - step_size * gathered.astype(jnp.float32)).astype(jnp.bfloat16)
+    doubled_right = jnp.concatenate([resid_blocks, resid_blocks], axis=0)
     direct_right = jnp.stack(
-        [jnp.roll(resid_blocks[:, offset], offset, axis=0) for offset in range(kept)], 0
+        [doubled_right[shard_count - offset : 2 * shard_count - offset, offset] for offset in range(kept)], 0
     )
     mirror_right = resid_blocks[:, 1 : mirrored + 1].transpose(1, 0, 2, 3)
 
     def times_resid0(left_rows):
         left = left_rows.reshape(row_total, shard_count, row_total).transpose(1, 0, 2)
-        direct_left = jnp.stack([jnp.roll(left, offset, axis=0) for offset in range(kept)], 0)
+        doubled = jnp.concatenate([left, left], axis=0)
+        direct_left = jnp.stack(
+            [doubled[shard_count - offset : 2 * shard_count - offset] for offset in range(kept)], 0
+        )
         mirror_left = jnp.stack(
-            [jnp.roll(left, -offset, axis=0) for offset in range(1, mirrored + 1)], 0
+            [doubled[offset : shard_count + offset] for offset in range(1, mirrored + 1)], 0
         )
         product = jnp.einsum(
             "kjab,kjbc->jac", direct_left, direct_right, preferred_element_type=jnp.float32

time: 136 us -> 130 us (0.956)
  waiting for transfers between devices: 61.4 us -> 55 us
  starting transfers between devices: 13.5 us -> 15.3 us
  local copies, waits for them, and re-layouts: 16.3 us -> 14.8 us
    ppermute x4, waiting for transfers between devices: 31 us -> 25.3 us  [halving_sum(): other = lax.ppermute(value, axis, [(i, i ^ stride) for i in range(count)])]
    ppermute x4, starting transfers between devices: 3.74 us -> 5.8 us  [halving_sum(): other = lax.ppermute(value, axis, [(i, i ^ stride) for i in range(count)])]
    slice x45 -> x0, local copies, waits for them, and re-layouts: 1.87 us -> none  [the longest x16 0.72 us: times_resid0(): jnp.roll(left, offset, axis=0)]
    unnamed x28 -> x26, local copies, waits for them, and re-layouts: 6.25 us -> 5.48 us
    unnamed x34 -> x33, other arithmetic: 4.16 us -> 4.06 us
  transfers between devices with their start and end apart: 10 -> 10, of which waited for: 9 -> 9; matrix products, arithmetic and copies ran while one was open for 9% -> 10% of each run, Pallas kernels for 0% -> 0%
where the time goes in v6:
time: 130 us; the launch traced here: 129 us
  waiting for transfers between devices  55 us (42%)
  between operations  16.1 us (12%)
  starting transfers between devices  15.3 us (12%)
  other arithmetic  14.9 us (11%)
  local copies, waits for them, and re-layouts  14.8 us (11%)
  matrix products  13.3 us (10%)
    ppermute x4, waiting for transfers between devices, halving_sum(): lax.ppermute(send, axis, [(i, i ^ stride) for i in range(count)])  28.2 us
    ppermute x4, waiting for transfers between devices, halving_sum(): other = lax.ppermute(value, axis, [(i, i ^ stride) for i in range(count)])  25.3 us
    ppermute x4, starting transfers between devices, halving_sum(): lax.ppermute(send, axis, [(i, i ^ stride) for i in range(count)])  7.94 us
    ppermute x4, starting transfers between devices, halving_sum(): other = lax.ppermute(value, axis, [(i, i ^ stride) for i in range(count)])  5.8 us
    unnamed x26, local copies, waits for them, and re-layouts  5.48 us
    unnamed x33, other arithmetic  4.06 us
    reduce_sum x1, other arithmetic, compressed_products(): column_sums = jnp.sum(magnitudes, axis=2)  4.01 us
    transpose x1, matrix products, conv_back_weight(): summed.transpose(2, 3, 4, 0, 1)  3.67 us
  transfers between devices with their start and end apart: 10, of which 9 were waited for; matrix products, arithmetic and copies ran while one was open for 10% of the time, Pallas kernels for 0%

profile of v6, /device:TPU:0, one launch (start us, length us, event | category | flops | bytes accessed | tf_op | source)
XLA Modules:
  0.0 129.4 jit_solution(17997982518046345385)
XLA Ops:
  7.2 1.9 %reshape_squeeze.8 = bf16[108,16,108]{2,1,0:T(8,128)(2,1)S(1)} reshape(bf16[1,108,1728]{2,1,0:T(8,128)(2,1)} %param.10) | data formatting | bytes 746496 | tf_op jit(solution)/shard_map/reshape;squeeze | solution.py:197
  9.2 0.4 fusion.141
  9.6 0.8 copy.113
  10.4 1.5 %reshape_squeeze.7 = bf16[64,3,3,3,64]{4,3,2,1,0:T(4,128)(2,1)S(1)} reshape(bf16[1,64,1728]{2,1,0:T(8,128)(2,1)} %param.9) | data formatting | bytes 442368 | tf_op jit(solution)/shard_map/reshape;squeeze | solution.py:171
  11.9 1.0 copy.103
  12.9 1.0 copy.102
  14.3 0.7 fusion.21
  15.3 1.5 %collective-permute-start = (bf16[64,2,2,128]{0,2,3,1:T(2,128)(2,1)S(1)}, bf16[64,2,2,128]{0,2,3,1:T(2,128)(2,1)S(1)}, u32[]{:S(2)}, u32[]{:S(2)}) collective-permute-start(bf16[64,2,2,128]{0,2,3,1:T(2,128)(2,1)S(1)} %slice_bitcast_fusion.13), channel_id=1, source_target_pairs={{16,0},{17,1},{18,2},{19,3},{20,4},{21,5},{22,6},{23,7},{24,8},{25... | collective-permute-start | bytes 196616 | tf_op jit(solution)/shard_map/ppermute | solution.py:13
  17.0 1.5 %collective-permute-done = bf16[64,2,2,128]{0,2,3,1:T(2,128)(2,1)S(1)} collective-permute-done((bf16[64,2,2,128]{0,2,3,1:T(2,128)(2,1)S(1)}, bf16[64,2,2,128]{0,2,3,1:T(2,128)(2,1)S(1)}, u32[]{:S(2)}, u32[]{:S(2)}) %collective-permute-start) | collective-permute-done | bytes 65568 | tf_op jit(solution)/shard_map/ppermute | solution.py:13
  18.5 0.3 fusion.167
  18.8 3.7 %fusion.152 = f32[3,3,3,64,64]{4,3,2,1,0:T(8,128)S(1)} fusion(bf16[64,1,2,2,128]{0,1,4,3,2:T(2,128)(2,1)S(1)} %copy.149, bf16[64,1,2,2,128]{0,3,4,2,1:T(2,128)(2,1)S(1)} %get-tuple-element.13), kind=kOutput, calls=%fused_computation.242 | convolution fusion | flops 50069504 | bytes 573440 | tf_op jit(solution)/shard_map/transpose | solution.py:185
  22.6 3.0 %collective-permute-start.1 = (f32[864,64]{1,0:T(8,128)S(1)}, f32[864,64]{1,0:T(8,128)S(1)}, u32[]{:S(2)}, u32[]{:S(2)}) collective-permute-start(f32[864,64]{1,0:T(8,128)S(1)} %slice_select_fusion), channel_id=1, source_target_pairs={{0,1},{1,0},{2,3},{3,2},{4,5},{5,4},{6,7},{7,6},{8,9},{9,8},{10,11... | collective-permute-start | bytes 663560 | tf_op jit(solution)/shard_map/ppermute | solution.py:91
  25.7 0.6 reduce_max.19
  27.0 9.7 %collective-permute-done.1 = f32[864,64]{1,0:T(8,128)S(1)} collective-permute-done((f32[864,64]{1,0:T(8,128)S(1)}, f32[864,64]{1,0:T(8,128)S(1)}, u32[]{:S(2)}, u32[]{:S(2)}) %collective-permute-start.1) | collective-permute-done | bytes 221216 | tf_op jit(solution)/shard_map/ppermute | solution.py:91
  36.8 1.5 %collective-permute-start.2 = (f32[432,64]{1,0:T(8,128)S(1)}, f32[432,64]{1,0:T(8,128)S(1)}, u32[]{:S(2)}, u32[]{:S(2)}) collective-permute-start(f32[432,64]{1,0:T(8,128)S(1)} %slice_select_fusion.1), channel_id=1, source_target_pairs={{0,2},{1,3},{2,0},{3,1},{4,6},{5,7},{6,4},{7,5},{8,10},{9,11},{10,... | collective-permute-start | bytes 331784 | tf_op jit(solution)/shard_map/ppermute | solution.py:91
  38.5 8.4 %collective-permute-done.2 = f32[432,64]{1,0:T(8,128)S(1)} collective-permute-done((f32[432,64]{1,0:T(8,128)S(1)}, f32[432,64]{1,0:T(8,128)S(1)}, u32[]{:S(2)}, u32[]{:S(2)}) %collective-permute-start.2) | collective-permute-done | bytes 110624 | tf_op jit(solution)/shard_map/ppermute | solution.py:91
  46.9 1.2 collective-permute-start.3
  48.2 5.7 %collective-permute-done.3 = f32[216,64]{1,0:T(8,128)S(1)} collective-permute-done((f32[216,64]{1,0:T(8,128)S(1)}, f32[216,64]{1,0:T(8,128)S(1)}, u32[]{:S(2)}, u32[]{:S(2)}) %collective-permute-start.3) | collective-permute-done | bytes 55328 | tf_op jit(solution)/shard_map/ppermute | solution.py:91
  53.9 2.2 %collective-permute-start.4 = (f32[108,64]{1,0:T(8,128)S(1)}, f32[108,64]{1,0:T(8,128)S(1)}, u32[]{:S(2)}, u32[]{:S(2)}) collective-permute-start(f32[108,64]{1,0:T(8,128)S(1)} %slice_select_fusion.3), channel_id=1, source_target_pairs={{0,8},{1,9},{2,10},{3,11},{4,12},{5,13},{6,14},{7,15},{8,0},{9,1},... | collective-permute-start | bytes 82952 | tf_op jit(solution)/shard_map/ppermute | solution.py:91
  56.1 4.4 %collective-permute-done.4 = f32[108,64]{1,0:T(8,128)S(1)} collective-permute-done((f32[108,64]{1,0:T(8,128)S(1)}, f32[108,64]{1,0:T(8,128)S(1)}, u32[]{:S(2)}, u32[]{:S(2)}) %collective-permute-start.4) | collective-permute-done | bytes 27680 | tf_op jit(solution)/shard_map/ppermute | solution.py:91
  60.6 1.1 collective-permute-start.5
  61.7 5.7 %collective-permute-done.5 = f32[108,64]{1,0:T(8,128)S(1)} collective-permute-done((f32[108,64]{1,0:T(8,128)S(1)}, f32[108,64]{1,0:T(8,128)S(1)}, u32[]{:S(2)}, u32[]{:S(2)}) %collective-permute-start.5) | collective-permute-done | bytes 27680 | tf_op jit(solution)/shard_map/ppermute | solution.py:95
  67.4 0.7 collective-permute-start.6
  68.3 10.0 %collective-permute-done.6 = f32[216,64]{1,0:T(8,128)S(1)} collective-permute-done((f32[216,64]{1,0:T(8,128)S(1)}, f32[216,64]{1,0:T(8,128)S(1)}, u32[]{:S(2)}, u32[]{:S(2)}) %collective-permute-start.6) | collective-permute-done | bytes 55328 | tf_op jit(solution)/shard_map/ppermute | solution.py:95
  78.3 3.0 %collective-permute-start.7 = (f32[432,64]{1,0:T(8,128)S(1)}, f32[432,64]{1,0:T(8,128)S(1)}, u32[]{:S(2)}, u32[]{:S(2)}) collective-permute-start(f32[432,64]{1,0:T(8,128)S(1)} %maximum_select_fusion.2), channel_id=1, source_target_pairs={{0,2},{1,3},{2,0},{3,1},{4,6},{5,7},{6,4},{7,5},{8,10},{9,11},{10,... | collective-permute-start | bytes 331784 | tf_op jit(solution)/shard_map/ppermute | solution.py:95
  81.3 0.7 fusion.23
  82.2 3.1 %collective-permute-done.7 = f32[432,64]{1,0:T(8,128)S(1)} collective-permute-done((f32[432,64]{1,0:T(8,128)S(1)}, f32[432,64]{1,0:T(8,128)S(1)}, u32[]{:S(2)}, u32[]{:S(2)}) %collective-permute-start.7) | collective-permute-done | bytes 110624 | tf_op jit(solution)/shard_map/ppermute | solution.py:95
  85.3 1.0 collective-permute-start.8
  86.4 0.7 copy.153
  87.1 6.5 %collective-permute-done.8 = f32[864,64]{1,0:T(8,128)S(1)} collective-permute-done((f32[864,64]{1,0:T(8,128)S(1)}, f32[864,64]{1,0:T(8,128)S(1)}, u32[]{:S(2)}, u32[]{:S(2)}) %collective-permute-start.8) | collective-permute-done | bytes 221216 | tf_op jit(solution)/shard_map/ppermute | solution.py:95
  93.7 1.2 fusion.26
  94.9 4.0 %fusion.1 = (f32[144,108]{1,0:T(8,128)S(1)}, f32[144,108]{1,0:T(8,128)S(1)}) fusion(bf16[144,108,108]{2,1,0:T(8,128)(2,1)} %all-gather.3.cloned.1.call-done), kind=kLoop, calls=%fused_computation.3 | loop fusion | flops 6687360 | bytes 3483648 | tf_op jit(solution)/shard_map/reduce_sum | solution.py:108
  99.3 0.6 fusion.189
  102.0 1.0 copy-done
  103.0 0.5 convert_multiply_fusion
  103.5 1.1 fusion.2
  106.5 1.3 %convolution_bitcast_fusion = f32[16,108,108]{2,1,0:T(8,128)S(1)} fusion(bf16[9,16,108,108]{3,2,0,1:T(8,128)(2,1)S(1)} %get-tuple-element.17, bf16[9,16,108,108]{3,2,0,1:T(8,128)(2,1)S(1)} %get-tuple-element.18), kind=kOutput, calls=%fused_computation.72 | convolution fusion | flops 362797056 | bytes 7464960 | tf_op jit(solution)/shard_map/kjab,kjbc->jac/dot_general | solution.py:133
  107.8 1.1 bitcast_dynamic-update-slice_fusion.1
  110.8 1.1 fusion.9
  111.9 1.3 %fusion.16 = f32[108,16,108]{2,0,1:T(8,128)S(1)} fusion(f32[16,108,108]{2,1,0:T(8,128)S(1)} %fusion.9, bf16[9,16,108,108]{3,2,1,0:T(8,128)(2,1)S(1)} %get-tuple-element.11, bf16[9,16,108,108]{3,2,0,1:T(8,128)(2,1)S(1)} %get-tuple-element.18), kind=kOutput, calls=%fused_computation.74 | convolution fusion | flops 362983680 | bytes 8211456 | tf_op jit(solution)/shard_map/kjab,kjbc->jac/dot_general | solution.py:133
  113.3 0.3 copy.148
  113.6 0.4 reshape.184
  114.0 1.3 %reshape.186 = f32[1,108,1728]{2,1,0:T(8,128)} reshape(f32[108,16,108]{2,1,0:T(8,128)S(1)} %copy.148) | data formatting | bytes 1492992 | tf_op jit(solution)/shard_map/reshape | solution.py:138
  115.6 0.4 reshape.201
  116.0 1.3 %reshape.202 = f32[1,108,1728]{2,1,0:T(8,128)} reshape(f32[108,16,108]{2,1,0:T(8,128)S(1)} %copy.146) | data formatting | bytes 1492992 | tf_op jit(solution)/shard_map/convert_element_type | solution.py:242
  117.4 1.7 %fusion.41 = f32[1,108,1728]{2,1,0:T(8,128)S(1)} fusion(f32[1,108,1728]{2,1,0:T(8,128)} %reshape.186, f32[1,108,1728]{2,1,0:T(8,128)} %reshape.202, bf16[1,108,1728]{2,1,0:T(8,128)(2,1)S(1)} %copy-done.1, s32[108]{0:T(128)S(1)} %iota_add_fusion, f32[]{:T(128)S(6)} %div.39), kind=kLoop, calls=%fused_computation.109 | loop fusion | flops 2052864 | bytes 2613172 | tf_op jit(solution)/shard_map/mul | solution.py:241
  119.0 1.7 %copy.154 = f32[1,108,1728]{2,0,1:T(1,128)} copy(f32[1,108,1728]{2,1,0:T(8,128)S(1)} %fusion.41) | data formatting | bytes 1492992
  120.7 1.9 %convolution_bitcast_fusion.1 = f32[1,108,64]{1,2,0:T(8,128)} fusion(f32[1728,64]{0,1:T(8,128)S(1)} %fusion.26, f32[108,1728]{1,0:T(8,128)S(1)} %reshape.184, f32[108,1728]{1,0:T(8,128)S(1)} %reshape.201, bf16[1,108,1728]{2,1,0:T(8,128)(2,1)S(1)} %copy-done.1, f32[]{:T(128)S(6)} %div.39, s32[108]{0:T(128)S(1)} %iota_add_fusion), kind=kOutput, calls=%fused_computation.82 | convolution fusion | flops 145380096 | bytes 2336692 | tf_op jit(solution)/shard_map/dot_general | solution.py:248
  (110 shorter events, 7.4 us)
Async XLA Ops:
  7.2 7.2 %copy-start.4 = (pred[8,17]{0,1:T(8,128)(4,1)S(1)}, pred[8,17]{0,1:T(8,128)(4,1)}, u32[]{:S(2)}) copy-start(pred[8,17]{0,1:T(8,128)(4,1)} %constant.134) | copy-start | bytes 412
  7.2 9.6 %copy-start.2 = (bf16[1,1,1,64,2,2,128]{6,5,4,3,2,1,0:T(2,128)(2,1)S(1)}, bf16[1,1,1,64,2,2,128]{6,5,4,3,2,1,0:T(2,128)(2,1)}, u32[]{:S(2)}) copy-start(bf16[1,1,1,64,2,2,128]{6,5,4,3,2,1,0:T(2,128)(2,1)} %param.6) | copy-start | bytes 196612
  7.2 87.7 %all-gather.3.cloned.1.call-start = ((), (), s32[]{:S(2)}) async-start(), calls=%async_computation | async-start | bytes 4386816 | tf_op jit(solution)/shard_map/all_gather | solution.py:200
  15.3 3.2 %collective-permute-start = (bf16[64,2,2,128]{0,2,3,1:T(2,128)(2,1)S(1)}, bf16[64,2,2,128]{0,2,3,1:T(2,128)(2,1)S(1)}, u32[]{:S(2)}, u32[]{:S(2)}) collective-permute-start(bf16[64,2,2,128]{0,2,3,1:T(2,128)(2,1)S(1)} %slice_bitcast_fusion.13), channel_id=1, source_target_pairs={{16,0},{17,1},{18,2},{19,3},{20,4},{21,5},{22,6},{23,7},{24,8},{25... | collective-permute-start | bytes 196616 | tf_op jit(solution)/shard_map/ppermute | solution.py:13
  18.8 6.8 %copy-start.3 = (bf16[1,64,64]{2,1,0:T(8,128)(2,1)S(1)}, bf16[1,64,64]{2,1,0:T(8,128)(2,1)}, u32[]{:S(2)}) copy-start(bf16[1,64,64]{2,1,0:T(8,128)(2,1)} %param.11) | copy-start | bytes 24580
  22.6 14.2 %collective-permute-start.1 = (f32[864,64]{1,0:T(8,128)S(1)}, f32[864,64]{1,0:T(8,128)S(1)}, u32[]{:S(2)}, u32[]{:S(2)}) collective-permute-start(f32[864,64]{1,0:T(8,128)S(1)} %slice_select_fusion), channel_id=1, source_target_pairs={{0,1},{1,0},{2,3},{3,2},{4,5},{5,4},{6,7},{7,6},{8,9},{9,8},{10,11... | collective-permute-start | bytes 663560 | tf_op jit(solution)/shard_map/ppermute | solution.py:91
  36.8 10.0 %collective-permute-start.2 = (f32[432,64]{1,0:T(8,128)S(1)}, f32[432,64]{1,0:T(8,128)S(1)}, u32[]{:S(2)}, u32[]{:S(2)}) collective-permute-start(f32[432,64]{1,0:T(8,128)S(1)} %slice_select_fusion.1), channel_id=1, source_target_pairs={{0,2},{1,3},{2,0},{3,1},{4,6},{5,7},{6,4},{7,5},{8,10},{9,11},{10,... | collective-permute-start | bytes 331784 | tf_op jit(solution)/shard_map/ppermute | solution.py:91
  46.9 7.0 %collective-permute-start.3 = (f32[216,64]{1,0:T(8,128)S(1)}, f32[216,64]{1,0:T(8,128)S(1)}, u32[]{:S(2)}, u32[]{:S(2)}) collective-permute-start(f32[216,64]{1,0:T(8,128)S(1)} %slice_select_fusion.2), channel_id=1, source_target_pairs={{0,4},{1,5},{2,6},{3,7},{4,0},{5,1},{6,2},{7,3},{8,12},{9,13},{10,... | collective-permute-start | bytes 165896 | tf_op jit(solution)/shard_map/ppermute | solution.py:91
  53.9 6.6 %collective-permute-start.4 = (f32[108,64]{1,0:T(8,128)S(1)}, f32[108,64]{1,0:T(8,128)S(1)}, u32[]{:S(2)}, u32[]{:S(2)}) collective-permute-start(f32[108,64]{1,0:T(8,128)S(1)} %slice_select_fusion.3), channel_id=1, source_target_pairs={{0,8},{1,9},{2,10},{3,11},{4,12},{5,13},{6,14},{7,15},{8,0},{9,1},... | collective-permute-start | bytes 82952 | tf_op jit(solution)/shard_map/ppermute | solution.py:91
  60.6 6.8 %collective-permute-start.5 = (f32[108,64]{1,0:T(8,128)S(1)}, f32[108,64]{1,0:T(8,128)S(1)}, u32[]{:S(2)}, u32[]{:S(2)}) collective-permute-start(f32[108,64]{1,0:T(8,128)S(1)} %select_add_fusion.3), channel_id=1, source_target_pairs={{0,8},{1,9},{2,10},{3,11},{4,12},{5,13},{6,14},{7,15},{8,0},{9,1},... | collective-permute-start | bytes 82952 | tf_op jit(solution)/shard_map/ppermute | solution.py:95
  67.4 10.8 %collective-permute-start.6 = (f32[216,64]{1,0:T(8,128)S(1)}, f32[216,64]{1,0:T(8,128)S(1)}, u32[]{:S(2)}, u32[]{:S(2)}) collective-permute-start(f32[216,64]{1,0:T(8,128)S(1)} %maximum_select_fusion.3), channel_id=1, source_target_pairs={{0,4},{1,5},{2,6},{3,7},{4,0},{5,1},{6,2},{7,3},{8,12},{9,13},{10,... | collective-permute-start | bytes 165896 | tf_op jit(solution)/shard_map/ppermute | solution.py:95
  78.3 6.9 %collective-permute-start.7 = (f32[432,64]{1,0:T(8,128)S(1)}, f32[432,64]{1,0:T(8,128)S(1)}, u32[]{:S(2)}, u32[]{:S(2)}) collective-permute-start(f32[432,64]{1,0:T(8,128)S(1)} %maximum_select_fusion.2), channel_id=1, source_target_pairs={{0,2},{1,3},{2,0},{3,1},{4,6},{5,7},{6,4},{7,5},{8,10},{9,11},{10,... | collective-permute-start | bytes 331784 | tf_op jit(solution)/shard_map/ppermute | solution.py:95
  85.3 8.4 %collective-permute-start.8 = (f32[864,64]{1,0:T(8,128)S(1)}, f32[864,64]{1,0:T(8,128)S(1)}, u32[]{:S(2)}, u32[]{:S(2)}) collective-permute-start(f32[864,64]{1,0:T(8,128)S(1)} %maximum_select_fusion.1), channel_id=1, source_target_pairs={{0,1},{1,0},{2,3},{3,2},{4,5},{5,4},{6,7},{7,6},{8,9},{9,8},{10,11... | collective-permute-start | bytes 663560 | tf_op jit(solution)/shard_map/ppermute | solution.py:95
  100.8 2.2 %copy-start = (bf16[144,108,108]{2,1,0:T(8,128)(2,1)S(1)}, bf16[144,108,108]{2,1,0:T(8,128)(2,1)}, u32[]{:S(2)}) copy-start(bf16[144,108,108]{2,1,0:T(8,128)(2,1)} %all-gather.3.cloned.1.call-done) | copy-start | bytes 10077700
  113.6 3.8 %copy-start.1 = (bf16[1,108,1728]{2,1,0:T(8,128)(2,1)S(1)}, bf16[1,108,1728]{2,1,0:T(8,128)(2,1)}, u32[]{:S(2)}) copy-start(bf16[1,108,1728]{2,1,0:T(8,128)(2,1)} %param.10) | copy-start | bytes 1119748
Sparse Core Ops, SparseCore 0:
  11.4 81.3 all-gather.2

commit v7 on v6

--- a/solution.py
+++ b/solution.py
@@ -78,7 +78,7 @@
     return (column_ids == start_row + row_ids).astype(jnp.float32)
 
 
-def halving_sum(value, axis):
+def halving_sum(value, axis, extra=None):
     count = lax.axis_size(axis)
     assert count & (count - 1) == 0 and value.shape[0] % count == 0
     index = lax.axis_index(axis)
@@ -90,25 +90,25 @@
         send = jnp.where(upper, value[:half], value[half:])
         value = keep + lax.ppermute(send, axis, [(i, i ^ stride) for i in range(count)])
         stride *= 2
+    if extra is not None:
+        value = jnp.concatenate([value, extra], axis=0)
     stride = count // 2
     while stride >= 1:
         other = lax.ppermute(value, axis, [(i, i ^ stride) for i in range(count)])
         upper = (index // stride) % 2 == 1
         value = jnp.where(upper, jnp.concatenate([other, value]), jnp.concatenate([value, other]))
         stride //= 2
-    return value
-
-
-def compressed_products(gathered, a_rows, own_eye, shard_count, row_total):
+    if extra is None:
+        return value
+    pieces = value.reshape(count, -1, value.shape[1])
+    held = pieces.shape[1] - extra.shape[0]
+    return pieces[:, :held].reshape(-1, value.shape[1]), pieces[:, held:]
+
+
+def compressed_products(gathered, a_rows, own_eye, shard_count, row_total, step_size):
     kept = shard_count // 2 + 1
     order_full = a_rows.shape[1]
     mirrored = shard_count - kept
-    magnitudes = jnp.abs(gathered.astype(jnp.float32))
-    direct_sums = jnp.sum(jnp.sum(magnitudes, axis=3), axis=1)
-    column_sums = jnp.sum(magnitudes, axis=2)
-    for offset in range(1, mirrored + 1):
-        direct_sums = direct_sums + jnp.roll(column_sums[:, offset], offset, axis=0)
-    step_size = 1.0 / jnp.max(direct_sums)
     block_eye = jnp.logical_and(
         lax.broadcasted_iota(jnp.int32, gathered.shape, 1) == 0,
         lax.broadcasted_iota(jnp.int32, gathered.shape, 2)
@@ -140,7 +140,7 @@
     resid0 = (own_eye - step_size * a_rows.astype(jnp.float32)).astype(jnp.bfloat16)
     resid1 = times_resid0(resid0).astype(jnp.bfloat16)
     cross_term = times_resid0(resid1)
-    return step_size, resid0, resid1, cross_term
+    return resid0, resid1, cross_term
 
 
 def dense_products(gathered, a_rows, own_eye):
@@ -226,15 +226,21 @@
     for micro in range(1, micro_count):
         local_grad = local_grad + conv_back_weight(inputs[micro], stored_slopes[micro])
     stored_grads = jnp.stack(stored_grads, 0)
-    summed_grad = halving_sum(local_grad, "dp")
+    if compressed:
+        local_largest = jnp.max(jnp.sum(jnp.abs(a_factor[0].astype(jnp.float32)), axis=1))
+        carried = jnp.zeros((1, local_grad.shape[1]), jnp.float32).at[0, 0].set(local_largest)
+        summed_grad, carried = halving_sum(local_grad, "dp", carried)
+        step_size = 1.0 / jnp.max(carried[:, 0, 0])
+    else:
+        summed_grad = halving_sum(local_grad, "dp")
     mean_grad = summed_grad / lax.axis_size("dp")
     a_rows = a_factor[0]
     order_full = a_rows.shape[1]
     first_row = lax.axis_index("dp") * row_total
     own_eye = eye_rows(first_row, row_total, order_full)
     if compressed:
-        step_size, resid0, resid1, cross_term = compressed_products(
-            gathered, a_rows, own_eye, shard_count, row_total
+        resid0, resid1, cross_term = compressed_products(
+            gathered, a_rows, own_eye, shard_count, row_total, step_size
         )
     else:
         step_size, resid0, resid1, cross_term = dense_products(gathered, a_rows, own_eye)

time: 130 us -> 133 us (1.023)
  waiting for transfers between devices: 55 us -> 44.7 us
  local copies, waits for them, and re-layouts: 14.8 us -> 20.4 us
  starting transfers between devices: 15.3 us -> 19 us
  matrix products: 13.3 us -> 15.5 us
    ppermute x4, waiting for transfers between devices: 28.2 us -> 14 us  [halving_sum(): lax.ppermute(send, axis, [(i, i ^ stride) for i in range(count)])]
    all_gather x1, waiting for transfers between devices: 0.02 us -> 11 us  [shards(): gathered = lax.all_gather(upper_blocks, 'dp', axis=0)]
    ppermute x4, waiting for transfers between devices: 25.3 us -> 19.6 us  [halving_sum(): other = lax.ppermute(value, axis, [(i, i ^ stride) for i in range(count)])]
    unnamed x26 -> x23, local copies, waits for them, and re-layouts: 5.48 us -> 10.4 us
    reduce_sum x2 -> x1, other arithmetic: 4.04 us -> 0.17 us  [shards(): jnp.sum(jnp.abs(a_factor[0].astype(jnp.float32)), axis=1)]
    mul x1, other arithmetic: 0.53 us -> 2.7 us  [compressed_products(): step_size * gathered.astype(jnp.float32)]
    ppermute x4, starting transfers between devices: 5.8 us -> 7.76 us  [halving_sum(): other = lax.ppermute(value, axis, [(i, i ^ stride) for i in range(count)])]
    ppermute x4, starting transfers between devices: 7.94 us -> 9.9 us  [halving_sum(): lax.ppermute(send, axis, [(i, i ^ stride) for i in range(count)])]
  transfers between devices with their start and end apart: 10 -> 10, of which waited for: 9 -> 8; matrix products, arithmetic and copies ran while one was open for 10% -> 14% of each run, Pallas kernels for 0% -> 0%
where the time goes in v7:
time: 133 us; the launch traced here: 132 us
  waiting for transfers between devices  44.7 us (34%)
  local copies, waits for them, and re-layouts  20.4 us (15%)
  starting transfers between devices  19 us (14%)
  between operations  17.3 us (13%)
  matrix products  15.5 us (12%)
  other arithmetic  15.2 us (11%)
    ppermute x4, waiting for transfers between devices, halving_sum(): other = lax.ppermute(value, axis, [(i, i ^ stride) for i in range(count)])  19.6 us
    ppermute x4, waiting for transfers between devices, halving_sum(): lax.ppermute(send, axis, [(i, i ^ stride) for i in range(count)])  14 us
    all_gather x1, waiting for transfers between devices, shards(): gathered = lax.all_gather(upper_blocks, 'dp', axis=0)  11 us
    unnamed x23, local copies, waits for them, and re-layouts  10.4 us
    ppermute x4, starting transfers between devices, halving_sum(): lax.ppermute(send, axis, [(i, i ^ stride) for i in range(count)])  9.9 us
    ppermute x4, starting transfers between devices, halving_sum(): other = lax.ppermute(value, axis, [(i, i ^ stride) for i in range(count)])  7.76 us
    unnamed x33, other arithmetic  4.04 us
    transpose x1, matrix products, conv_back_weight(): summed.transpose(2, 3, 4, 0, 1)  3.75 us
  transfers between devices with their start and end apart: 10, of which 8 were waited for; matrix products, arithmetic and copies ran while one was open for 14% of the time, Pallas kernels for 0%

profile of v7, /device:TPU:0, one launch (start us, length us, event | category | flops | bytes accessed | tf_op | source)
XLA Modules:
  0.0 132.1 jit_solution(4884251273625868989)
XLA Ops:
  7.2 1.5 %reshape_squeeze.2 = bf16[64,3,3,3,64]{4,3,2,1,0:T(4,128)(2,1)S(1)} reshape(bf16[1,64,1728]{2,1,0:T(8,128)(2,1)} %param.11) | data formatting | bytes 442368 | tf_op jit(solution)/shard_map/reshape;squeeze | solution.py:171
  8.8 1.0 copy.81
  9.8 1.0 copy.80
  11.2 1.4 %fusion.19 = bf16[2,2,8,17,64]{4,2,3,1,0:T(8,128)(2,1)S(1)} fusion(bf16[64,3,3,3,64]{4,3,2,1,0:T(4,128)(2,1)S(1)} %reshape_squeeze.2, bf16[64,2,2,1,7,2]{0,4,5,2,1,3:T(8,128)(2,1)S(1)} %slice.230, bf16[64,2,2,1,8,17]{0,4,5,2,1,3:T(8,128)(2,1)S(1)} %copy.84, pred[8,17]{0,1:T(8,128)(4,1)} %constant.167), kind=kOutput, calls=%fused_computation.76 | convolution fusion | flops 53780480 | bytes 367752 | tf_op jit(solution)/shard_map/conv_general_dilated | solution.py:172
  12.8 1.3 collective-permute-start
  14.1 1.9 %squeeze.18 = bf16[108,16,108]{2,1,0:T(8,128)(2,1)S(1)} reshape(bf16[1,108,1728]{2,1,0:T(8,128)(2,1)} %param.12) | data formatting | bytes 746496 | tf_op jit(solution)/shard_map/squeeze | solution.py:230
  16.5 0.8 copy.104
  17.6 0.6 reduce_max.29
  19.3 3.8 %fusion.142 = f32[3,3,3,64,64]{4,3,2,1,0:T(8,128)S(1)} fusion(bf16[64,1,2,2,128]{0,1,4,3,2:T(2,128)(2,1)S(1)} %copy.91, bf16[64,1,2,2,128]{0,3,4,2,1:T(2,128)(2,1)S(1)} %get-tuple-element.25), kind=kOutput, calls=%fused_computation.231 | convolution fusion | flops 50069504 | bytes 573440 | tf_op jit(solution)/shard_map/transpose | solution.py:185
  23.5 3.0 %collective-permute-start.1 = (f32[864,64]{0,1:T(8,128)S(1)}, f32[864,64]{0,1:T(8,128)S(1)}, u32[]{:S(2)}, u32[]{:S(2)}) collective-permute-start(f32[864,64]{0,1:T(8,128)S(1)} %broadcast_select_fusion.5), channel_id=1, source_target_pairs={{0,1},{1,0},{2,3},{3,2},{4,5},{5,4},{6,7},{7,6},{8,9},{9,8},{10,11... | collective-permute-start | bytes 663560 | tf_op jit(solution)/shard_map/ppermute | solution.py:91
  26.7 7.5 %collective-permute-done.1 = f32[864,64]{0,1:T(8,128)S(1)} collective-permute-done((f32[864,64]{0,1:T(8,128)S(1)}, f32[864,64]{0,1:T(8,128)S(1)}, u32[]{:S(2)}, u32[]{:S(2)}) %collective-permute-start.1) | collective-permute-done | bytes 221216 | tf_op jit(solution)/shard_map/ppermute | solution.py:91
  34.4 2.0 %collective-permute-start.2 = (f32[432,64]{0,1:T(8,128)S(1)}, f32[432,64]{0,1:T(8,128)S(1)}, u32[]{:S(2)}, u32[]{:S(2)}) collective-permute-start(f32[432,64]{0,1:T(8,128)S(1)} %slice_select_fusion), channel_id=1, source_target_pairs={{0,2},{1,3},{2,0},{3,1},{4,6},{5,7},{6,4},{7,5},{8,10},{9,11},{10,... | collective-permute-start | bytes 331784 | tf_op jit(solution)/shard_map/ppermute | solution.py:91
  36.5 4.2 %collective-permute-done.2 = f32[432,64]{0,1:T(8,128)S(1)} collective-permute-done((f32[432,64]{0,1:T(8,128)S(1)}, f32[432,64]{0,1:T(8,128)S(1)}, u32[]{:S(2)}, u32[]{:S(2)}) %collective-permute-start.2) | collective-permute-done | bytes 110624 | tf_op jit(solution)/shard_map/ppermute | solution.py:91
  41.0 1.9 %collective-permute-start.3 = (f32[216,64]{0,1:T(8,128)S(1)}, f32[216,64]{0,1:T(8,128)S(1)}, u32[]{:S(2)}, u32[]{:S(2)}) collective-permute-start(f32[216,64]{0,1:T(8,128)S(1)} %slice_select_fusion.1), channel_id=1, source_target_pairs={{0,4},{1,5},{2,6},{3,7},{4,0},{5,1},{6,2},{7,3},{8,12},{9,13},{10,... | collective-permute-start | bytes 165896 | tf_op jit(solution)/shard_map/ppermute | solution.py:91
  43.1 2.2 %collective-permute-done.3 = f32[216,64]{0,1:T(8,128)S(1)} collective-permute-done((f32[216,64]{0,1:T(8,128)S(1)}, f32[216,64]{0,1:T(8,128)S(1)}, u32[]{:S(2)}, u32[]{:S(2)}) %collective-permute-start.3) | collective-permute-done | bytes 55328 | tf_op jit(solution)/shard_map/ppermute | solution.py:91
  45.5 2.9 %collective-permute-start.4 = (f32[108,64]{0,1:T(8,128)S(1)}, f32[108,64]{0,1:T(8,128)S(1)}, u32[]{:S(2)}, u32[]{:S(2)}) collective-permute-start(f32[108,64]{0,1:T(8,128)S(1)} %slice_select_fusion.2), channel_id=1, source_target_pairs={{0,8},{1,9},{2,10},{3,11},{4,12},{5,13},{6,14},{7,15},{8,0},{9,1},... | collective-permute-start | bytes 82952 | tf_op jit(solution)/shard_map/ppermute | solution.py:91
  48.4 0.6 reduce_max.27
  49.0 0.6 compare_reduce_fusion
  51.1 2.8 %collective-permute-start.5 = (f32[109,64]{0,1:T(8,128)S(1)}, f32[109,64]{0,1:T(8,128)S(1)}, u32[]{:S(2)}, u32[]{:S(2)}) collective-permute-start(f32[109,64]{0,1:T(8,128)S(1)} %pad_maximum_fusion.3), channel_id=1, source_target_pairs={{0,8},{1,9},{2,10},{3,11},{4,12},{5,13},{6,14},{7,15},{8,0},{9,1},... | collective-permute-start | bytes 83720 | tf_op jit(solution)/shard_map/ppermute | solution.py:97
  54.0 3.5 %collective-permute-done.5 = f32[109,64]{0,1:T(8,128)S(1)} collective-permute-done((f32[109,64]{0,1:T(8,128)S(1)}, f32[109,64]{0,1:T(8,128)S(1)}, u32[]{:S(2)}, u32[]{:S(2)}) %collective-permute-start.5) | collective-permute-done | bytes 27936 | tf_op jit(solution)/shard_map/ppermute | solution.py:97
  57.6 1.7 %collective-permute-start.6 = (f32[218,64]{0,1:T(8,128)S(1)}, f32[218,64]{0,1:T(8,128)S(1)}, u32[]{:S(2)}, u32[]{:S(2)}) collective-permute-start(f32[218,64]{0,1:T(8,128)S(1)} %maximum_select_fusion.3), channel_id=1, source_target_pairs={{0,4},{1,5},{2,6},{3,7},{4,0},{5,1},{6,2},{7,3},{8,12},{9,13},{10,... | collective-permute-start | bytes 167432 | tf_op jit(solution)/shard_map/ppermute | solution.py:97
  59.5 5.1 %collective-permute-done.6 = f32[218,64]{0,1:T(8,128)S(1)} collective-permute-done((f32[218,64]{0,1:T(8,128)S(1)}, f32[218,64]{0,1:T(8,128)S(1)}, u32[]{:S(2)}, u32[]{:S(2)}) %collective-permute-start.6) | collective-permute-done | bytes 55840 | tf_op jit(solution)/shard_map/ppermute | solution.py:97
  64.8 1.6 %collective-permute-start.7 = (f32[436,64]{0,1:T(8,128)S(1)}, f32[436,64]{0,1:T(8,128)S(1)}, u32[]{:S(2)}, u32[]{:S(2)}) collective-permute-start(f32[436,64]{0,1:T(8,128)S(1)} %maximum_select_fusion.2), channel_id=1, source_target_pairs={{0,2},{1,3},{2,0},{3,1},{4,6},{5,7},{6,4},{7,5},{8,10},{9,11},{10,... | collective-permute-start | bytes 334856 | tf_op jit(solution)/shard_map/ppermute | solution.py:97
  66.3 0.7 fusion.21
  67.2 2.6 %collective-permute-done.7 = f32[436,64]{0,1:T(8,128)S(1)} collective-permute-done((f32[436,64]{0,1:T(8,128)S(1)}, f32[436,64]{0,1:T(8,128)S(1)}, u32[]{:S(2)}, u32[]{:S(2)}) %collective-permute-start.7) | collective-permute-done | bytes 111648 | tf_op jit(solution)/shard_map/ppermute | solution.py:97
  69.9 1.6 %collective-permute-start.8 = (f32[872,64]{0,1:T(8,128)S(1)}, f32[872,64]{0,1:T(8,128)S(1)}, u32[]{:S(2)}, u32[]{:S(2)}) collective-permute-start(f32[872,64]{0,1:T(8,128)S(1)} %maximum_select_fusion.1), channel_id=1, source_target_pairs={{0,1},{1,0},{2,3},{3,2},{4,5},{5,4},{6,7},{7,6},{8,9},{9,8},{10,11... | collective-permute-start | bytes 669704 | tf_op jit(solution)/shard_map/ppermute | solution.py:97
  71.6 0.7 copy.119
  72.4 8.4 %collective-permute-done.8 = f32[872,64]{0,1:T(8,128)S(1)} collective-permute-done((f32[872,64]{0,1:T(8,128)S(1)}, f32[872,64]{0,1:T(8,128)S(1)}, u32[]{:S(2)}, u32[]{:S(2)}) %collective-permute-start.8) | collective-permute-done | bytes 223264 | tf_op jit(solution)/shard_map/ppermute | solution.py:97
  81.0 0.5 select_n.263
  81.8 0.7 slice_reduce_fusion
  85.5 1.2 copy-done
  86.7 1.8 %copy-done.3 = bf16[7,16,108,108]{3,2,1,0:T(8,128)(2,1)} copy-done((bf16[7,16,108,108]{3,2,1,0:T(8,128)(2,1)}, bf16[7,16,108,108]{3,2,1,0:T(8,128)(2,1)S(1)}, u32[]{:S(2)}) %copy-start.3) | copy-done | bytes 2612760
  88.5 1.3 %fusion.181 = f32[1728,64]{0,1:T(8,128)} fusion(f32[1728,64]{0,1:T(8,128)S(1)} %div.53, f32[64,64]{1,0:T(8,128)S(1)} %fusion.22), kind=kOutput, calls=%fused_computation.297 | convolution fusion | flops 84934656 | bytes 901120 | tf_op jit(solution)/shard_map/dot_general | solution.py:251
  89.8 11.0 %all-gather.3.cloned.1.call-done = bf16[144,108,108]{2,1,0:T(8,128)(2,1)} async-done(((bf16[9,108,108]{2,1,0:T(8,128)(2,1)}), bf16[144,108,108]{2,1,0:T(8,128)(2,1)}) %all-gather.3.cloned.1.call-update) | async-done | bytes 3359248 | tf_op jit(solution)/shard_map/all_gather | solution.py:200
  100.8 2.7 %convert_multiply_fusion = f32[144,108,108]{2,1,0:T(8,128)S(1)} fusion(bf16[144,108,108]{2,1,0:T(8,128)(2,1)} %all-gather.3.cloned.1.call-done, f32[]{:T(128)S(6)} %div.50), kind=kLoop, calls=%fused_computation.2 | loop fusion | flops 3359232 | bytes 10077700 | tf_op jit(solution)/shard_map/mul | solution.py:117
  103.5 0.8 fusion
  105.4 1.9 %copy-done.1 = bf16[9,16,108,108]{3,2,0,1:T(8,128)(2,1)S(1)} copy-done((bf16[9,16,108,108]{3,2,0,1:T(8,128)(2,1)S(1)}, bf16[9,16,108,108]{3,2,0,1:T(8,128)(2,1)}, u32[]{:S(2)}) %copy-start.1) | copy-done | bytes 3359256
  107.3 1.3 convolution_bitcast_fusion
  108.6 0.6 copy-done.4
  109.2 1.2 bitcast_dynamic-update-slice_fusion.1
  112.2 1.4 %fusion.7 = f32[16,108,108]{2,1,0:T(8,128)S(1)} fusion(bf16[7,16,108,108]{3,2,1,0:T(8,128)(2,1)S(1)} %fusion.120, bf16[16,9,108,108]{3,2,0,1:T(8,128)(2,1)S(1)} %fusion), kind=kOutput, calls=%fused_computation.67 | convolution fusion | flops 282175488 | bytes 7169024 | tf_op jit(solution)/shard_map/mjab,mjcb->jac/dot_general | solution.py:135
  113.6 1.3 fusion.14
  115.2 0.4 reshape.215
  115.7 1.3 reshape.216
  117.7 1.3 reshape.232
  119.0 1.7 %fusion.33 = f32[1,108,1728]{2,1,0:T(8,128)S(1)} fusion(f32[1,108,1728]{2,1,0:T(8,128)} %reshape.216, f32[1,108,1728]{2,1,0:T(8,128)} %reshape.232, bf16[1,108,1728]{2,1,0:T(8,128)(2,1)S(1)} %copy-done.2, s32[108]{0:T(128)S(1)} %iota_add_fusion, f32[]{:T(128)S(6)} %div.50), kind=kLoop, calls=%fused_computation.102 | loop fusion | flops 2052864 | bytes 2613172 | tf_op jit(solution)/shard_map/mul | solution.py:247
  120.7 1.7 %copy.120 = f32[1,108,1728]{2,0,1:T(1,128)} copy(f32[1,108,1728]{2,1,0:T(8,128)S(1)} %fusion.33) | data formatting | bytes 1492992
  122.4 2.9 %convolution_bitcast_fusion.1 = f32[1,108,64]{1,2,0:T(8,128)} fusion(f32[1728,64]{0,1:T(8,128)} %fusion.181, f32[108,1728]{1,0:T(8,128)S(1)} %reshape.215, f32[108,1728]{1,0:T(8,128)S(1)} %reshape.231, bf16[1,108,1728]{2,1,0:T(8,128)(2,1)S(1)} %copy-done.2, f32[]{:T(128)S(6)} %div.50, s32[108]{0:T(128)S(1)} %iota_add_fusion), kind=kOutput, calls=%fused_computation.79 | convolution fusion | flops 145380096 | bytes 2336692 | tf_op jit(solution)/shard_map/dot_general | solution.py:254
  (100 shorter events, 10.4 us)
Async XLA Ops:
  7.2 10.1 %copy-start.5 = (bf16[1,1,1,64,2,2,128]{6,5,4,3,2,1,0:T(2,128)(2,1)S(1)}, bf16[1,1,1,64,2,2,128]{6,5,4,3,2,1,0:T(2,128)(2,1)}, u32[]{:S(2)}) copy-start(bf16[1,1,1,64,2,2,128]{6,5,4,3,2,1,0:T(2,128)(2,1)} %param.8) | copy-start | bytes 196612
  7.2 10.4 %copy-start.6 = (bf16[1,64,64]{2,1,0:T(8,128)(2,1)S(1)}, bf16[1,64,64]{2,1,0:T(8,128)(2,1)}, u32[]{:S(2)}) copy-start(bf16[1,64,64]{2,1,0:T(8,128)(2,1)} %param.13) | copy-start | bytes 24580
  7.2 93.6 %all-gather.3.cloned.1.call-start = ((), (), s32[]{:S(2)}) async-start(), calls=%async_computation | async-start | bytes 4386816 | tf_op jit(solution)/shard_map/all_gather | solution.py:200
  12.8 6.1 %collective-permute-start = (bf16[64,2,2,128]{0,2,3,1:T(2,128)(2,1)S(1)}, bf16[64,2,2,128]{0,2,3,1:T(2,128)(2,1)S(1)}, u32[]{:S(2)}, u32[]{:S(2)}) collective-permute-start(bf16[64,2,2,128]{0,2,3,1:T(2,128)(2,1)S(1)} %slice_bitcast_fusion.13), channel_id=1, source_target_pairs={{16,0},{17,1},{18,2},{19,3},{20,4},{21,5},{22,6},{23,7},{24,8},{25... | collective-permute-start | bytes 196616 | tf_op jit(solution)/shard_map/ppermute | solution.py:13
  23.0 19.8 %copy-start.2 = (bf16[1,108,1728]{2,1,0:T(8,128)(2,1)S(1)}, bf16[1,108,1728]{2,1,0:T(8,128)(2,1)}, u32[]{:S(2)}) copy-start(bf16[1,108,1728]{2,1,0:T(8,128)(2,1)} %param.12) | copy-start | bytes 1119748
  23.0 43.3 %copy-start.7 = (pred[8,17]{0,1:T(8,128)(4,1)S(1)}, pred[8,17]{0,1:T(8,128)(4,1)}, u32[]{:S(2)}) copy-start(pred[8,17]{0,1:T(8,128)(4,1)} %constant.167) | copy-start | bytes 412
  23.5 10.7 %collective-permute-start.1 = (f32[864,64]{0,1:T(8,128)S(1)}, f32[864,64]{0,1:T(8,128)S(1)}, u32[]{:S(2)}, u32[]{:S(2)}) collective-permute-start(f32[864,64]{0,1:T(8,128)S(1)} %broadcast_select_fusion.5), channel_id=1, source_target_pairs={{0,1},{1,0},{2,3},{3,2},{4,5},{5,4},{6,7},{7,6},{8,9},{9,8},{10,11... | collective-permute-start | bytes 663560 | tf_op jit(solution)/shard_map/ppermute | solution.py:91
  34.4 6.4 %collective-permute-start.2 = (f32[432,64]{0,1:T(8,128)S(1)}, f32[432,64]{0,1:T(8,128)S(1)}, u32[]{:S(2)}, u32[]{:S(2)}) collective-permute-start(f32[432,64]{0,1:T(8,128)S(1)} %slice_select_fusion), channel_id=1, source_target_pairs={{0,2},{1,3},{2,0},{3,1},{4,6},{5,7},{6,4},{7,5},{8,10},{9,11},{10,... | collective-permute-start | bytes 331784 | tf_op jit(solution)/shard_map/ppermute | solution.py:91
  41.0 4.3 %collective-permute-start.3 = (f32[216,64]{0,1:T(8,128)S(1)}, f32[216,64]{0,1:T(8,128)S(1)}, u32[]{:S(2)}, u32[]{:S(2)}) collective-permute-start(f32[216,64]{0,1:T(8,128)S(1)} %slice_select_fusion.1), channel_id=1, source_target_pairs={{0,4},{1,5},{2,6},{3,7},{4,0},{5,1},{6,2},{7,3},{8,12},{9,13},{10,... | collective-permute-start | bytes 165896 | tf_op jit(solution)/shard_map/ppermute | solution.py:91
  45.5 5.5 %collective-permute-start.4 = (f32[108,64]{0,1:T(8,128)S(1)}, f32[108,64]{0,1:T(8,128)S(1)}, u32[]{:S(2)}, u32[]{:S(2)}) collective-permute-start(f32[108,64]{0,1:T(8,128)S(1)} %slice_select_fusion.2), channel_id=1, source_target_pairs={{0,8},{1,9},{2,10},{3,11},{4,12},{5,13},{6,14},{7,15},{8,0},{9,1},... | collective-permute-start | bytes 82952 | tf_op jit(solution)/shard_map/ppermute | solution.py:91
  51.1 6.4 %collective-permute-start.5 = (f32[109,64]{0,1:T(8,128)S(1)}, f32[109,64]{0,1:T(8,128)S(1)}, u32[]{:S(2)}, u32[]{:S(2)}) collective-permute-start(f32[109,64]{0,1:T(8,128)S(1)} %pad_maximum_fusion.3), channel_id=1, source_target_pairs={{0,8},{1,9},{2,10},{3,11},{4,12},{5,13},{6,14},{7,15},{8,0},{9,1},... | collective-permute-start | bytes 83720 | tf_op jit(solution)/shard_map/ppermute | solution.py:97
  57.6 7.0 %collective-permute-start.6 = (f32[218,64]{0,1:T(8,128)S(1)}, f32[218,64]{0,1:T(8,128)S(1)}, u32[]{:S(2)}, u32[]{:S(2)}) collective-permute-start(f32[218,64]{0,1:T(8,128)S(1)} %maximum_select_fusion.3), channel_id=1, source_target_pairs={{0,4},{1,5},{2,6},{3,7},{4,0},{5,1},{6,2},{7,3},{8,12},{9,13},{10,... | collective-permute-start | bytes 167432 | tf_op jit(solution)/shard_map/ppermute | solution.py:97
  64.8 5.0 %collective-permute-start.7 = (f32[436,64]{0,1:T(8,128)S(1)}, f32[436,64]{0,1:T(8,128)S(1)}, u32[]{:S(2)}, u32[]{:S(2)}) collective-permute-start(f32[436,64]{0,1:T(8,128)S(1)} %maximum_select_fusion.2), channel_id=1, source_target_pairs={{0,2},{1,3},{2,0},{3,1},{4,6},{5,7},{6,4},{7,5},{8,10},{9,11},{10,... | collective-permute-start | bytes 334856 | tf_op jit(solution)/shard_map/ppermute | solution.py:97
  69.9 10.9 %collective-permute-start.8 = (f32[872,64]{0,1:T(8,128)S(1)}, f32[872,64]{0,1:T(8,128)S(1)}, u32[]{:S(2)}, u32[]{:S(2)}) collective-permute-start(f32[872,64]{0,1:T(8,128)S(1)} %maximum_select_fusion.1), channel_id=1, source_target_pairs={{0,1},{1,0},{2,3},{3,2},{4,5},{5,4},{6,7},{7,6},{8,9},{9,8},{10,11... | collective-permute-start | bytes 669704 | tf_op jit(solution)/shard_map/ppermute | solution.py:97
  84.8 2.0 %copy-start = (bf16[9,16,108,108]{3,2,0,1:T(8,128)(2,1)}, bf16[9,16,108,108]{3,2,0,1:T(8,128)(2,1)S(1)}, u32[]{:S(2)}) copy-start(bf16[9,16,108,108]{3,2,0,1:T(8,128)(2,1)S(1)} %fusion.103) | copy-start | bytes 10077700
  86.7 1.8 %copy-start.3 = (bf16[7,16,108,108]{3,2,1,0:T(8,128)(2,1)}, bf16[7,16,108,108]{3,2,1,0:T(8,128)(2,1)S(1)}, u32[]{:S(2)}) copy-start(bf16[7,16,108,108]{3,2,1,0:T(8,128)(2,1)S(1)} %fusion.122) | copy-start | bytes 7838212
  105.2 2.2 %copy-start.1 = (bf16[9,16,108,108]{3,2,0,1:T(8,128)(2,1)S(1)}, bf16[9,16,108,108]{3,2,0,1:T(8,128)(2,1)}, u32[]{:S(2)}) copy-start(bf16[9,16,108,108]{3,2,0,1:T(8,128)(2,1)} %copy-done) | copy-start | bytes 10077700
  107.3 1.9 %copy-start.4 = (bf16[7,16,108,108]{3,2,1,0:T(8,128)(2,1)S(1)}, bf16[7,16,108,108]{3,2,1,0:T(8,128)(2,1)}, u32[]{:S(2)}) copy-start(bf16[7,16,108,108]{3,2,1,0:T(8,128)(2,1)} %copy-done.3) | copy-start | bytes 7838212
Sparse Core Ops, SparseCore 0:
  17.4 83.4 all-gather.2
